TPU v7x, 32 devices: a whole 2x2x4 slice. The times are simulated.
32 devices in a mesh: groups: 2 (over x), heads: 4 (over y, core), seq: 4 (over z).
Axes of the slice: x: 2, y: 2, z: 4, core: 2. Of those that a mesh axis runs over, the one named last changes fastest.
Arguments:
- lin_query: bfloat16 [4096, 4096], P(('groups', 'seq'), 'heads'), parts along dimension 0, may hold values from -6 to 6
- lin_key: bfloat16 [4096, 4096], P(('groups', 'seq'), 'heads'), parts along dimension 0, may hold values from -6 to 6
- lin_value: bfloat16 [4096, 4096], P(('groups', 'seq'), 'heads'), parts along dimension 0, may hold values from -6 to 6
- log_decay: float32 [4096, 32], P(('groups', 'seq'), 'heads'), parts along dimension 0, may hold values from -1 to 0
- stream: bfloat16 [4096, 6144], P(('groups', 'seq'), 'heads'), parts along dimension 0, may hold values from -400 to 400
- out_weight: bfloat16 [4096, 6144], P('heads', 'seq'), may hold values from -0.125 to 0.125
- norm_gain: bfloat16 [6144], P('heads'), may hold values from 0.5 to 1.5
- query_weight: bfloat16 [6144, 4096], P('seq', 'heads'), may hold values from -12 to 12
- kv_weight: bfloat16 [4, 6144, 256], P(None, 'seq'), may hold values from -1 to 1
Outputs:
- stream_next: bfloat16 [4096, 6144], P(('groups', 'seq'), 'heads'), parts along dimension 0
- attended: bfloat16 [4096, 4096], P(('groups', 'seq'), 'heads'), parts along dimension 0
There are 2 independent parts, one for each index of `groups`. A program takes and returns all parts, laid end to end along the dimension named above; an argument that names none is the same for every part. Nothing has to cross between parts.
All inputs are finite; a program needn't handle non-finite values.
Results may differ from a plain program's by a relative error of at most 0.019.
Values may be sent and summed in bfloat16 or wider, within the bound.
No kernel may reach another device: no remote copies, remote signals or barrier semaphores. Data moves between devices by JAX's collectives and lax.ppermute only.
A program may use at most 128 MiB of HBM per device.

v0:
```python
import jax
import jax.numpy as jnp
from jax import lax
from jax.sharding import PartitionSpec as P

D = 6144
QUERY_HEADS = 32
KVH = 4
DH = 128
BLOCK = 256


def from_behind(value, axis, steps):
    count = lax.axis_size(axis)
    leading, last = (max(0, -steps), min(count, count - steps))
    return lax.ppermute(value, axis, [(source, source + steps) for source in range(leading, last)])


def lightning_block(kv_state, block_inputs):
    query_blk, key_blk, value_blk, decay_blk = block_inputs
    block_len = query_blk.shape[0]
    local_cum = jnp.cumsum(decay_blk, axis=0)
    causal_mask = (jnp.arange(block_len)[:, None] >= jnp.arange(block_len)[None, :])[:, :, None]
    decay_diff = local_cum[:, None, :] - local_cum[None, :, :]
    decays = jnp.where(causal_mask, jnp.exp(jnp.where(causal_mask, decay_diff, 0.0)), 0.0)
    scores = jnp.einsum("thd,shd->hts", query_blk, key_blk, preferred_element_type=jnp.float32)
    weights = (scores * jnp.transpose(decays, (2, 0, 1))).astype(jnp.bfloat16)
    intra_out = jnp.einsum("hts,shd->thd", weights, value_blk, preferred_element_type=jnp.float32)
    query_f = query_blk.astype(jnp.float32)
    inter_out = jnp.einsum(
        "thd,hde->the",
        query_f * jnp.exp(local_cum)[:, :, None],
        kv_state,
        precision=lax.Precision.HIGHEST,
    )
    tail_decay = jnp.exp(local_cum[-1][None, :] - local_cum)
    key_f = key_blk.astype(jnp.float32) * tail_decay[:, :, None]
    kv_state = jnp.exp(local_cum[-1])[:, None, None] * kv_state + jnp.einsum(
        "shd,she->hde", key_f, value_blk.astype(jnp.float32), precision=lax.Precision.HIGHEST
    )
    return (kv_state, intra_out + inter_out)


def shards(
    lin_query, lin_key, lin_value, log_decay, stream, out_weight, norm_gain, query_weight, kv_weight
):
    tok_rows = lin_query.shape[0]
    heads_here = log_decay.shape[1]
    head_width = heads_here * DH
    nblocks = tok_rows // BLOCK
    block_shape = (nblocks, BLOCK, heads_here, DH)
    inputs = (
        lin_query.reshape(block_shape),
        lin_key.reshape(block_shape),
        lin_value.reshape(block_shape),
        log_decay.reshape(nblocks, BLOCK, heads_here),
    )
    start_state = jnp.zeros((heads_here, DH, DH), jnp.float32)
    local_state, local_out = lax.scan(lightning_block, start_state, inputs)
    local_out = local_out.reshape(tok_rows, heads_here, DH)
    decay_total = jnp.sum(log_decay, axis=0)
    totals, states = (
        lax.all_gather(decay_total[None].astype(jnp.bfloat16), "seq", axis=0, tiled=True).astype(
            jnp.float32
        ),
        lax.all_gather(local_state[None].astype(jnp.bfloat16), "seq", axis=0, tiled=True).astype(
            jnp.float32
        ),
    )
    position = lax.axis_index("seq")
    device_order = jnp.arange(totals.shape[0])
    earlier = (device_order < position)[:, None]
    before = jnp.sum(jnp.where(earlier, totals, 0.0), axis=0)
    inclusive = jnp.cumsum(totals, axis=0)
    factors = jnp.where(earlier, jnp.exp(jnp.where(earlier, before[None, :] - inclusive, 0.0)), 0.0)
    incoming = jnp.einsum("jh,jhde->hde", factors, states, precision=lax.Precision.HIGHEST)
    running = jnp.cumsum(log_decay, axis=0)
    query_f = (
        lin_query.reshape(tok_rows, heads_here, DH).astype(jnp.float32)
        * jnp.exp(running)[:, :, None]
    )
    carried = jnp.einsum("thd,hde->the", query_f, incoming, precision=lax.Precision.HIGHEST)
    lin_raw = local_out + carried
    lin_out = (
        (lin_raw * lax.rsqrt(jnp.mean(lin_raw * lin_raw, axis=-1, keepdims=True) + 1e-06))
        .astype(jnp.bfloat16)
        .reshape(tok_rows, head_width)
    )
    branch = jnp.dot(
        lin_out,
        lax.all_gather(out_weight, "seq", axis=1, tiled=True),
        preferred_element_type=jnp.float32,
    )
    kv_group = lax.axis_index("heads") * heads_here // (QUERY_HEADS // KVH)
    kv_mine = lax.dynamic_index_in_dim(kv_weight, kv_group, 0, keepdims=False)
    query_rows, kv_rows = (
        lax.all_gather(query_weight, "seq", axis=0, tiled=True),
        lax.all_gather(kv_mine, "seq", axis=0, tiled=True),
    )
    projection = jnp.concatenate([query_rows, kv_rows], axis=1)
    own_sum = lax.psum_scatter(
        branch.astype(jnp.bfloat16), "heads", scatter_dimension=1, tiled=True
    ).astype(jnp.float32)
    mixed_sum = stream.astype(jnp.float32) + own_sum
    stream_next = mixed_sum.astype(jnp.bfloat16)
    total_sq = lax.psum(jnp.sum(mixed_sum * mixed_sum, axis=1), "heads")
    normed = (
        mixed_sum
        * lax.rsqrt(total_sq / D + 1e-05)[:, None]
        * norm_gain.astype(jnp.float32)[None, :]
    ).astype(jnp.bfloat16)
    projected = jnp.dot(
        lax.all_gather(normed, "heads", axis=1, tiled=True),
        projection,
        preferred_element_type=jnp.float32,
    )
    projected = projected.astype(jnp.bfloat16)
    queries = projected[:, :head_width].reshape(tok_rows, heads_here, DH)
    keys_values = projected[:, head_width:]
    position = lax.axis_index("seq")
    query_pos = position * tok_rows + jnp.arange(tok_rows)
    score_scale = float(DH) ** (-0.5)

    def attend(state_in, kv_block, key_start):
        old_max, row_total, weighted = state_in
        key_count = kv_block.shape[0]
        key_part = kv_block[:, :DH]
        value_part = kv_block[:, DH:]
        scores = (
            jnp.einsum("thd,sd->hts", queries, key_part, preferred_element_type=jnp.float32)
            * score_scale
        )
        key_pos = key_start + jnp.arange(key_count)
        allowed = ((key_pos[None, :] <= query_pos[:, None]) & (key_pos[None, :] >= 0))[None, :, :]
        scores = jnp.where(allowed, scores, -1e30)
        new_max = jnp.maximum(old_max, jnp.max(scores, axis=-1))
        expos = jnp.where(allowed, jnp.exp(scores - new_max[:, :, None]), 0.0)
        rescale = jnp.exp(old_max - new_max)
        row_total = row_total * rescale + jnp.sum(expos, axis=-1)
        prob_bf16 = expos.astype(jnp.bfloat16)
        weighted = weighted * rescale[:, :, None] + jnp.einsum(
            "hts,sd->htd", prob_bf16, value_part, preferred_element_type=jnp.float32
        )
        return (new_max, row_total, weighted)

    initial = (
        jnp.full((heads_here, tok_rows), -1e30, jnp.float32),
        jnp.zeros((heads_here, tok_rows), jnp.float32),
        jnp.zeros((heads_here, tok_rows, DH), jnp.float32),
    )
    first_state = attend(initial, keys_values, position * tok_rows)
    seq_count = lax.axis_size("seq")

    def cycle_turn(turn_index, loop_state):
        moving, inner_state = loop_state
        moving = from_behind(moving, "seq", 1)
        source = position - turn_index
        return (moving, attend(inner_state, moving, source * tok_rows))

    _, final_state = lax.fori_loop(1, seq_count, cycle_turn, (keys_values, first_state))
    _, row_total, weighted = final_state
    attended = (
        jnp.transpose(weighted / row_total[:, :, None], (1, 0, 2))
        .reshape(tok_rows, head_width)
        .astype(jnp.bfloat16)
    )
    return (stream_next, attended)


def solution(mesh):
    return jax.shard_map(
        shards,
        mesh=mesh,
        in_specs=(
            P(("groups", "seq"), "heads"),
            P(("groups", "seq"), "heads"),
            P(("groups", "seq"), "heads"),
            P(("groups", "seq"), "heads"),
            P(("groups", "seq"), "heads"),
            P("heads", "seq"),
            P("heads"),
            P("seq", "heads"),
            P(None, "seq", None),
        ),
        out_specs=(P(("groups", "seq"), "heads"), P(("groups", "seq"), "heads")),
        check_vma=False,
    )
```

profile of v0, /device:TPU:21, one launch (start us, length us, event | category | flops | bytes accessed | tf_op | source)
XLA Modules:
  0.0 824.5 jit_solution(3079648835785859866)
XLA Ops:
  13.6 79.9 %while.34 = (s32[]{:T(128)}, f32[8,128,128]{2,1,0:T(8,128)}, f32[2,256,8,128]{1,0,3,2:T(2,128)}, f32[2,256,8]{1,2,0:T(8,128)S(1)}, bf16[2,256,8,128]{3,2,1,0:T(8...) while((s32[]{:T(128)}, f32[8,128,128]{2,1,0:T(8,128)}, ...), condition=%wide.region_3.4_spmd.clone, body=%wide.region_0.3_spmd.clone.sunk | while | flops 1078530048 | bytes 19645352 | solution.py:59
  16.8 3.5 convolution_bitcast_fusion.2
  23.9 3.8 fusion.84
  31.0 22.0 %dynamic_update_slice.6 = f32[2,256,8,128]{1,0,3,2:T(2,128)} dynamic-update-slice(f32[2,256,8,128]{1,0,3,2:T(2,128)} %get-tuple-element.452, f32[1,256,8,128]{1,0,3,2:T(1,128)} %copy.136, s32[]{:T(128)S(6)} %copy.141, s32[]{:T(128)} %constant.109.clone.1..sunk, s32[]{:T(128)} %constant.109.clone.1..sunk, s32[]{:T(128)} %constant.109.clone.1..sunk) | dynamic-update-slice | bytes 2097156 | tf_op jit(solution)/shard_map/while/body/jit(dynamic_update_index_in_dim)/dynamic_update_slice | solution.py:59
  56.0 3.7 convolution_bitcast_fusion.2
  64.5 3.8 fusion.84
  71.6 22.0 %dynamic_update_slice.6 = f32[2,256,8,128]{1,0,3,2:T(2,128)} dynamic-update-slice(f32[2,256,8,128]{1,0,3,2:T(2,128)} %get-tuple-element.452, f32[1,256,8,128]{1,0,3,2:T(1,128)} %copy.136, s32[]{:T(128)S(6)} %copy.141, s32[]{:T(128)} %constant.109.clone.1..sunk, s32[]{:T(128)} %constant.109.clone.1..sunk, s32[]{:T(128)} %constant.109.clone.1..sunk) | dynamic-update-slice | bytes 2097156 | tf_op jit(solution)/shard_map/while/body/jit(dynamic_update_index_in_dim)/dynamic_update_slice | solution.py:59
  96.3 3.9 reshape.219
  101.7 8.4 %all-reduce = bf16[32]{0:T(256)(128)(2,1)S(1)} all-reduce(bf16[32]{0:T(256)(128)(2,1)S(1)} %dynamic-update-slice), channel_id=2, replica_groups=mesh['groups'=2,'heads'=4,'seq'=4] {'seq'}, use_global_device_ids=true, to_apply=%add | all-reduce | flops 32 | bytes 128
  111.8 12.2 %all-gather.15.cloned.1.call-done = bf16[32,128,128]{2,1,0:T(8,128)(2,1)} async-done(((bf16[8,128,128]{2,1,0:T(8,128)(2,1)}), bf16[32,128,128]{2,1,0:T(8,128)(2,1)}) %all-gather.15.cloned.1.call-update) | async-done | bytes 1048592 | tf_op jit(solution)/shard_map/all_gather | solution.py:66
  125.6 4.7 multiply_reduce_fusion.2
  131.6 210.4 %all-gather.9.cloned.1.call-done = bf16[1024,6144]{1,0:T(8,128)(2,1)} async-done(((bf16[1024,1536]{1,0:T(8,128)(2,1)}), bf16[1024,6144]{1,0:T(8,128)(2,1)}) %all-gather.9.cloned.1.call-update) | async-done | bytes 12582928 | tf_op jit(solution)/shard_map/all_gather | solution.py:91
  341.9 11.8 %convolution_convert_fusion = bf16[512,6144]{1,0:T(8,128)(2,1)} fusion(bf16[512,1024]{0,1:T(8,128)(2,1)} %bitcast.181, bf16[1024,6144]{1,0:T(8,128)(2,1)} %all-gather.9.cloned.1.call-done), kind=kOutput, calls=%fused_computation.60 | convolution fusion | flops 6445596672 | bytes 19922944 | tf_op jit(solution)/shard_map/dot_general | solution.py:89
  355.5 55.4 %reduce-scatter.2.cloned.1.call-done = bf16[512,1536]{1,0:T(8,128)(2,1)} async-done(((bf16[512,6144]{1,0:T(8,128)(2,1)}), bf16[512,1536]{1,0:T(8,128)(2,1)}) %reduce-scatter.2.cloned.1.call-update) | async-done | bytes 1572880 | tf_op jit(solution)/shard_map/reduce_scatter | solution.py:101
  413.0 6.1 psum.7
  421.7 54.2 %all-gather.17.cloned.1.call-done = bf16[1,6144,256]{2,1,0:T(8,128)(2,1)} async-done(((bf16[1,1536,256]{2,1,0:T(8,128)(2,1)}), bf16[1,6144,256]{2,1,0:T(8,128)(2,1)}) %all-gather.17.cloned.1.call-update) | async-done | bytes 3145744 | tf_op jit(solution)/shard_map/all_gather | solution.py:98
  475.9 217.8 %all-gather.13.cloned.1.call-done = bf16[6144,1024]{1,0:T(8,128)(2,1)} async-done(((bf16[1536,1024]{1,0:T(8,128)(2,1)}), bf16[6144,1024]{1,0:T(8,128)(2,1)}) %all-gather.13.cloned.1.call-update) | async-done | bytes 12582928 | tf_op jit(solution)/shard_map/all_gather | solution.py:97
  693.7 47.5 %all-gather.11.cloned.1.call-done = bf16[512,6144]{1,0:T(8,128)(2,1)} async-done(((bf16[512,1536]{1,0:T(8,128)(2,1)}), bf16[512,6144]{1,0:T(8,128)(2,1)}) %all-gather.11.cloned.1.call-update) | async-done | bytes 6291472 | tf_op jit(solution)/shard_map/all_gather | solution.py:113
  741.2 15.6 %fusion.43 = bf16[512,1280]{1,0:T(8,128)(2,1)S(1)} fusion(bf16[512,6144]{1,0:T(8,128)(2,1)} %all-gather.11.cloned.1.call-done, bf16[6144,256]{1,0:T(8,128)(2,1)} %bitcast.188, bf16[6144,1024]{1,0:T(8,128)(2,1)} %all-gather.13.cloned.1.call-done), kind=kOutput, calls=%fused_computation.71 | convolution fusion | flops 8085176320 | bytes 23330816 | tf_op jit(solution)/shard_map/dot_general | solution.py:112
  760.6 3.9 fusion.49
  764.5 50.3 %while.33 = (s32[]{:T(128)}, bf16[512,256]{1,0:T(8,128)(2,1)S(1)}, f32[8,512]{1,0:T(8,128)S(1)}, f32[8,512]{1,0:T(8,128)S(1)}, f32[8,512,128]{2,1,0:T(8,128)}, /...) while((s32[]{:T(128)}, bf16[512,256]{1,0:T(8,128)(2,1)S(1)}, ...), condition=%wide.region_18.19_spmd.clone, body=%wide.region_15.18_spmd.clone.sunk | while | flops 1102587904 | bytes 50341096 | solution.py:160
  767.9 6.1 collective-permute-done
  785.5 5.2 collective-permute-done
  802.3 4.4 collective-permute-done
  (149 shorter events, 83.0 us)
Async XLA Ops:
  7.2 346.7 %copy-start = (bf16[4,1536,256]{2,1,0:T(8,128)(2,1)S(1)}, bf16[4,1536,256]{2,1,0:T(8,128)(2,1)}, u32[]{:S(2)}) copy-start(bf16[4,1536,256]{2,1,0:T(8,128)(2,1)} %param.21) | copy-start | bytes 9437188
  7.2 116.8 %all-gather.15.cloned.1.call-start = ((), (), s32[]{:S(2)}) async-start(), calls=%async_computation.5 | async-start | bytes 1310720 | tf_op jit(solution)/shard_map/all_gather | solution.py:66
  7.2 5.1 copy-start.6
  7.3 6.4 copy-start.9
  16.7 4.9 copy-start.2
  21.6 2.2 copy-start.3
  56.0 5.0 copy-start.2
  61.0 3.4 copy-start.3
  95.3 4.9 copy-start.11
  95.4 246.6 %all-gather.9.cloned.1.call-start = ((), (), s32[]{:S(2)}) async-start(), calls=%async_computation.1 | async-start | bytes 15728640 | tf_op jit(solution)/shard_map/all_gather | solution.py:91
  96.1 314.8 %reduce-scatter.2.cloned.1.call-start = ((), (), s32[]{:S(2)}) async-start(), calls=%async_computation.2 | async-start | bytes 7864320 | tf_op jit(solution)/shard_map/reduce_scatter | solution.py:101
  353.7 1.7 copy-start.10
  353.8 122.2 %all-gather.17.cloned.1.call-start = ((), (), s32[]{:S(2)}) async-start(), calls=%async_computation.6 | async-start | bytes 3932160 | tf_op jit(solution)/shard_map/all_gather | solution.py:98
  354.8 56.1 %copy-start.4 = (bf16[512,1536]{1,0:T(8,128)(2,1)S(1)}, bf16[512,1536]{1,0:T(8,128)(2,1)}, u32[]{:S(2)}) copy-start(bf16[512,1536]{1,0:T(8,128)(2,1)} %param.17) | copy-start | bytes 4718596
  354.8 338.9 %all-gather.13.cloned.1.call-start = ((), (), s32[]{:S(2)}) async-start(), calls=%async_computation.4 | async-start | bytes 15728640 | tf_op jit(solution)/shard_map/all_gather | solution.py:97
  355.4 385.8 %all-gather.11.cloned.1.call-start = ((), (), s32[]{:S(2)}) async-start(), calls=%async_computation.3 | async-start | bytes 7864320 | tf_op jit(solution)/shard_map/all_gather | solution.py:113
  410.9 8.2 copy-start.5
  764.5 9.5 %collective-permute-start = (bf16[512,256]{1,0:T(8,128)(2,1)S(1)}, bf16[512,256]{1,0:T(8,128)(2,1)S(1)}, u32[]{:S(2)}, u32[]{:S(2)}) collective-permute-start(bf16[512,256]{1,0:T(8,128)(2,1)S(1)} %get-tuple-element.481), channel_id=1, source_target_pairs={{0,1},{1,2},{2,3},{4,5},{5,6},{6,7},{8,9},{9,10},{10,11},{12,13},{... | collective-permute-start | bytes 786440 | tf_op jit(solution)/shard_map/while/body/eval_jaxpr/ppermute | solution.py:16
  775.6 2.1 copy-start.7
  782.1 8.6 %collective-permute-start = (bf16[512,256]{1,0:T(8,128)(2,1)S(1)}, bf16[512,256]{1,0:T(8,128)(2,1)S(1)}, u32[]{:S(2)}, u32[]{:S(2)}) collective-permute-start(bf16[512,256]{1,0:T(8,128)(2,1)S(1)} %get-tuple-element.481), channel_id=1, source_target_pairs={{0,1},{1,2},{2,3},{4,5},{5,6},{6,7},{8,9},{9,10},{10,11},{12,13},{... | collective-permute-start | bytes 786440 | tf_op jit(solution)/shard_map/while/body/eval_jaxpr/ppermute | solution.py:16
  792.3 2.1 copy-start.7
  798.9 7.8 collective-permute-start
  808.2 2.1 copy-start.7
  814.8 2.9 copy-start.1
  (3 other events, 4.1 us)
Sparse Core Ops, SparseCore 0:
  95.5 28.4 all-gather.14
  125.6 216.3 all-gather.8
  353.9 56.9 reduce-scatter.1
  412.9 63.0 all-gather.16
  477.3 216.3 all-gather.12
  695.2 45.9 all-gather.10
where the time goes:
time: 832 us; the launch traced here: 825 us
  waiting for transfers between devices  614 us (74%)
  local copies, waits for them, and re-layouts  74.6 us (9%)
  matrix products  71.7 us (9%)
  other arithmetic  24.5 us (3%)
  between operations  15 us (2%)
  blocking collectives  14.5 us (2%)
  starting transfers between devices  9.54 us (1%)
    all_gather x1, waiting for transfers between devices, shards(): lax.all_gather(query_weight, 'seq', axis=0, tiled=True)  218 us
    all_gather x1, waiting for transfers between devices, shards(): lax.all_gather(out_weight, 'seq', axis=1, tiled=True)  210 us
    reduce_scatter x1, waiting for transfers between devices, shards(): lax.psum_scatter(branch.astype(jnp.bfloat16), 'heads', scatter_dimension=...  55.4 us
    all_gather x1, waiting for transfers between devices, shards(): lax.all_gather(kv_mine, 'seq', axis=0, tiled=True)  54.2 us
    dynamic_update_slice x4, local copies, waits for them, and re-layouts, shards(): local_state, local_out = lax.scan(lightning_block, start_state, inputs)  50.5 us
    all_gather x1, waiting for transfers between devices, shards(): lax.all_gather(normed, 'heads', axis=1, tiled=True)  47.5 us
  transfers between devices with their start and end apart: 9, of which 9 were waited for; matrix products, arithmetic and copies ran while one was open for 2% of the time, Pallas kernels for 0%

commit v1 on v0

--- a/solution.py
+++ b/solution.py
@@ -41,7 +41,7 @@
     return (kv_state, intra_out + inter_out)
 
 
-def shards(
+def shards_base(
     lin_query, lin_key, lin_value, log_decay, stream, out_weight, norm_gain, query_weight, kv_weight
 ):
     tok_rows = lin_query.shape[0]
@@ -167,7 +167,132 @@
     return (stream_next, attended)
 
 
+def lightning_local(lin_query, lin_key, lin_value, log_decay):
+    tok_rows = lin_query.shape[0]
+    heads_here = log_decay.shape[1]
+    nblocks = tok_rows // BLOCK
+    shape4 = (tok_rows, heads_here, DH)
+    q4, k4, v4 = (x.reshape(shape4) for x in (lin_query, lin_key, lin_value))
+    state = jnp.zeros((heads_here, DH, DH), jnp.float32)
+    outs = []
+    for blk in range(nblocks):
+        rows = slice(blk * BLOCK, (blk + 1) * BLOCK)
+        state, out = lightning_block(state, (q4[rows], k4[rows], v4[rows], log_decay[rows]))
+        outs.append(out)
+    local_out = jnp.concatenate(outs, axis=0)
+    decay_total = jnp.sum(log_decay, axis=0)
+    totals = lax.all_gather(decay_total[None].astype(jnp.bfloat16), "seq", axis=0, tiled=True)
+    states = lax.all_gather(state[None].astype(jnp.bfloat16), "seq", axis=0, tiled=True)
+    totals = totals.astype(jnp.float32)
+    states = states.astype(jnp.float32)
+    position = lax.axis_index("seq")
+    device_order = jnp.arange(totals.shape[0])
+    earlier = (device_order < position)[:, None]
+    before = jnp.sum(jnp.where(earlier, totals, 0.0), axis=0)
+    inclusive = jnp.cumsum(totals, axis=0)
+    factors = jnp.where(earlier, jnp.exp(jnp.where(earlier, before[None, :] - inclusive, 0.0)), 0.0)
+    incoming = jnp.einsum("jh,jhde->hde", factors, states, precision=lax.Precision.HIGHEST)
+    running = jnp.cumsum(log_decay, axis=0)
+    query_f = q4.astype(jnp.float32) * jnp.exp(running)[:, :, None]
+    carried = jnp.einsum("thd,hde->the", query_f, incoming, precision=lax.Precision.HIGHEST)
+    lin_raw = local_out + carried
+    lin_out = (
+        (lin_raw * lax.rsqrt(jnp.mean(lin_raw * lin_raw, axis=-1, keepdims=True) + 1e-06))
+        .astype(jnp.bfloat16)
+        .reshape(tok_rows, heads_here * DH)
+    )
+    return lin_out
+
+
+def attend_block(queries, query_pos, state_in, kv_block, key_start):
+    old_max, row_total, weighted = state_in
+    key_count = kv_block.shape[0]
+    key_part = kv_block[:, :DH]
+    value_part = kv_block[:, DH:]
+    score_scale = float(DH) ** (-0.5)
+    scores = (
+        jnp.einsum("thd,sd->hts", queries, key_part, preferred_element_type=jnp.float32)
+        * score_scale
+    )
+    key_pos = key_start + jnp.arange(key_count)
+    allowed = (key_pos[None, :] <= query_pos[:, None])[None, :, :]
+    scores = jnp.where(allowed, scores, -1e30)
+    new_max = jnp.maximum(old_max, jnp.max(scores, axis=-1))
+    expos = jnp.where(allowed, jnp.exp(scores - new_max[:, :, None]), 0.0)
+    rescale = jnp.exp(old_max - new_max)
+    row_total = row_total * rescale + jnp.sum(expos, axis=-1)
+    prob_bf16 = expos.astype(jnp.bfloat16)
+    weighted = weighted * rescale[:, :, None] + jnp.einsum(
+        "hts,sd->htd", prob_bf16, value_part, preferred_element_type=jnp.float32
+    )
+    return (new_max, row_total, weighted)
+
+
+def shards_fast(
+    lin_query, lin_key, lin_value, log_decay, stream, out_weight, norm_gain, query_weight, kv_weight
+):
+    n_heads = lax.axis_size("heads")
+    n_seq = lax.axis_size("seq")
+    tok_rows = lin_query.shape[0]
+    heads_here = log_decay.shape[1]
+    head_width = heads_here * DH
+    mine_a = lax.axis_index("heads")
+    mine_b = lax.axis_index("seq")
+    swap = [(x * n_seq + y, y * n_seq + x) for x in range(n_heads) for y in range(n_seq)]
+    stream_t = lax.ppermute(stream, ("heads", "seq"), swap)
+
+    lin_out = lightning_local(lin_query, lin_key, lin_value, log_decay)
+    lin_all = lax.all_gather(lin_out, "seq", axis=0, tiled=True)
+    part = jnp.dot(lin_all, out_weight, preferred_element_type=jnp.float32).astype(jnp.bfloat16)
+    own_sum = lax.psum_scatter(part, "heads", scatter_dimension=0, tiled=True)
+    mixed_sum = stream_t.astype(jnp.float32) + own_sum.astype(jnp.float32)
+    stream_next = lax.ppermute(mixed_sum.astype(jnp.bfloat16), ("heads", "seq"), swap)
+    total_sq = lax.psum(jnp.sum(mixed_sum * mixed_sum, axis=1), "seq")
+    cols = mixed_sum.shape[1]
+    gain_all = lax.all_gather(norm_gain, "heads", axis=0, tiled=True)
+    gain_b = lax.dynamic_slice_in_dim(gain_all, mine_b * cols, cols)
+    normed = (
+        mixed_sum
+        * lax.rsqrt(total_sq / D + 1e-05)[:, None]
+        * gain_b.astype(jnp.float32)[None, :]
+    ).astype(jnp.bfloat16)
+    normed_all = lax.all_gather(normed, "heads", axis=0, tiled=True)
+    kv_group = mine_a * heads_here // (QUERY_HEADS // KVH)
+    kv_mine = lax.dynamic_index_in_dim(kv_weight, kv_group, 0, keepdims=False)
+    projection = jnp.concatenate([query_weight, kv_mine], axis=1)
+    part2 = jnp.dot(normed_all, projection, preferred_element_type=jnp.float32).astype(
+        jnp.bfloat16
+    )
+    queries = lax.psum_scatter(part2[:, :head_width], "seq", scatter_dimension=0, tiled=True)
+    keys_values = lax.psum(part2[:, head_width:], "seq")
+    queries = queries.reshape(tok_rows, heads_here, DH)
+    query_pos = mine_b * tok_rows + jnp.arange(tok_rows)
+    state = (
+        jnp.full((heads_here, tok_rows), -1e30, jnp.float32),
+        jnp.zeros((heads_here, tok_rows), jnp.float32),
+        jnp.zeros((heads_here, tok_rows, DH), jnp.float32),
+    )
+    for blk in range(n_seq):
+        kv_block = keys_values[blk * tok_rows : (blk + 1) * tok_rows]
+        state = attend_block(queries, query_pos, state, kv_block, blk * tok_rows)
+    _, row_total, weighted = state
+    attended = (
+        jnp.transpose(weighted / row_total[:, :, None], (1, 0, 2))
+        .reshape(tok_rows, head_width)
+        .astype(jnp.bfloat16)
+    )
+    return (stream_next, attended)
+
+
 def solution(mesh):
+    n_heads = mesh.shape["heads"]
+    n_seq = mesh.shape["seq"]
+    fast_ok = n_heads == n_seq and QUERY_HEADS % n_heads == 0
+    if fast_ok:
+        heads_here = QUERY_HEADS // n_heads
+        fast_ok = (QUERY_HEADS // KVH) % heads_here == 0 and D % n_seq == 0
+    shards = shards_fast if fast_ok else shards_base
+
     return jax.shard_map(
         shards,
         mesh=mesh,

time: 832 us -> 558 us (0.67)
  waiting for transfers between devices: 614 us -> 373 us
  local copies, waits for them, and re-layouts: 74.6 us -> 39 us
    all_gather x5 -> x3, waiting for transfers between devices: 542 us -> 130 us  [the longest x1 82.1 us: shards_fast(): lin_all = lax.all_gather(lin_out, 'seq', axis=0, tiled=True)]
    reduce_scatter x1 -> x2, waiting for transfers between devices: 55.4 us -> 126 us  [the longest x1 83 us: shards_fast(): lax.psum_scatter(part2[:, :head_width], 'seq', scatter_dimension=0, tiled...]
    ppermute x3 -> x2, waiting for transfers between devices: 15.7 us -> 73.4 us  [the longest x1 44.6 us: shards_fast(): lax.ppermute(mixed_sum.astype(jnp.bfloat16), ('heads', 'seq'), swap)]
    dynamic_update_slice x4 -> x0, local copies, waits for them, and re-layouts: 50.5 us -> none  [shards(): local_state, local_out = lax.scan(lightning_block, start_state, inputs)]
    psum x0 -> x1, waiting for transfers between devices: none -> 43.4 us  [shards_fast(): keys_values = lax.psum(part2[:, head_width:], 'seq')]
    unnamed x22 -> x35, local copies, waits for them, and re-layouts: 7.24 us -> 21.2 us
    slice x1 -> x6, local copies, waits for them, and re-layouts: 0.02 us -> 12.6 us  [the longest x1 4.64 us: shards_fast(): part2[:, :head_width]]
  transfers between devices with their start and end apart: 9 -> 8, of which waited for: 9 -> 7; matrix products, arithmetic and copies ran while one was open for 2% -> 6% of each run, Pallas kernels for 0% -> 0%
where the time goes in v1:
time: 558 us; the launch traced here: 552 us
  waiting for transfers between devices  373 us (67%)
  matrix products  72.7 us (13%)
  local copies, waits for them, and re-layouts  39 us (7%)
  blocking collectives  22.8 us (4%)
  other arithmetic  22.2 us (4%)
  between operations  15.3 us (3%)
  starting transfers between devices  6.7 us (1%)
    reduce_scatter x1, waiting for transfers between devices, shards_fast(): lax.psum_scatter(part2[:, :head_width], 'seq', scatter_dimension=0, tiled...  83 us
    all_gather x1, waiting for transfers between devices, shards_fast(): lin_all = lax.all_gather(lin_out, 'seq', axis=0, tiled=True)  82.1 us
    all_gather x1, waiting for transfers between devices, shards_fast(): normed_all = lax.all_gather(normed, 'heads', axis=0, tiled=True)  48.1 us
    ppermute x1, waiting for transfers between devices, shards_fast(): lax.ppermute(mixed_sum.astype(jnp.bfloat16), ('heads', 'seq'), swap)  44.6 us
    psum x1, waiting for transfers between devices, shards_fast(): keys_values = lax.psum(part2[:, head_width:], 'seq')  43.4 us
    reduce_scatter x1, waiting for transfers between devices, shards_fast(): own_sum = lax.psum_scatter(part, 'heads', scatter_dimension=0, tiled=True)  42.7 us
    ppermute x1, waiting for transfers between devices, shards_fast(): stream_t = lax.ppermute(stream, ('heads', 'seq'), swap)  28.8 us
    unnamed x35, local copies, waits for them, and re-layouts  21.2 us
  transfers between devices with their start and end apart: 8, of which 7 were waited for; matrix products, arithmetic and copies ran while one was open for 6% of the time, Pallas kernels for 0%

profile of v1, /device:TPU:21, one launch (start us, length us, event | category | flops | bytes accessed | tf_op | source)
XLA Modules:
  0.0 551.6 jit_solution(12346058882184269390)
XLA Ops:
  30.2 7.5 %all-reduce = bf16[32]{0:T(256)(128)(2,1)S(1)} all-reduce(bf16[32]{0:T(256)(128)(2,1)S(1)} %dynamic-update-slice), channel_id=2, replica_groups=mesh['groups'=2,'heads'=4,'seq'=4] {'seq'}, use_global_device_ids=true, to_apply=%add | all-reduce | flops 32 | bytes 128
  45.8 3.3 fusion.38
  49.1 4.3 fusion.42
  56.7 4.5 fusion.41
  62.8 4.5 multiply_reduce_fusion.2
  71.3 82.1 %all-gather.7.cloned.1.call-done = bf16[2048,1024]{0,1:T(8,128)(2,1)} async-done(((bf16[512,1024]{0,1:T(8,128)(2,1)}), bf16[2048,1024]{0,1:T(8,128)(2,1)}) %all-gather.7.cloned.1.call-update) | async-done | bytes 4194320 | tf_op jit(solution)/shard_map/all_gather | solution.py:245
  153.4 11.0 %convolution_convert_fusion.1 = bf16[2048,1536]{1,0:T(8,128)(2,1)} fusion(bf16[2048,1024]{0,1:T(8,128)(2,1)} %all-gather.7.cloned.1.call-done, bf16[1024,1536]{1,0:T(8,128)(2,1)S(1)} %copy-done), kind=kOutput, calls=%fused_computation.9 | convolution fusion | flops 6445596672 | bytes 13631488 | tf_op jit(solution)/shard_map/dot_general | solution.py:246
  167.3 6.5 %all-gather.2 = bf16[4,1,1536]{2,1,0:T(2,128)(2,1)S(1)} all-gather(bf16[1,1,1536]{2,1,0:T(2,128)(2,1)S(1)} %reshape.317), channel_id=1, replica_groups=mesh['groups'=2,'heads'=4,'seq'=4] {'heads'}, dimensions={0}, use_global_device_ids=true | all-gather | bytes 15360 | tf_op jit(solution)/shard_map/all_gather | solution.py:252
  174.0 28.8 %collective-permute-done = bf16[512,1536]{1,0:T(8,128)(2,1)S(1)} collective-permute-done((bf16[512,1536]{1,0:T(8,128)(2,1)}, bf16[512,1536]{1,0:T(8,128)(2,1)S(1)}, u32[]{:S(2)}, u32[]{:S(2)}) %collective-permute-start) | collective-permute-done | bytes 1572896 | tf_op jit(solution)/shard_map/ppermute | solution.py:242
  202.8 42.7 %reduce-scatter.3.cloned.1.call-done = bf16[512,1536]{1,0:T(8,128)(2,1)} async-done(((bf16[2048,1536]{1,0:T(8,128)(2,1)}), bf16[512,1536]{1,0:T(8,128)(2,1)}) %reduce-scatter.3.cloned.1.call-update) | async-done | bytes 1572880 | tf_op jit(solution)/shard_map/reduce_scatter | solution.py:247
  247.6 8.8 %psum.14 = f32[512]{0:T(512)S(1)} all-reduce(f32[512]{0:T(512)S(1)} %multiply_reduce_fusion), channel_id=1, replica_groups=mesh['groups'=2,'heads'=4,'seq'=4] {'seq'}, use_global_device_ids=true, to_apply=%region_12.13 | all-reduce | flops 512 | bytes 4096 | tf_op jit(solution)/shard_map/psum | solution.py:250
  260.0 48.1 %all-gather.9.cloned.1.call-done = bf16[2048,1536]{1,0:T(8,128)(2,1)} async-done(((bf16[512,1536]{1,0:T(8,128)(2,1)}), bf16[2048,1536]{1,0:T(8,128)(2,1)}) %all-gather.9.cloned.1.call-update) | async-done | bytes 6291472 | tf_op jit(solution)/shard_map/all_gather | solution.py:259
  308.1 11.3 %convolution_convert_fusion = bf16[2048,1280]{1,0:T(8,128)(2,1)S(1)} fusion(bf16[2048,1536]{1,0:T(8,128)(2,1)} %all-gather.9.cloned.1.call-done, bf16[1536,256]{1,0:T(8,128)(2,1)S(1)} %dynamic-slice_bitcast_fusion, bf16[1536,1024]{1,0:T(8,128)(2,1)} %param.16), kind=kOutput, calls=%fused_computation.8 | convolution fusion | flops 8063549440 | bytes 15466496 | tf_op jit(solution)/shard_map/dot_general | solution.py:263
  322.9 4.6 slice.149
  327.5 3.5 collective-permute-start.1
  331.7 44.6 %collective-permute-done.1 = bf16[512,1536]{1,0:T(8,128)(2,1)} collective-permute-done((bf16[512,1536]{1,0:T(8,128)(2,1)}, bf16[512,1536]{1,0:T(8,128)(2,1)}, u32[]{:S(2)}, u32[]{:S(2)}) %collective-permute-start.1) | collective-permute-done | bytes 1572896 | tf_op jit(solution)/shard_map/ppermute | solution.py:249
  376.3 43.4 %all-reduce.3.cloned.1.call-done = bf16[2048,256]{1,0:T(8,128)(2,1)} async-done(((bf16[2048,256]{1,0:T(8,128)(2,1)}), bf16[2048,256]{1,0:T(8,128)(2,1)}) %all-reduce.3.cloned.1.call-update) | async-done | bytes 1048592 | tf_op jit(solution)/shard_map/psum | solution.py:267
  419.7 83.0 %reduce-scatter.5.cloned.1.call-done = bf16[512,1024]{1,0:T(8,128)(2,1)} async-done(((bf16[2048,1024]{1,0:T(8,128)(2,1)}), bf16[512,1024]{1,0:T(8,128)(2,1)}) %reduce-scatter.5.cloned.1.call-update) | async-done | bytes 1048592 | tf_op jit(solution)/shard_map/reduce_scatter | solution.py:266
  505.8 4.8 fusion.1
  513.8 6.6 %fusion.4 = (f32[8,512]{1,0:T(8,128)S(1)}, f32[8,512]{1,0:T(8,128)S(1)}) fusion(f32[512,512,8]{1,0,2:T(8,128)S(1)} %get-tuple-element.48, f32[8,512]{1,0:T(8,128)S(1)} %get-tuple-element.32, pred[512,512]{0,1:T(8,128)(4,1)S(1)} %get-tuple-element.35, f32[8,512]{1,0:T(8,128)S(1)} %get-tuple-element.17, f32[512,512,8]{1,0,2:T(8,128)} %get-tuple-element.46, ...), kind=kLoop, calls=%fused_computation.14 | loop fusion | flops 20963328 | bytes 17367040 | tf_op jit(solution)/shard_map/reduce_sum | solution.py:223
  520.4 4.0 fusion.8
  524.5 5.5 %fusion.16 = f32[8,512,128]{1,2,0:T(8,128)S(1)} fusion(f32[512,512,8]{1,0,2:T(8,128)} %get-tuple-element.46, f32[8,512]{1,0:T(8,128)S(1)} %get-tuple-element.17, pred[512,512]{0,1:T(8,128)(4,1)S(1)} %get-tuple-element.36, bf16[2048,256]{1,0:T(8,128)(2,1)S(1)} %copy-done.6), kind=kOutput, calls=%fused_computation.24 | convolution fusion | flops 547356672 | bytes 10895360 | tf_op jit(solution)/shard_map/hts,sd->htd/dot_general | solution.py:225
  530.0 3.5 fusion.14
  535.8 3.8 fusion.31
  (108 shorter events, 65.4 us)
Async XLA Ops:
  7.2 146.2 %copy-start = (bf16[1024,1536]{1,0:T(8,128)(2,1)S(1)}, bf16[1024,1536]{1,0:T(8,128)(2,1)}, u32[]{:S(2)}) copy-start(bf16[1024,1536]{1,0:T(8,128)(2,1)} %param.14) | copy-start | bytes 9437188
  7.2 54.0 %all-gather.11.cloned.1.call-start = ((), (), s32[]{:S(2)}) async-start(), calls=%async_computation.7 | async-start | bytes 1310720 | tf_op jit(solution)/shard_map/all_gather | solution.py:185
  14.7 13.7 %copy-start.7 = (f32[512,8]{0,1:T(8,128)S(1)}, f32[512,8]{0,1:T(8,128)}, u32[]{:S(2)}) copy-start(f32[512,8]{0,1:T(8,128)} %param.12) | copy-start | bytes 49156
  14.7 14.0 %copy-start.9 = (u32[32]{0:T(128)S(1)}, u32[32]{0:T(128)}, u32[]{:S(2)}) copy-start(u32[32]{0:T(128)} %constant.74) | copy-start | bytes 388
  25.0 0.8 copy-start.5
  28.3 125.1 %all-gather.7.cloned.1.call-start = ((), (), s32[]{:S(2)}) async-start(), calls=%async_computation.2 | async-start | bytes 5242880 | tf_op jit(solution)/shard_map/all_gather | solution.py:245
  71.1 174.4 %reduce-scatter.3.cloned.1.call-start = ((), (), s32[]{:S(2)}) async-start(), calls=%async_computation.3 | async-start | bytes 7864320 | tf_op jit(solution)/shard_map/reduce_scatter | solution.py:247
  164.4 2.9 copy-start.8
  164.4 143.7 %all-gather.9.cloned.1.call-start = ((), (), s32[]{:S(2)}) async-start(), calls=%async_computation.4 | async-start | bytes 7864320 | tf_op jit(solution)/shard_map/all_gather | solution.py:259
  164.5 38.3 %collective-permute-start = (bf16[512,1536]{1,0:T(8,128)(2,1)}, bf16[512,1536]{1,0:T(8,128)(2,1)S(1)}, u32[]{:S(2)}, u32[]{:S(2)}) collective-permute-start(bf16[512,1536]{1,0:T(8,128)(2,1)} %param.13), channel_id=1, source_target_pairs={{0,0},{1,4},{2,8},{3,12},{4,1},{5,5},{6,9},{7,13},{8,2},{9,6},{10,... | collective-permute-start | bytes 4718600 | tf_op jit(solution)/shard_map/ppermute | solution.py:242
  245.5 11.0 %copy-start.3 = (bf16[512,1536]{1,0:T(8,128)(2,1)S(1)}, bf16[512,1536]{1,0:T(8,128)(2,1)}, u32[]{:S(2)}) copy-start(bf16[512,1536]{1,0:T(8,128)(2,1)} %reduce-scatter.3.cloned.1.call-done) | copy-start | bytes 4718596
  258.7 161.0 %all-reduce.3.cloned.1.call-start = ((), (), s32[]{:S(2)}) async-start(), calls=%async_computation.5 | async-start | bytes 2097152 | tf_op jit(solution)/shard_map/psum | solution.py:267
  319.5 2.3 copy-start.4
  322.8 179.9 %reduce-scatter.5.cloned.1.call-start = ((), (), s32[]{:S(2)}) async-start(), calls=%async_computation.6 | async-start | bytes 5242880 | tf_op jit(solution)/shard_map/reduce_scatter | solution.py:266
  327.5 48.8 %collective-permute-start.1 = (bf16[512,1536]{1,0:T(8,128)(2,1)}, bf16[512,1536]{1,0:T(8,128)(2,1)}, u32[]{:S(2)}, u32[]{:S(2)}) collective-permute-start(bf16[512,1536]{1,0:T(8,128)(2,1)} %get-tuple-element.23), channel_id=1, source_target_pairs={{0,0},{1,4},{2,8},{3,12},{4,1},{5,5},{6,9},{7,13},{8,2},{9,6},{10,... | collective-permute-start | bytes 4718600 | tf_op jit(solution)/shard_map/ppermute | solution.py:249
  502.8 3.0 copy-start.2
  502.8 3.0 copy-start.6
  533.6 2.2 copy-start.10
  535.8 8.7 %copy-start.1 = (bf16[1024,1536]{1,0:T(8,128)(2,1)S(1)}, bf16[1024,1536]{1,0:T(8,128)(2,1)}, u32[]{:S(2)}) copy-start(bf16[1024,1536]{1,0:T(8,128)(2,1)} %param.14) | copy-start | bytes 9437188
Sparse Core Ops, SparseCore 0:
  28.5 27.9 all-gather.10
  71.2 82.1 all-gather.6
  164.5 80.8 reduce-scatter.2
  258.8 49.2 all-gather.8
  322.9 96.7 all-reduce.2
  421.9 80.8 reduce-scatter.4

commit v2 on v1

--- a/solution.py
+++ b/solution.py
@@ -181,10 +181,11 @@
         outs.append(out)
     local_out = jnp.concatenate(outs, axis=0)
     decay_total = jnp.sum(log_decay, axis=0)
-    totals = lax.all_gather(decay_total[None].astype(jnp.bfloat16), "seq", axis=0, tiled=True)
-    states = lax.all_gather(state[None].astype(jnp.bfloat16), "seq", axis=0, tiled=True)
-    totals = totals.astype(jnp.float32)
-    states = states.astype(jnp.float32)
+    packed = jnp.concatenate([state.reshape(-1), decay_total]).astype(jnp.bfloat16)
+    gathered = lax.all_gather(packed, "seq", axis=0, tiled=False).astype(jnp.float32)
+    state_size = state.size
+    states = gathered[:, :state_size].reshape((-1,) + state.shape)
+    totals = gathered[:, state_size:]
     position = lax.axis_index("seq")
     device_order = jnp.arange(totals.shape[0])
     earlier = (device_order < position)[:, None]
@@ -215,7 +216,7 @@
         * score_scale
     )
     key_pos = key_start + jnp.arange(key_count)
-    allowed = (key_pos[None, :] <= query_pos[:, None])[None, :, :]
+    allowed = ((key_pos[None, :] <= query_pos[:, None]) & (key_pos[None, :] >= 0))[None, :, :]
     scores = jnp.where(allowed, scores, -1e30)
     new_max = jnp.maximum(old_max, jnp.max(scores, axis=-1))
     expos = jnp.where(allowed, jnp.exp(scores - new_max[:, :, None]), 0.0)
@@ -263,18 +264,20 @@
     part2 = jnp.dot(normed_all, projection, preferred_element_type=jnp.float32).astype(
         jnp.bfloat16
     )
-    queries = lax.psum_scatter(part2[:, :head_width], "seq", scatter_dimension=0, tiled=True)
-    keys_values = lax.psum(part2[:, head_width:], "seq")
-    queries = queries.reshape(tok_rows, heads_here, DH)
+    reduced = lax.psum_scatter(part2, "seq", scatter_dimension=0, tiled=True)
+    queries = reduced[:, :head_width].reshape(tok_rows, heads_here, DH)
+    kv_own = reduced[:, head_width:]
     query_pos = mine_b * tok_rows + jnp.arange(tok_rows)
     state = (
         jnp.full((heads_here, tok_rows), -1e30, jnp.float32),
         jnp.zeros((heads_here, tok_rows), jnp.float32),
         jnp.zeros((heads_here, tok_rows, DH), jnp.float32),
     )
-    for blk in range(n_seq):
-        kv_block = keys_values[blk * tok_rows : (blk + 1) * tok_rows]
-        state = attend_block(queries, query_pos, state, kv_block, blk * tok_rows)
+    earlier_kv = [from_behind(kv_own, "seq", dist) for dist in range(1, n_seq)]
+    state = attend_block(queries, query_pos, state, kv_own, mine_b * tok_rows)
+    for dist in range(1, n_seq):
+        key_start = (mine_b - dist) * tok_rows
+        state = attend_block(queries, query_pos, state, earlier_kv[dist - 1], key_start)
     _, row_total, weighted = state
     attended = (
         jnp.transpose(weighted / row_total[:, :, None], (1, 0, 2))

time: 558 us -> 571 us (1.023)
  the two profiles are of different devices: /device:TPU:21 before, /device:TPU:28 now
where the time goes in v2:
time: 571 us; the launch traced here: 567 us
  waiting for transfers between devices  389 us (68%)
  matrix products  70.3 us (12%)
  local copies, waits for them, and re-layouts  38.9 us (7%)
  other arithmetic  26 us (5%)
  blocking collectives  19 us (3%)
  between operations  14.3 us (3%)
  starting transfers between devices  9.71 us (2%)
    ppermute x1, waiting for transfers between devices, shards_fast(): lax.ppermute(mixed_sum.astype(jnp.bfloat16), ('heads', 'seq'), swap)  101 us
    all_gather x1, waiting for transfers between devices, shards_fast(): lin_all = lax.all_gather(lin_out, 'seq', axis=0, tiled=True)  78.9 us
    all_gather x1, waiting for transfers between devices, shards_fast(): normed_all = lax.all_gather(normed, 'heads', axis=0, tiled=True)  45.3 us
    reduce_scatter x1, waiting for transfers between devices, shards_fast(): reduced = lax.psum_scatter(part2, 'seq', scatter_dimension=0, tiled=True)  41.8 us
    reduce_scatter x1, waiting for transfers between devices, shards_fast(): own_sum = lax.psum_scatter(part, 'heads', scatter_dimension=0, tiled=True)  40.5 us
    ppermute x1, waiting for transfers between devices, shards_fast(): stream_t = lax.ppermute(stream, ('heads', 'seq'), swap)  30.6 us
    ppermute x3, waiting for transfers between devices, from_behind(): lax.ppermute(value, axis, [(source, source + steps) for source in range(l...  29.5 us
    unnamed x43, local copies, waits for them, and re-layouts  25.2 us
  transfers between devices with their start and end apart: 10, of which 10 were waited for; matrix products, arithmetic and copies ran while one was open for 6% of the time, Pallas kernels for 0%

profile of v2, /device:TPU:28, one launch (start us, length us, event | category | flops | bytes accessed | tf_op | source)
XLA Modules:
  0.0 567.0 jit_solution(838677574151914979)
XLA Ops:
  29.3 3.3 maximum_bitcast_fusion
  40.8 3.4 fusion.38
  44.2 4.3 fusion.42
  48.5 3.3 fusion.40
  51.9 4.5 fusion.41
  56.3 20.9 %all-gather.10.cloned.1.call-done = bf16[4,1,131080]{2,1,0:T(2,128)(2,1)} async-done(((bf16[1,1,131080]{2,1,0:T(2,128)(2,1)}), bf16[4,1,131080]{2,1,0:T(2,128)(2,1)}) %all-gather.10.cloned.1.call-update) | async-done | bytes 1048656 | tf_op jit(solution)/shard_map/all_gather | solution.py:185
  90.5 78.9 %all-gather.6.cloned.1.call-done = bf16[2048,1024]{0,1:T(8,128)(2,1)} async-done(((bf16[512,1024]{0,1:T(8,128)(2,1)}), bf16[2048,1024]{0,1:T(8,128)(2,1)}) %all-gather.6.cloned.1.call-update) | async-done | bytes 4194320 | tf_op jit(solution)/shard_map/all_gather | solution.py:246
  169.3 11.0 %convolution_convert_fusion.1 = bf16[2048,1536]{1,0:T(8,128)(2,1)} fusion(bf16[2048,1024]{0,1:T(8,128)(2,1)} %all-gather.6.cloned.1.call-done, bf16[1024,1536]{1,0:T(8,128)(2,1)S(1)} %copy-done), kind=kOutput, calls=%fused_computation.9 | convolution fusion | flops 6445596672 | bytes 13631488 | tf_op jit(solution)/shard_map/dot_general | solution.py:247
  183.2 6.2 %all-gather.1 = bf16[4,1,1536]{2,1,0:T(2,128)(2,1)S(1)} all-gather(bf16[1,1,1536]{2,1,0:T(2,128)(2,1)S(1)} %reshape.428), channel_id=1, replica_groups=mesh['groups'=2,'heads'=4,'seq'=4] {'heads'}, dimensions={0}, use_global_device_ids=true | all-gather | bytes 15360 | tf_op jit(solution)/shard_map/all_gather | solution.py:253
  189.6 30.6 %collective-permute-done = bf16[512,1536]{1,0:T(8,128)(2,1)S(1)} collective-permute-done((bf16[512,1536]{1,0:T(8,128)(2,1)}, bf16[512,1536]{1,0:T(8,128)(2,1)S(1)}, u32[]{:S(2)}, u32[]{:S(2)}) %collective-permute-start) | collective-permute-done | bytes 1572896 | tf_op jit(solution)/shard_map/ppermute | solution.py:243
  220.2 40.5 %reduce-scatter.3.cloned.1.call-done = bf16[512,1536]{1,0:T(8,128)(2,1)} async-done(((bf16[2048,1536]{1,0:T(8,128)(2,1)}), bf16[512,1536]{1,0:T(8,128)(2,1)}) %reduce-scatter.3.cloned.1.call-update) | async-done | bytes 1572880 | tf_op jit(solution)/shard_map/reduce_scatter | solution.py:248
  262.8 12.8 %psum.7 = f32[512]{0:T(512)S(1)} all-reduce(f32[512]{0:T(512)S(1)} %multiply_reduce_fusion), channel_id=1, replica_groups=mesh['groups'=2,'heads'=4,'seq'=4] {'seq'}, use_global_device_ids=true, to_apply=%region_12.13 | all-reduce | flops 512 | bytes 4096 | tf_op jit(solution)/shard_map/psum | solution.py:251
  279.2 45.3 %all-gather.8.cloned.1.call-done = bf16[2048,1536]{1,0:T(8,128)(2,1)} async-done(((bf16[512,1536]{1,0:T(8,128)(2,1)}), bf16[2048,1536]{1,0:T(8,128)(2,1)}) %all-gather.8.cloned.1.call-update) | async-done | bytes 6291472 | tf_op jit(solution)/shard_map/all_gather | solution.py:260
  324.5 12.9 %convolution_convert_fusion = bf16[2048,1280]{1,0:T(8,128)(2,1)} fusion(bf16[2048,1536]{1,0:T(8,128)(2,1)} %all-gather.8.cloned.1.call-done, bf16[1536,256]{1,0:T(8,128)(2,1)S(1)} %dynamic-slice_bitcast_fusion, bf16[1536,1024]{1,0:T(8,128)(2,1)} %param.16), kind=kOutput, calls=%fused_computation.8 | convolution fusion | flops 8063549440 | bytes 15466496 | tf_op jit(solution)/shard_map/dot_general | solution.py:264
  342.9 101.0 %collective-permute-done.1 = bf16[512,1536]{1,0:T(8,128)(2,1)S(1)} collective-permute-done((bf16[512,1536]{1,0:T(8,128)(2,1)S(1)}, bf16[512,1536]{1,0:T(8,128)(2,1)S(1)}, u32[]{:S(2)}, u32[]{:S(2)}) %collective-permute-start.1) | collective-permute-done | bytes 1572896 | tf_op jit(solution)/shard_map/ppermute | solution.py:250
  443.9 41.8 %reduce-scatter.5.cloned.1.call-done = bf16[512,1280]{1,0:T(8,128)(2,1)} async-done(((bf16[2048,1280]{1,0:T(8,128)(2,1)}), bf16[512,1280]{1,0:T(8,128)(2,1)}) %reduce-scatter.5.cloned.1.call-update) | async-done | bytes 1310736 | tf_op jit(solution)/shard_map/reduce_scatter | solution.py:267
  493.6 15.3 %collective-permute-done.2 = bf16[512,256]{1,0:T(8,128)(2,1)S(1)} collective-permute-done((bf16[512,256]{1,0:T(8,128)(2,1)S(1)}, bf16[512,256]{1,0:T(8,128)(2,1)S(1)}, u32[]{:S(2)}, u32[]{:S(2)}) %collective-permute-start.2) | collective-permute-done | bytes 262176 | tf_op jit(solution)/shard_map/ppermute | solution.py:16
  510.4 4.6 collective-permute-done.4
  516.6 9.7 %collective-permute-done.3 = bf16[512,256]{1,0:T(8,128)(2,1)S(1)} collective-permute-done((bf16[512,256]{1,0:T(8,128)(2,1)S(1)}, bf16[512,256]{1,0:T(8,128)(2,1)S(1)}, u32[]{:S(2)}, u32[]{:S(2)}) %collective-permute-start.3) | collective-permute-done | bytes 262176 | tf_op jit(solution)/shard_map/ppermute | solution.py:16
  526.2 4.8 fusion.2
  531.0 4.2 fusion.4
  535.2 6.3 %fusion.8 = (f32[8,512]{1,0:T(8,128)S(1)}, f32[8,512]{1,0:T(8,128)S(1)}) fusion(f32[512,512,8]{1,0,2:T(8,128)} %get-tuple-element.46, f32[8,512]{1,0:T(8,128)S(1)} %get-tuple-element.18, pred[512,512]{0,1:T(8,128)(4,1)S(1)} %copy-done.9, f32[8,512]{1,0:T(8,128)S(1)} %get-tuple-element.17, f32[512,512,8]{1,0,2:T(8,128)S(1)} %get-tuple-element.44, ...), kind=kLoop, calls=%fused_computation.18 | loop fusion | flops 20963328 | bytes 17367040 | tf_op jit(solution)/shard_map/reduce_sum | solution.py:224
  545.9 5.6 fusion.14
  551.5 3.8 fusion.31
  (123 shorter events, 77.6 us)
Async XLA Ops:
  7.2 162.2 %copy-start = (bf16[1024,1536]{1,0:T(8,128)(2,1)S(1)}, bf16[1024,1536]{1,0:T(8,128)(2,1)}, u32[]{:S(2)}) copy-start(bf16[1024,1536]{1,0:T(8,128)(2,1)} %param.14) | copy-start | bytes 9437188
  7.2 70.1 %all-gather.10.cloned.1.call-start = ((), (), s32[]{:S(2)}) async-start(), calls=%async_computation.6 | async-start | bytes 2624000 | tf_op jit(solution)/shard_map/all_gather | solution.py:185
  23.8 11.4 %copy-start.12 = (f32[512,8]{0,1:T(8,128)S(1)}, f32[512,8]{0,1:T(8,128)}, u32[]{:S(2)}) copy-start(f32[512,8]{0,1:T(8,128)} %param.12) | copy-start | bytes 49156
  32.6 136.7 %all-gather.6.cloned.1.call-start = ((), (), s32[]{:S(2)}) async-start(), calls=%async_computation.2 | async-start | bytes 5242880 | tf_op jit(solution)/shard_map/all_gather | solution.py:246
  81.3 1.9 copy-start.4
  81.3 1.9 copy-start.5
  81.3 2.2 copy-start.6
  90.0 170.7 %reduce-scatter.3.cloned.1.call-start = ((), (), s32[]{:S(2)}) async-start(), calls=%async_computation.3 | async-start | bytes 7864320 | tf_op jit(solution)/shard_map/reduce_scatter | solution.py:248
  180.3 2.8 copy-start.14
  180.4 144.2 %all-gather.8.cloned.1.call-start = ((), (), s32[]{:S(2)}) async-start(), calls=%async_computation.4 | async-start | bytes 7864320 | tf_op jit(solution)/shard_map/all_gather | solution.py:260
  180.4 39.8 %collective-permute-start = (bf16[512,1536]{1,0:T(8,128)(2,1)}, bf16[512,1536]{1,0:T(8,128)(2,1)S(1)}, u32[]{:S(2)}, u32[]{:S(2)}) collective-permute-start(bf16[512,1536]{1,0:T(8,128)(2,1)} %param.13), channel_id=1, source_target_pairs={{0,0},{1,4},{2,8},{3,12},{4,1},{5,5},{6,9},{7,13},{8,2},{9,6},{10,... | collective-permute-start | bytes 4718600 | tf_op jit(solution)/shard_map/ppermute | solution.py:243
  260.7 14.9 %copy-start.2 = (bf16[512,1536]{1,0:T(8,128)(2,1)S(1)}, bf16[512,1536]{1,0:T(8,128)(2,1)}, u32[]{:S(2)}) copy-start(bf16[512,1536]{1,0:T(8,128)(2,1)} %reduce-scatter.3.cloned.1.call-done) | copy-start | bytes 4718596
  278.0 207.7 %reduce-scatter.5.cloned.1.call-start = ((), (), s32[]{:S(2)}) async-start(), calls=%async_computation.5 | async-start | bytes 6553600 | tf_op jit(solution)/shard_map/reduce_scatter | solution.py:267
  337.4 1.4 copy-start.8
  338.8 105.1 %collective-permute-start.1 = (bf16[512,1536]{1,0:T(8,128)(2,1)S(1)}, bf16[512,1536]{1,0:T(8,128)(2,1)S(1)}, u32[]{:S(2)}, u32[]{:S(2)}) collective-permute-start(bf16[512,1536]{1,0:T(8,128)(2,1)S(1)} %copy-done.8), channel_id=1, source_target_pairs={{0,0},{1,4},{2,8},{3,12},{4,1},{5,5},{6,9},{7,13},{8,2},{9,6},{10,... | collective-permute-start | bytes 4718600 | tf_op jit(solution)/shard_map/ppermute | solution.py:250
  443.9 49.7 %copy-start.7 = (bf16[512,1536]{1,0:T(8,128)(2,1)}, bf16[512,1536]{1,0:T(8,128)(2,1)S(1)}, u32[]{:S(2)}) copy-start(bf16[512,1536]{1,0:T(8,128)(2,1)S(1)} %collective-permute-done.1) | copy-start | bytes 4718596
  486.7 22.2 %collective-permute-start.2 = (bf16[512,256]{1,0:T(8,128)(2,1)S(1)}, bf16[512,256]{1,0:T(8,128)(2,1)S(1)}, u32[]{:S(2)}, u32[]{:S(2)}) collective-permute-start(bf16[512,256]{1,0:T(8,128)(2,1)S(1)} %slice.154), channel_id=1, source_target_pairs={{0,1},{1,2},{2,3},{4,5},{5,6},{6,7},{8,9},{9,10},{10,11},{12,13},{... | collective-permute-start | bytes 786440 | tf_op jit(solution)/shard_map/ppermute | solution.py:16
  488.0 27.0 %collective-permute-start.4 = (bf16[512,256]{1,0:T(8,128)(2,1)S(1)}, bf16[512,256]{1,0:T(8,128)(2,1)S(1)}, u32[]{:S(2)}, u32[]{:S(2)}) collective-permute-start(bf16[512,256]{1,0:T(8,128)(2,1)S(1)} %slice.154), channel_id=1, source_target_pairs={{0,3},{4,7},{8,11},{12,15},{16,19},{20,23},{24,27},{28,31}} | collective-permute-start | bytes 786440 | tf_op jit(solution)/shard_map/ppermute | solution.py:16
  489.3 37.0 %collective-permute-start.3 = (bf16[512,256]{1,0:T(8,128)(2,1)S(1)}, bf16[512,256]{1,0:T(8,128)(2,1)S(1)}, u32[]{:S(2)}, u32[]{:S(2)}) collective-permute-start(bf16[512,256]{1,0:T(8,128)(2,1)S(1)} %slice.154), channel_id=1, source_target_pairs={{0,2},{1,3},{4,6},{5,7},{8,10},{9,11},{12,14},{13,15},{16,18},{17,... | collective-permute-start | bytes 786440 | tf_op jit(solution)/shard_map/ppermute | solution.py:16
  490.6 18.3 %copy-start.10 = (pred[512,512]{0,1:T(8,128)(4,1)S(1)}, pred[512,512]{0,1:T(8,128)(4,1)}, u32[]{:S(2)}) copy-start(pred[512,512]{0,1:T(8,128)(4,1)} %get-tuple-element.40) | copy-start | bytes 786436
  490.6 18.3 %copy-start.13 = (bf16[512,1280]{1,0:T(8,128)(2,1)S(1)}, bf16[512,1280]{1,0:T(8,128)(2,1)}, u32[]{:S(2)}) copy-start(bf16[512,1280]{1,0:T(8,128)(2,1)} %reduce-scatter.5.cloned.1.call-done) | copy-start | bytes 3932164
  515.0 11.2 %copy-start.9 = (pred[512,512]{0,1:T(8,128)(4,1)S(1)}, pred[512,512]{0,1:T(8,128)(4,1)}, u32[]{:S(2)}) copy-start(pred[512,512]{0,1:T(8,128)(4,1)} %get-tuple-element.39) | copy-start | bytes 786436
  526.2 4.8 copy-start.11
  551.5 8.7 %copy-start.1 = (bf16[1024,1536]{1,0:T(8,128)(2,1)S(1)}, bf16[1024,1536]{1,0:T(8,128)(2,1)}, u32[]{:S(2)}) copy-start(bf16[1024,1536]{1,0:T(8,128)(2,1)} %param.14) | copy-start | bytes 9437188
  (1 other events, 0.8 us)
Sparse Core Ops, SparseCore 0:
  32.7 44.4 all-gather.9
  90.1 79.1 all-gather.5
  180.5 80.1 reduce-scatter.2
  278.1 46.3 all-gather.7
  337.5 148.1 reduce-scatter.4

commit v3 on v2

--- a/solution.py
+++ b/solution.py
@@ -181,11 +181,10 @@
         outs.append(out)
     local_out = jnp.concatenate(outs, axis=0)
     decay_total = jnp.sum(log_decay, axis=0)
-    packed = jnp.concatenate([state.reshape(-1), decay_total]).astype(jnp.bfloat16)
-    gathered = lax.all_gather(packed, "seq", axis=0, tiled=False).astype(jnp.float32)
-    state_size = state.size
-    states = gathered[:, :state_size].reshape((-1,) + state.shape)
-    totals = gathered[:, state_size:]
+    totals = lax.all_gather(decay_total[None].astype(jnp.bfloat16), "seq", axis=0, tiled=True)
+    states = lax.all_gather(state[None].astype(jnp.bfloat16), "seq", axis=0, tiled=True)
+    totals = totals.astype(jnp.float32)
+    states = states.astype(jnp.float32)
     position = lax.axis_index("seq")
     device_order = jnp.arange(totals.shape[0])
     earlier = (device_order < position)[:, None]
@@ -260,13 +259,12 @@
     normed_all = lax.all_gather(normed, "heads", axis=0, tiled=True)
     kv_group = mine_a * heads_here // (QUERY_HEADS // KVH)
     kv_mine = lax.dynamic_index_in_dim(kv_weight, kv_group, 0, keepdims=False)
-    projection = jnp.concatenate([query_weight, kv_mine], axis=1)
-    part2 = jnp.dot(normed_all, projection, preferred_element_type=jnp.float32).astype(
-        jnp.bfloat16
-    )
-    reduced = lax.psum_scatter(part2, "seq", scatter_dimension=0, tiled=True)
-    queries = reduced[:, :head_width].reshape(tok_rows, heads_here, DH)
-    kv_own = reduced[:, head_width:]
+    q_part = jnp.dot(normed_all, query_weight, preferred_element_type=jnp.float32)
+    kv_part = jnp.dot(normed_all, kv_mine, preferred_element_type=jnp.float32)
+    queries = lax.psum_scatter(
+        q_part.astype(jnp.bfloat16), "seq", scatter_dimension=0, tiled=True
+    ).reshape(tok_rows, heads_here, DH)
+    kv_own = lax.psum_scatter(kv_part.astype(jnp.bfloat16), "seq", scatter_dimension=0, tiled=True)
     query_pos = mine_b * tok_rows + jnp.arange(tok_rows)
     state = (
         jnp.full((heads_here, tok_rows), -1e30, jnp.float32),

time: 571 us -> 548 us (0.960)
  the two profiles are of different devices: /device:TPU:28 before, /device:TPU:21 now
where the time goes in v3:
time: 548 us; the launch traced here: 543 us
  waiting for transfers between devices  365 us (67%)
  matrix products  76.8 us (14%)
  local copies, waits for them, and re-layouts  29.8 us (5%)
  other arithmetic  22.5 us (4%)
  blocking collectives  22.5 us (4%)
  between operations  15.4 us (3%)
  starting transfers between devices  10.8 us (2%)
    reduce_scatter x1, waiting for transfers between devices, shards_fast(): lax.psum_scatter(q_part.astype(jnp.bfloat16), 'seq', scatter_dimension=0,...  116 us
    all_gather x1, waiting for transfers between devices, shards_fast(): lin_all = lax.all_gather(lin_out, 'seq', axis=0, tiled=True)  81.7 us
    all_gather x1, waiting for transfers between devices, shards_fast(): normed_all = lax.all_gather(normed, 'heads', axis=0, tiled=True)  49.3 us
    ppermute x1, waiting for transfers between devices, shards_fast(): lax.ppermute(mixed_sum.astype(jnp.bfloat16), ('heads', 'seq'), swap)  42.9 us
    reduce_scatter x1, waiting for transfers between devices, shards_fast(): own_sum = lax.psum_scatter(part, 'heads', scatter_dimension=0, tiled=True)  42.7 us
    ppermute x1, waiting for transfers between devices, shards_fast(): stream_t = lax.ppermute(stream, ('heads', 'seq'), swap)  28.8 us
    unnamed x37, local copies, waits for them, and re-layouts  18.9 us
    dot_general x4, matrix products, attend_block(): jnp.einsum('hts,sd->htd', prob_bf16, value_part, preferred_element_type=j...  13.7 us
  transfers between devices with their start and end apart: 11, of which 7 were waited for; matrix products, arithmetic and copies ran while one was open for 8% of the time, Pallas kernels for 0%

profile of v3, /device:TPU:21, one launch (start us, length us, event | category | flops | bytes accessed | tf_op | source)
XLA Modules:
  0.0 542.8 jit_solution(15144506512457973695)
XLA Ops:
  30.2 7.1 %all-reduce = bf16[32]{0:T(256)(128)(2,1)S(1)} all-reduce(bf16[32]{0:T(256)(128)(2,1)S(1)} %dynamic-update-slice), channel_id=2, replica_groups=mesh['groups'=2,'heads'=4,'seq'=4] {'seq'}, use_global_device_ids=true, to_apply=%add | all-reduce | flops 32 | bytes 128
  45.4 3.3 fusion.35
  48.8 4.3 fusion.39
  53.1 3.3 fusion.37
  56.4 4.5 fusion.38
  62.4 4.5 multiply_reduce_fusion.2
  71.2 81.7 %all-gather.7.cloned.1.call-done = bf16[2048,1024]{0,1:T(8,128)(2,1)} async-done(((bf16[512,1024]{0,1:T(8,128)(2,1)}), bf16[2048,1024]{0,1:T(8,128)(2,1)}) %all-gather.7.cloned.1.call-update) | async-done | bytes 4194320 | tf_op jit(solution)/shard_map/all_gather | solution.py:245
  152.9 11.0 %convolution_convert_fusion = bf16[2048,1536]{1,0:T(8,128)(2,1)} fusion(bf16[2048,1024]{0,1:T(8,128)(2,1)} %all-gather.7.cloned.1.call-done, bf16[1024,1536]{1,0:T(8,128)(2,1)S(1)} %copy-done), kind=kOutput, calls=%fused_computation.8 | convolution fusion | flops 6445596672 | bytes 13631488 | tf_op jit(solution)/shard_map/dot_general | solution.py:246
  166.8 6.5 %all-gather.2 = bf16[4,1,1536]{2,1,0:T(2,128)(2,1)S(1)} all-gather(bf16[1,1,1536]{2,1,0:T(2,128)(2,1)S(1)} %reshape.405), channel_id=1, replica_groups=mesh['groups'=2,'heads'=4,'seq'=4] {'heads'}, dimensions={0}, use_global_device_ids=true | all-gather | bytes 15360 | tf_op jit(solution)/shard_map/all_gather | solution.py:252
  173.6 28.8 %collective-permute-done = bf16[512,1536]{1,0:T(8,128)(2,1)S(1)} collective-permute-done((bf16[512,1536]{1,0:T(8,128)(2,1)}, bf16[512,1536]{1,0:T(8,128)(2,1)S(1)}, u32[]{:S(2)}, u32[]{:S(2)}) %collective-permute-start) | collective-permute-done | bytes 1572896 | tf_op jit(solution)/shard_map/ppermute | solution.py:242
  202.3 42.7 %reduce-scatter.4.cloned.1.call-done = bf16[512,1536]{1,0:T(8,128)(2,1)} async-done(((bf16[2048,1536]{1,0:T(8,128)(2,1)}), bf16[512,1536]{1,0:T(8,128)(2,1)}) %reduce-scatter.4.cloned.1.call-update) | async-done | bytes 1572880 | tf_op jit(solution)/shard_map/reduce_scatter | solution.py:247
  247.1 8.8 %psum.7 = f32[512]{0:T(512)S(1)} all-reduce(f32[512]{0:T(512)S(1)} %multiply_reduce_fusion), channel_id=1, replica_groups=mesh['groups'=2,'heads'=4,'seq'=4] {'seq'}, use_global_device_ids=true, to_apply=%region_12.13 | all-reduce | flops 512 | bytes 4096 | tf_op jit(solution)/shard_map/psum | solution.py:250
  258.4 49.3 %all-gather.9.cloned.1.call-done = bf16[2048,1536]{1,0:T(8,128)(2,1)} async-done(((bf16[512,1536]{1,0:T(8,128)(2,1)}), bf16[2048,1536]{1,0:T(8,128)(2,1)}) %all-gather.9.cloned.1.call-update) | async-done | bytes 6291472 | tf_op jit(solution)/shard_map/all_gather | solution.py:259
  307.7 5.7 %convolution_convert_fusion.2 = bf16[2048,256]{1,0:T(8,128)(2,1)} fusion(bf16[2048,1536]{1,0:T(8,128)(2,1)} %all-gather.9.cloned.1.call-done, bf16[4,1536,256]{2,1,0:T(8,128)(2,1)} %param.17, s32[]{:T(128)S(6)} %select_n.73), kind=kOutput, calls=%fused_computation.34 | convolution fusion | flops 1611137024 | bytes 8126468 | tf_op jit(solution)/shard_map/dot_general | solution.py:263
  313.5 11.1 %convolution_convert_fusion.1 = bf16[2048,1024]{1,0:T(8,128)(2,1)} fusion(bf16[2048,1536]{1,0:T(8,128)(2,1)} %all-gather.9.cloned.1.call-done, bf16[1536,1024]{1,0:T(8,128)(2,1)S(1)} %copy-done.10), kind=kOutput, calls=%fused_computation.29 | convolution fusion | flops 6444548096 | bytes 13631488 | tf_op jit(solution)/shard_map/dot_general | solution.py:262
  324.6 3.3 collective-permute-start.1
  329.1 42.9 %collective-permute-done.1 = bf16[512,1536]{1,0:T(8,128)(2,1)} collective-permute-done((bf16[512,1536]{1,0:T(8,128)(2,1)}, bf16[512,1536]{1,0:T(8,128)(2,1)}, u32[]{:S(2)}, u32[]{:S(2)}) %collective-permute-start.1) | collective-permute-done | bytes 1572896 | tf_op jit(solution)/shard_map/ppermute | solution.py:249
  372.0 3.5 reduce-scatter.6.cloned.1.call-done
  379.6 116.1 %reduce-scatter.8.cloned.1.call-done = bf16[512,1024]{1,0:T(8,128)(2,1)} async-done(((bf16[2048,1024]{1,0:T(8,128)(2,1)}), bf16[512,1024]{1,0:T(8,128)(2,1)}) %reduce-scatter.8.cloned.1.call-update) | async-done | bytes 1048592 | tf_op jit(solution)/shard_map/reduce_scatter | solution.py:264
  501.8 4.8 fusion.2
  506.6 4.0 fusion.4
  510.7 6.4 %fusion.8 = (f32[8,512]{1,0:T(8,128)S(1)}, f32[8,512]{1,0:T(8,128)S(1)}) fusion(f32[512,512,8]{1,0,2:T(8,128)} %get-tuple-element.44, f32[8,512]{1,0:T(8,128)S(1)} %get-tuple-element.16, pred[512,512]{0,1:T(8,128)(4,1)S(1)} %get-tuple-element.37, f32[8,512]{1,0:T(8,128)S(1)} %get-tuple-element.15, f32[512,512,8]{1,0,2:T(8,128)S(1)} %get-tuple-element.42, ...), kind=kLoop, calls=%fused_computation.17 | loop fusion | flops 20963328 | bytes 17367040 | tf_op jit(solution)/shard_map/reduce_sum | solution.py:223
  521.5 5.6 %fusion.14 = f32[8,512,128]{1,2,0:T(8,128)S(1)} fusion(f32[512,512,8]{1,0,2:T(8,128)} %get-tuple-element.44, f32[8,512]{1,0:T(8,128)S(1)} %get-tuple-element.16, pred[512,512]{0,1:T(8,128)(4,1)S(1)} %get-tuple-element.37, bf16[512,256]{1,0:T(8,128)(2,1)S(1)} %collective-permute-done.3), kind=kOutput, calls=%fused_computation.22 | convolution fusion | flops 547356672 | bytes 10895360 | tf_op jit(solution)/shard_map/hts,sd->htd/dot_general | solution.py:225
  527.1 3.8 fusion.28
  (118 shorter events, 64.4 us)
Async XLA Ops:
  7.2 145.8 %copy-start = (bf16[1024,1536]{1,0:T(8,128)(2,1)S(1)}, bf16[1024,1536]{1,0:T(8,128)(2,1)}, u32[]{:S(2)}) copy-start(bf16[1024,1536]{1,0:T(8,128)(2,1)} %param.14) | copy-start | bytes 9437188
  7.2 53.7 %all-gather.11.cloned.1.call-start = ((), (), s32[]{:S(2)}) async-start(), calls=%async_computation.8 | async-start | bytes 1310720 | tf_op jit(solution)/shard_map/all_gather | solution.py:185
  14.7 13.7 %copy-start.5 = (f32[512,8]{0,1:T(8,128)S(1)}, f32[512,8]{0,1:T(8,128)}, u32[]{:S(2)}) copy-start(f32[512,8]{0,1:T(8,128)} %param.12) | copy-start | bytes 49156
  14.7 14.0 %copy-start.11 = (u32[32]{0:T(128)S(1)}, u32[32]{0:T(128)}, u32[]{:S(2)}) copy-start(u32[32]{0:T(128)} %constant.79) | copy-start | bytes 388
  25.0 0.8 copy-start.4
  28.3 124.6 %all-gather.7.cloned.1.call-start = ((), (), s32[]{:S(2)}) async-start(), calls=%async_computation.3 | async-start | bytes 5242880 | tf_op jit(solution)/shard_map/all_gather | solution.py:245
  70.7 174.3 %reduce-scatter.4.cloned.1.call-start = ((), (), s32[]{:S(2)}) async-start(), calls=%async_computation.4 | async-start | bytes 7864320 | tf_op jit(solution)/shard_map/reduce_scatter | solution.py:247
  163.9 2.9 copy-start.9
  164.0 143.7 %all-gather.9.cloned.1.call-start = ((), (), s32[]{:S(2)}) async-start(), calls=%async_computation.5 | async-start | bytes 7864320 | tf_op jit(solution)/shard_map/all_gather | solution.py:259
  164.0 38.3 %collective-permute-start = (bf16[512,1536]{1,0:T(8,128)(2,1)}, bf16[512,1536]{1,0:T(8,128)(2,1)S(1)}, u32[]{:S(2)}, u32[]{:S(2)}) collective-permute-start(bf16[512,1536]{1,0:T(8,128)(2,1)} %param.13), channel_id=1, source_target_pairs={{0,0},{1,4},{2,8},{3,12},{4,1},{5,5},{6,9},{7,13},{8,2},{9,6},{10,... | collective-permute-start | bytes 4718600 | tf_op jit(solution)/shard_map/ppermute | solution.py:242
  245.0 11.0 %copy-start.3 = (bf16[512,1536]{1,0:T(8,128)(2,1)S(1)}, bf16[512,1536]{1,0:T(8,128)(2,1)}, u32[]{:S(2)}) copy-start(bf16[512,1536]{1,0:T(8,128)(2,1)} %reduce-scatter.4.cloned.1.call-done) | copy-start | bytes 4718596
  258.3 117.2 %reduce-scatter.6.cloned.1.call-start = ((), (), s32[]{:S(2)}) async-start(), calls=%async_computation.6 | async-start | bytes 1310720 | tf_op jit(solution)/shard_map/reduce_scatter | solution.py:267
  258.3 55.1 %copy-start.10 = (bf16[1536,1024]{1,0:T(8,128)(2,1)S(1)}, bf16[1536,1024]{1,0:T(8,128)(2,1)}, u32[]{:S(2)}) copy-start(bf16[1536,1024]{1,0:T(8,128)(2,1)} %param.16) | copy-start | bytes 9437188
  313.4 182.3 %reduce-scatter.8.cloned.1.call-start = ((), (), s32[]{:S(2)}) async-start(), calls=%async_computation.7 | async-start | bytes 5242880 | tf_op jit(solution)/shard_map/reduce_scatter | solution.py:264
  324.6 47.4 %collective-permute-start.1 = (bf16[512,1536]{1,0:T(8,128)(2,1)}, bf16[512,1536]{1,0:T(8,128)(2,1)}, u32[]{:S(2)}, u32[]{:S(2)}) collective-permute-start(bf16[512,1536]{1,0:T(8,128)(2,1)} %get-tuple-element.23), channel_id=1, source_target_pairs={{0,0},{1,4},{2,8},{3,12},{4,1},{5,5},{6,9},{7,13},{8,2},{9,6},{10,... | collective-permute-start | bytes 4718600 | tf_op jit(solution)/shard_map/ppermute | solution.py:249
  375.5 123.1 %collective-permute-start.2 = (bf16[512,256]{1,0:T(8,128)(2,1)}, bf16[512,256]{1,0:T(8,128)(2,1)S(1)}, u32[]{:S(2)}, u32[]{:S(2)}) collective-permute-start(bf16[512,256]{1,0:T(8,128)(2,1)} %reduce-scatter.6.cloned.1.call-done), channel_id=1, source_target_pairs={{0,1},{1,2},{2,3},{4,5},{5,6},{6,7},{8,9},{9,10},{10,11},{12,13},{... | collective-permute-start | bytes 786440 | tf_op jit(solution)/shard_map/ppermute | solution.py:16
  377.4 122.8 %collective-permute-start.4 = (bf16[512,256]{1,0:T(8,128)(2,1)}, bf16[512,256]{1,0:T(8,128)(2,1)S(1)}, u32[]{:S(2)}, u32[]{:S(2)}) collective-permute-start(bf16[512,256]{1,0:T(8,128)(2,1)} %reduce-scatter.6.cloned.1.call-done), channel_id=1, source_target_pairs={{0,3},{4,7},{8,11},{12,15},{16,19},{20,23},{24,27},{28,31}} | collective-permute-start | bytes 786440 | tf_op jit(solution)/shard_map/ppermute | solution.py:16
  378.1 123.7 %collective-permute-start.3 = (bf16[512,256]{1,0:T(8,128)(2,1)}, bf16[512,256]{1,0:T(8,128)(2,1)S(1)}, u32[]{:S(2)}, u32[]{:S(2)}) collective-permute-start(bf16[512,256]{1,0:T(8,128)(2,1)} %reduce-scatter.6.cloned.1.call-done), channel_id=1, source_target_pairs={{0,2},{1,3},{4,6},{5,7},{8,10},{9,11},{12,14},{13,15},{16,18},{17,... | collective-permute-start | bytes 786440 | tf_op jit(solution)/shard_map/ppermute | solution.py:16
  495.7 3.0 copy-start.2
  500.2 1.6 copy-start.7
  510.7 6.4 %copy-start.6 = (bf16[512,256]{1,0:T(8,128)(2,1)S(1)}, bf16[512,256]{1,0:T(8,128)(2,1)}, u32[]{:S(2)}) copy-start(bf16[512,256]{1,0:T(8,128)(2,1)} %reduce-scatter.6.cloned.1.call-done) | copy-start | bytes 786436
  521.5 5.6 %copy-start.8 = (bf16[512,256]{1,0:T(8,128)(2,1)S(1)}, bf16[512,256]{1,0:T(8,128)(2,1)}, u32[]{:S(2)}) copy-start(bf16[512,256]{1,0:T(8,128)(2,1)} %copy-done.7) | copy-start | bytes 786436
  527.1 8.7 %copy-start.1 = (bf16[1024,1536]{1,0:T(8,128)(2,1)S(1)}, bf16[1024,1536]{1,0:T(8,128)(2,1)}, u32[]{:S(2)}) copy-start(bf16[1024,1536]{1,0:T(8,128)(2,1)} %param.14) | copy-start | bytes 9437188
Sparse Core Ops, SparseCore 0:
  28.5 27.9 all-gather.10
  70.9 82.0 all-gather.6
  164.1 80.8 reduce-scatter.3
  258.4 49.2 all-gather.8
  313.5 61.9 reduce-scatter.5
  377.6 118.0 reduce-scatter.7

commit v4 on v3

--- a/solution.py
+++ b/solution.py
@@ -181,10 +181,12 @@
         outs.append(out)
     local_out = jnp.concatenate(outs, axis=0)
     decay_total = jnp.sum(log_decay, axis=0)
-    totals = lax.all_gather(decay_total[None].astype(jnp.bfloat16), "seq", axis=0, tiled=True)
-    states = lax.all_gather(state[None].astype(jnp.bfloat16), "seq", axis=0, tiled=True)
-    totals = totals.astype(jnp.float32)
-    states = states.astype(jnp.float32)
+    pad_rows = 16
+    total_rows = jnp.broadcast_to(decay_total[:, None, None], (heads_here, pad_rows, DH))
+    packed = jnp.concatenate([state, total_rows], axis=1).astype(jnp.bfloat16)
+    gathered = lax.all_gather(packed[None], "seq", axis=0, tiled=True).astype(jnp.float32)
+    states = gathered[:, :, :DH, :]
+    totals = gathered[:, :, DH, 0]
     position = lax.axis_index("seq")
     device_order = jnp.arange(totals.shape[0])
     earlier = (device_order < position)[:, None]

time: 548 us -> 545 us (level)
  blocking collectives: 22.5 us -> 15.7 us
    unnamed x1 -> x0, blocking collectives: 7.13 us -> none
    all_gather x1, waiting for transfers between devices: 0.01 us -> 6.89 us  [lightning_local(): lax.all_gather(packed[None], 'seq', axis=0, tiled=True).astype(jnp.float32)]
    unnamed x37 -> x32, local copies, waits for them, and re-layouts: 18.9 us -> 18.1 us
  transfers between devices with their start and end apart: 11 -> 11, of which waited for: 7 -> 8; matrix products, arithmetic and copies ran while one was open for 8% -> 8% of each run, Pallas kernels for 0% -> 0%
where the time goes in v4:
time: 545 us; the launch traced here: 540 us
  waiting for transfers between devices  369 us (68%)
  matrix products  76.2 us (14%)
  local copies, waits for them, and re-layouts  28.8 us (5%)
  other arithmetic  25 us (5%)
  blocking collectives  15.7 us (3%)
  between operations  14.7 us (3%)
  starting transfers between devices  10.9 us (2%)
    reduce_scatter x1, waiting for transfers between devices, shards_fast(): lax.psum_scatter(q_part.astype(jnp.bfloat16), 'seq', scatter_dimension=0,...  116 us
    all_gather x1, waiting for transfers between devices, shards_fast(): lin_all = lax.all_gather(lin_out, 'seq', axis=0, tiled=True)  78.9 us
    all_gather x1, waiting for transfers between devices, shards_fast(): normed_all = lax.all_gather(normed, 'heads', axis=0, tiled=True)  49 us
    ppermute x1, waiting for transfers between devices, shards_fast(): lax.ppermute(mixed_sum.astype(jnp.bfloat16), ('heads', 'seq'), swap)  42.9 us
    reduce_scatter x1, waiting for transfers between devices, shards_fast(): own_sum = lax.psum_scatter(part, 'heads', scatter_dimension=0, tiled=True)  42.7 us
    ppermute x1, waiting for transfers between devices, shards_fast(): stream_t = lax.ppermute(stream, ('heads', 'seq'), swap)  28.8 us
    unnamed x32, local copies, waits for them, and re-layouts  18.1 us
    dot_general x4, matrix products, attend_block(): jnp.einsum('hts,sd->htd', prob_bf16, value_part, preferred_element_type=j...  13.7 us
  transfers between devices with their start and end apart: 11, of which 8 were waited for; matrix products, arithmetic and copies ran while one was open for 8% of the time, Pallas kernels for 0%

profile of v4, /device:TPU:21, one launch (start us, length us, event | category | flops | bytes accessed | tf_op | source)
XLA Modules:
  0.0 540.1 jit_solution(8769992686377670043)
XLA Ops:
  37.4 3.4 fusion.35
  40.8 4.3 fusion.39
  45.1 3.3 fusion.37
  48.4 4.5 fusion.38
  52.9 6.9 %all-gather.5.cloned.1.call-done = bf16[4,8,144,128]{3,2,1,0:T(8,128)(2,1)} async-done(((bf16[1,8,144,128]{3,2,1,0:T(8,128)(2,1)}), bf16[4,8,144,128]{3,2,1,0:T(8,128)(2,1)}) %all-gather.5.cloned.1.call-update) | async-done | bytes 1179664 | tf_op jit(solution)/shard_map/all_gather | solution.py:187
  62.5 4.5 multiply_reduce_fusion.2
  71.3 78.9 %all-gather.7.cloned.1.call-done = bf16[2048,1024]{0,1:T(8,128)(2,1)} async-done(((bf16[512,1024]{0,1:T(8,128)(2,1)}), bf16[2048,1024]{0,1:T(8,128)(2,1)}) %all-gather.7.cloned.1.call-update) | async-done | bytes 4194320 | tf_op jit(solution)/shard_map/all_gather | solution.py:247
  150.2 11.0 %convolution_convert_fusion = bf16[2048,1536]{1,0:T(8,128)(2,1)} fusion(bf16[2048,1024]{0,1:T(8,128)(2,1)} %all-gather.7.cloned.1.call-done, bf16[1024,1536]{1,0:T(8,128)(2,1)S(1)} %copy-done), kind=kOutput, calls=%fused_computation.8 | convolution fusion | flops 6445596672 | bytes 13631488 | tf_op jit(solution)/shard_map/dot_general | solution.py:248
  164.1 6.5 %all-gather = bf16[4,1,1536]{2,1,0:T(2,128)(2,1)S(1)} all-gather(bf16[1,1,1536]{2,1,0:T(2,128)(2,1)S(1)} %reshape.415), channel_id=1, replica_groups=mesh['groups'=2,'heads'=4,'seq'=4] {'heads'}, dimensions={0}, use_global_device_ids=true | all-gather | bytes 15360 | tf_op jit(solution)/shard_map/all_gather | solution.py:254
  170.9 28.8 %collective-permute-done = bf16[512,1536]{1,0:T(8,128)(2,1)S(1)} collective-permute-done((bf16[512,1536]{1,0:T(8,128)(2,1)}, bf16[512,1536]{1,0:T(8,128)(2,1)S(1)}, u32[]{:S(2)}, u32[]{:S(2)}) %collective-permute-start) | collective-permute-done | bytes 1572896 | tf_op jit(solution)/shard_map/ppermute | solution.py:244
  199.6 42.7 %reduce-scatter.4.cloned.1.call-done = bf16[512,1536]{1,0:T(8,128)(2,1)} async-done(((bf16[2048,1536]{1,0:T(8,128)(2,1)}), bf16[512,1536]{1,0:T(8,128)(2,1)}) %reduce-scatter.4.cloned.1.call-update) | async-done | bytes 1572880 | tf_op jit(solution)/shard_map/reduce_scatter | solution.py:249
  244.4 9.1 %psum.7 = f32[512]{0:T(512)S(1)} all-reduce(f32[512]{0:T(512)S(1)} %multiply_reduce_fusion), channel_id=1, replica_groups=mesh['groups'=2,'heads'=4,'seq'=4] {'seq'}, use_global_device_ids=true, to_apply=%region_12.13 | all-reduce | flops 512 | bytes 4096 | tf_op jit(solution)/shard_map/psum | solution.py:252
  255.9 49.0 %all-gather.9.cloned.1.call-done = bf16[2048,1536]{1,0:T(8,128)(2,1)} async-done(((bf16[512,1536]{1,0:T(8,128)(2,1)}), bf16[2048,1536]{1,0:T(8,128)(2,1)}) %all-gather.9.cloned.1.call-update) | async-done | bytes 6291472 | tf_op jit(solution)/shard_map/all_gather | solution.py:261
  305.0 5.7 %convolution_convert_fusion.2 = bf16[2048,256]{1,0:T(8,128)(2,1)} fusion(bf16[2048,1536]{1,0:T(8,128)(2,1)} %all-gather.9.cloned.1.call-done, bf16[4,1536,256]{2,1,0:T(8,128)(2,1)} %param.17, s32[]{:T(128)S(6)} %select_n.73), kind=kOutput, calls=%fused_computation.34 | convolution fusion | flops 1611137024 | bytes 8126468 | tf_op jit(solution)/shard_map/dot_general | solution.py:265
  310.8 11.1 %convolution_convert_fusion.1 = bf16[2048,1024]{1,0:T(8,128)(2,1)} fusion(bf16[2048,1536]{1,0:T(8,128)(2,1)} %all-gather.9.cloned.1.call-done, bf16[1536,1024]{1,0:T(8,128)(2,1)S(1)} %copy-done.10), kind=kOutput, calls=%fused_computation.29 | convolution fusion | flops 6444548096 | bytes 13631488 | tf_op jit(solution)/shard_map/dot_general | solution.py:264
  321.9 3.3 collective-permute-start.1
  326.4 42.9 %collective-permute-done.1 = bf16[512,1536]{1,0:T(8,128)(2,1)} collective-permute-done((bf16[512,1536]{1,0:T(8,128)(2,1)}, bf16[512,1536]{1,0:T(8,128)(2,1)}, u32[]{:S(2)}, u32[]{:S(2)}) %collective-permute-start.1) | collective-permute-done | bytes 1572896 | tf_op jit(solution)/shard_map/ppermute | solution.py:251
  369.3 3.5 reduce-scatter.6.cloned.1.call-done
  376.8 116.1 %reduce-scatter.8.cloned.1.call-done = bf16[512,1024]{1,0:T(8,128)(2,1)} async-done(((bf16[2048,1024]{1,0:T(8,128)(2,1)}), bf16[512,1024]{1,0:T(8,128)(2,1)}) %reduce-scatter.8.cloned.1.call-update) | async-done | bytes 1048592 | tf_op jit(solution)/shard_map/reduce_scatter | solution.py:266
  499.1 4.8 fusion.2
  503.9 4.0 fusion.4
  508.0 6.4 %fusion.8 = (f32[8,512]{1,0:T(8,128)S(1)}, f32[8,512]{1,0:T(8,128)S(1)}) fusion(f32[512,512,8]{1,0,2:T(8,128)} %get-tuple-element.44, f32[8,512]{1,0:T(8,128)S(1)} %get-tuple-element.16, pred[512,512]{0,1:T(8,128)(4,1)S(1)} %get-tuple-element.37, f32[8,512]{1,0:T(8,128)S(1)} %get-tuple-element.15, f32[512,512,8]{1,0,2:T(8,128)S(1)} %get-tuple-element.42, ...), kind=kLoop, calls=%fused_computation.17 | loop fusion | flops 20963328 | bytes 17367040 | tf_op jit(solution)/shard_map/reduce_sum | solution.py:225
  518.8 5.6 %fusion.14 = f32[8,512,128]{1,2,0:T(8,128)S(1)} fusion(f32[512,512,8]{1,0,2:T(8,128)} %get-tuple-element.44, f32[8,512]{1,0:T(8,128)S(1)} %get-tuple-element.16, pred[512,512]{0,1:T(8,128)(4,1)S(1)} %get-tuple-element.37, bf16[512,256]{1,0:T(8,128)(2,1)S(1)} %collective-permute-done.3), kind=kOutput, calls=%fused_computation.22 | convolution fusion | flops 547356672 | bytes 10895360 | tf_op jit(solution)/shard_map/hts,sd->htd/dot_general | solution.py:227
  524.4 3.8 fusion.28
  (114 shorter events, 65.3 us)
Async XLA Ops:
  7.2 143.1 %copy-start = (bf16[1024,1536]{1,0:T(8,128)(2,1)S(1)}, bf16[1024,1536]{1,0:T(8,128)(2,1)}, u32[]{:S(2)}) copy-start(bf16[1024,1536]{1,0:T(8,128)(2,1)} %param.14) | copy-start | bytes 9437188
  7.2 52.6 %all-gather.5.cloned.1.call-start = ((), (), s32[]{:S(2)}) async-start(), calls=%async_computation.3 | async-start | bytes 1474560 | tf_op jit(solution)/shard_map/all_gather | solution.py:187
  19.8 12.0 %copy-start.5 = (f32[512,8]{0,1:T(8,128)S(1)}, f32[512,8]{0,1:T(8,128)}, u32[]{:S(2)}) copy-start(f32[512,8]{0,1:T(8,128)} %param.12) | copy-start | bytes 49156
  25.7 0.8 copy-start.4
  29.2 121.0 %all-gather.7.cloned.1.call-start = ((), (), s32[]{:S(2)}) async-start(), calls=%async_computation.4 | async-start | bytes 5242880 | tf_op jit(solution)/shard_map/all_gather | solution.py:247
  70.9 171.5 %reduce-scatter.4.cloned.1.call-start = ((), (), s32[]{:S(2)}) async-start(), calls=%async_computation.5 | async-start | bytes 7864320 | tf_op jit(solution)/shard_map/reduce_scatter | solution.py:249
  161.2 2.9 copy-start.9
  161.3 143.7 %all-gather.9.cloned.1.call-start = ((), (), s32[]{:S(2)}) async-start(), calls=%async_computation.6 | async-start | bytes 7864320 | tf_op jit(solution)/shard_map/all_gather | solution.py:261
  161.3 38.3 %collective-permute-start = (bf16[512,1536]{1,0:T(8,128)(2,1)}, bf16[512,1536]{1,0:T(8,128)(2,1)S(1)}, u32[]{:S(2)}, u32[]{:S(2)}) collective-permute-start(bf16[512,1536]{1,0:T(8,128)(2,1)} %param.13), channel_id=1, source_target_pairs={{0,0},{1,4},{2,8},{3,12},{4,1},{5,5},{6,9},{7,13},{8,2},{9,6},{10,... | collective-permute-start | bytes 4718600 | tf_op jit(solution)/shard_map/ppermute | solution.py:244
  242.3 11.3 %copy-start.3 = (bf16[512,1536]{1,0:T(8,128)(2,1)S(1)}, bf16[512,1536]{1,0:T(8,128)(2,1)}, u32[]{:S(2)}) copy-start(bf16[512,1536]{1,0:T(8,128)(2,1)} %reduce-scatter.4.cloned.1.call-done) | copy-start | bytes 4718596
  255.9 116.9 %reduce-scatter.6.cloned.1.call-start = ((), (), s32[]{:S(2)}) async-start(), calls=%async_computation.7 | async-start | bytes 1310720 | tf_op jit(solution)/shard_map/reduce_scatter | solution.py:269
  255.9 54.8 %copy-start.10 = (bf16[1536,1024]{1,0:T(8,128)(2,1)S(1)}, bf16[1536,1024]{1,0:T(8,128)(2,1)}, u32[]{:S(2)}) copy-start(bf16[1536,1024]{1,0:T(8,128)(2,1)} %param.16) | copy-start | bytes 9437188
  310.7 182.3 %reduce-scatter.8.cloned.1.call-start = ((), (), s32[]{:S(2)}) async-start(), calls=%async_computation.8 | async-start | bytes 5242880 | tf_op jit(solution)/shard_map/reduce_scatter | solution.py:266
  321.9 47.4 %collective-permute-start.1 = (bf16[512,1536]{1,0:T(8,128)(2,1)}, bf16[512,1536]{1,0:T(8,128)(2,1)}, u32[]{:S(2)}, u32[]{:S(2)}) collective-permute-start(bf16[512,1536]{1,0:T(8,128)(2,1)} %get-tuple-element.23), channel_id=1, source_target_pairs={{0,0},{1,4},{2,8},{3,12},{4,1},{5,5},{6,9},{7,13},{8,2},{9,6},{10,... | collective-permute-start | bytes 4718600 | tf_op jit(solution)/shard_map/ppermute | solution.py:251
  372.8 123.1 %collective-permute-start.2 = (bf16[512,256]{1,0:T(8,128)(2,1)}, bf16[512,256]{1,0:T(8,128)(2,1)S(1)}, u32[]{:S(2)}, u32[]{:S(2)}) collective-permute-start(bf16[512,256]{1,0:T(8,128)(2,1)} %reduce-scatter.6.cloned.1.call-done), channel_id=1, source_target_pairs={{0,1},{1,2},{2,3},{4,5},{5,6},{6,7},{8,9},{9,10},{10,11},{12,13},{... | collective-permute-start | bytes 786440 | tf_op jit(solution)/shard_map/ppermute | solution.py:16
  374.7 122.8 %collective-permute-start.4 = (bf16[512,256]{1,0:T(8,128)(2,1)}, bf16[512,256]{1,0:T(8,128)(2,1)S(1)}, u32[]{:S(2)}, u32[]{:S(2)}) collective-permute-start(bf16[512,256]{1,0:T(8,128)(2,1)} %reduce-scatter.6.cloned.1.call-done), channel_id=1, source_target_pairs={{0,3},{4,7},{8,11},{12,15},{16,19},{20,23},{24,27},{28,31}} | collective-permute-start | bytes 786440 | tf_op jit(solution)/shard_map/ppermute | solution.py:16
  375.4 123.8 %collective-permute-start.3 = (bf16[512,256]{1,0:T(8,128)(2,1)}, bf16[512,256]{1,0:T(8,128)(2,1)S(1)}, u32[]{:S(2)}, u32[]{:S(2)}) collective-permute-start(bf16[512,256]{1,0:T(8,128)(2,1)} %reduce-scatter.6.cloned.1.call-done), channel_id=1, source_target_pairs={{0,2},{1,3},{4,6},{5,7},{8,10},{9,11},{12,14},{13,15},{16,18},{17,... | collective-permute-start | bytes 786440 | tf_op jit(solution)/shard_map/ppermute | solution.py:16
  493.0 3.0 copy-start.2
  497.5 1.6 copy-start.7
  508.0 6.4 %copy-start.6 = (bf16[512,256]{1,0:T(8,128)(2,1)S(1)}, bf16[512,256]{1,0:T(8,128)(2,1)}, u32[]{:S(2)}) copy-start(bf16[512,256]{1,0:T(8,128)(2,1)} %reduce-scatter.6.cloned.1.call-done) | copy-start | bytes 786436
  518.8 5.6 %copy-start.8 = (bf16[512,256]{1,0:T(8,128)(2,1)S(1)}, bf16[512,256]{1,0:T(8,128)(2,1)}, u32[]{:S(2)}) copy-start(bf16[512,256]{1,0:T(8,128)(2,1)} %copy-done.7) | copy-start | bytes 786436
  524.4 8.7 %copy-start.1 = (bf16[1024,1536]{1,0:T(8,128)(2,1)S(1)}, bf16[1024,1536]{1,0:T(8,128)(2,1)}, u32[]{:S(2)}) copy-start(bf16[1024,1536]{1,0:T(8,128)(2,1)} %param.14) | copy-start | bytes 9437188
Sparse Core Ops, SparseCore 0:
  29.4 30.3 all-gather.4
  71.0 79.2 all-gather.6
  161.4 80.8 reduce-scatter.3
  256.0 48.9 all-gather.8
  310.8 61.9 reduce-scatter.5
  374.9 118.0 reduce-scatter.7

commit v5 on v4

--- a/solution.py
+++ b/solution.py
@@ -206,6 +206,24 @@
     return lin_out
 
 
+def heads_reduce_scatter(part, n_heads):
+    if n_heads != 4:
+        return lax.psum_scatter(part, "heads", scatter_dimension=0, tiled=True).astype(jnp.float32)
+    mine = lax.axis_index("heads")
+    core = mine % 2
+    chip = mine // 2
+    rows = part.shape[0] // n_heads
+    grid = part.reshape(2, 2, rows, part.shape[1])
+    keep1 = lax.dynamic_index_in_dim(grid, core, axis=1, keepdims=False)
+    send1 = lax.dynamic_index_in_dim(grid, 1 - core, axis=1, keepdims=False)
+    recv1 = lax.ppermute(send1, "heads", [(i, i ^ 1) for i in range(n_heads)])
+    chip_sum = keep1.astype(jnp.float32) + recv1.astype(jnp.float32)
+    keep2 = lax.dynamic_index_in_dim(chip_sum, chip, axis=0, keepdims=False)
+    send2 = lax.dynamic_index_in_dim(chip_sum, 1 - chip, axis=0, keepdims=False)
+    recv2 = lax.ppermute(send2.astype(jnp.bfloat16), "heads", [(i, i ^ 2) for i in range(n_heads)])
+    return keep2 + recv2.astype(jnp.float32)
+
+
 def attend_block(queries, query_pos, state_in, kv_block, key_start):
     old_max, row_total, weighted = state_in
     key_count = kv_block.shape[0]
@@ -246,8 +264,8 @@
     lin_out = lightning_local(lin_query, lin_key, lin_value, log_decay)
     lin_all = lax.all_gather(lin_out, "seq", axis=0, tiled=True)
     part = jnp.dot(lin_all, out_weight, preferred_element_type=jnp.float32).astype(jnp.bfloat16)
-    own_sum = lax.psum_scatter(part, "heads", scatter_dimension=0, tiled=True)
-    mixed_sum = stream_t.astype(jnp.float32) + own_sum.astype(jnp.float32)
+    own_sum = heads_reduce_scatter(part, n_heads)
+    mixed_sum = stream_t.astype(jnp.float32) + own_sum
     stream_next = lax.ppermute(mixed_sum.astype(jnp.bfloat16), ("heads", "seq"), swap)
     total_sq = lax.psum(jnp.sum(mixed_sum * mixed_sum, axis=1), "seq")
     cols = mixed_sum.shape[1]

time: 545 us -> 540 us (level)
  waiting for transfers between devices: 369 us -> 301 us
  blocking collectives: 15.7 us -> 73.8 us
  local copies, waits for them, and re-layouts: 28.8 us -> 34.5 us
    all_gather x1, blocking collectives: 6.54 us -> 60.3 us  [shards_fast(): gain_all = lax.all_gather(norm_gain, 'heads', axis=0, tiled=True)]
    reduce_scatter x1 -> x0, waiting for transfers between devices: 42.7 us -> none  [shards_fast(): own_sum = lax.psum_scatter(part, 'heads', scatter_dimension=0, tiled=True)]
    ppermute x1, waiting for transfers between devices: 28.8 us -> 0.01 us  [shards_fast(): stream_t = lax.ppermute(stream, ('heads', 'seq'), swap)]
    unnamed x32 -> x38, local copies, waits for them, and re-layouts: 18.1 us -> 23.4 us
  transfers between devices with their start and end apart: 11 -> 12, of which waited for: 8 -> 7; matrix products, arithmetic and copies ran while one was open for 8% -> 9% of each run, Pallas kernels for 0% -> 0%
where the time goes in v5:
time: 540 us; the launch traced here: 535 us
  waiting for transfers between devices  301 us (56%)
  blocking collectives  73.8 us (14%)
  matrix products  72.3 us (13%)
  local copies, waits for them, and re-layouts  34.5 us (6%)
  other arithmetic  28 us (5%)
  between operations  14.6 us (3%)
  starting transfers between devices  11.5 us (2%)
    reduce_scatter x1, waiting for transfers between devices, shards_fast(): lax.psum_scatter(q_part.astype(jnp.bfloat16), 'seq', scatter_dimension=0,...  116 us
    all_gather x1, waiting for transfers between devices, shards_fast(): lin_all = lax.all_gather(lin_out, 'seq', axis=0, tiled=True)  79.1 us
    all_gather x1, blocking collectives, shards_fast(): gain_all = lax.all_gather(norm_gain, 'heads', axis=0, tiled=True)  60.3 us
    all_gather x1, waiting for transfers between devices, shards_fast(): normed_all = lax.all_gather(normed, 'heads', axis=0, tiled=True)  48.8 us
    ppermute x1, waiting for transfers between devices, shards_fast(): lax.ppermute(mixed_sum.astype(jnp.bfloat16), ('heads', 'seq'), swap)  42.9 us
    unnamed x38, local copies, waits for them, and re-layouts  23.4 us
    dot_general x4, matrix products, attend_block(): jnp.einsum('hts,sd->htd', prob_bf16, value_part, preferred_element_type=j...  13.7 us
    psum x1, blocking collectives, shards_fast(): total_sq = lax.psum(jnp.sum(mixed_sum * mixed_sum, axis=1), 'seq')  13.4 us
  transfers between devices with their start and end apart: 12, of which 7 were waited for; matrix products, arithmetic and copies ran while one was open for 9% of the time, Pallas kernels for 0%

profile of v5, /device:TPU:21, one launch (start us, length us, event | category | flops | bytes accessed | tf_op | source)
XLA Modules:
  0.0 535.3 jit_solution(1729550568251390348)
XLA Ops:
  37.7 3.4 fusion.36
  41.1 4.3 fusion.40
  45.4 3.3 fusion.38
  48.7 4.5 fusion.39
  53.2 6.6 %all-gather.5.cloned.1.call-done = bf16[4,8,144,128]{3,2,1,0:T(8,128)(2,1)} async-done(((bf16[1,8,144,128]{3,2,1,0:T(8,128)(2,1)}), bf16[4,8,144,128]{3,2,1,0:T(8,128)(2,1)}) %all-gather.5.cloned.1.call-update) | async-done | bytes 1179664 | tf_op jit(solution)/shard_map/all_gather | solution.py:187
  62.6 4.5 multiply_reduce_fusion.2
  71.1 79.1 %all-gather.7.cloned.1.call-done = bf16[2048,1024]{0,1:T(8,128)(2,1)} async-done(((bf16[512,1024]{0,1:T(8,128)(2,1)}), bf16[2048,1024]{0,1:T(8,128)(2,1)}) %all-gather.7.cloned.1.call-update) | async-done | bytes 4194320 | tf_op jit(solution)/shard_map/all_gather | solution.py:265
  150.3 9.3 %convolution_convert_fusion = bf16[2048,1536]{1,0:T(8,128)(2,1)S(1)} fusion(bf16[2048,1024]{0,1:T(8,128)(2,1)} %all-gather.7.cloned.1.call-done, bf16[1024,1536]{1,0:T(8,128)(2,1)S(1)} %copy-done), kind=kOutput, calls=%fused_computation.8 | convolution fusion | flops 6445596672 | bytes 13631488 | tf_op jit(solution)/shard_map/dot_general | solution.py:266
  165.4 3.4 collective-permute-done.1
  168.8 3.8 convert_add_fusion
  172.7 2.7 copy-done.3
  175.8 60.3 %all-gather = bf16[4,1,1536]{2,1,0:T(2,128)(2,1)S(1)} all-gather(bf16[1,1,1536]{2,1,0:T(2,128)(2,1)S(1)} %reshape.423), channel_id=1, replica_groups=mesh['groups'=2,'heads'=4,'seq'=4] {'heads'}, dimensions={0}, use_global_device_ids=true | all-gather | bytes 15360 | tf_op jit(solution)/shard_map/all_gather | solution.py:272
  236.4 3.5 multiply_reduce_fusion
  239.9 13.4 %psum.7 = f32[512]{0:T(512)S(1)} all-reduce(f32[512]{0:T(512)S(1)} %get-tuple-element.18), channel_id=1, replica_groups=mesh['groups'=2,'heads'=4,'seq'=4] {'seq'}, use_global_device_ids=true, to_apply=%region_11.12 | all-reduce | flops 512 | bytes 4096 | tf_op jit(solution)/shard_map/psum | solution.py:270
  255.6 48.8 %all-gather.9.cloned.1.call-done = bf16[2048,1536]{1,0:T(8,128)(2,1)} async-done(((bf16[512,1536]{1,0:T(8,128)(2,1)}), bf16[2048,1536]{1,0:T(8,128)(2,1)}) %all-gather.9.cloned.1.call-update) | async-done | bytes 6291472 | tf_op jit(solution)/shard_map/all_gather | solution.py:279
  304.4 5.7 %convolution_convert_fusion.2 = bf16[2048,256]{1,0:T(8,128)(2,1)} fusion(bf16[2048,1536]{1,0:T(8,128)(2,1)} %all-gather.9.cloned.1.call-done, bf16[4,1536,256]{2,1,0:T(8,128)(2,1)} %param.17, s32[]{:T(128)S(6)} %select_n.102), kind=kOutput, calls=%fused_computation.37 | convolution fusion | flops 1611137024 | bytes 8126468 | tf_op jit(solution)/shard_map/dot_general | solution.py:283
  310.2 11.1 %convolution_convert_fusion.1 = bf16[2048,1024]{1,0:T(8,128)(2,1)} fusion(bf16[2048,1536]{1,0:T(8,128)(2,1)} %all-gather.9.cloned.1.call-done, bf16[1536,1024]{1,0:T(8,128)(2,1)S(1)} %copy-done.13), kind=kOutput, calls=%fused_computation.30 | convolution fusion | flops 6444548096 | bytes 13631488 | tf_op jit(solution)/shard_map/dot_general | solution.py:282
  321.4 3.3 collective-permute-start.3
  325.9 42.9 %collective-permute-done.3 = bf16[512,1536]{1,0:T(8,128)(2,1)S(1)} collective-permute-done((bf16[512,1536]{1,0:T(8,128)(2,1)}, bf16[512,1536]{1,0:T(8,128)(2,1)S(1)}, u32[]{:S(2)}, u32[]{:S(2)}) %collective-permute-start.3) | collective-permute-done | bytes 1572896 | tf_op jit(solution)/shard_map/ppermute | solution.py:269
  368.8 3.4 reduce-scatter.3.cloned.1.call-done
  376.4 116.1 %reduce-scatter.5.cloned.1.call-done = bf16[512,1024]{1,0:T(8,128)(2,1)} async-done(((bf16[2048,1024]{1,0:T(8,128)(2,1)}), bf16[512,1024]{1,0:T(8,128)(2,1)}) %reduce-scatter.5.cloned.1.call-update) | async-done | bytes 1048592 | tf_op jit(solution)/shard_map/reduce_scatter | solution.py:284
  492.5 2.9 fusion
  514.1 5.6 %fusion.14 = f32[8,512,128]{1,2,0:T(8,128)S(1)} fusion(f32[512,512,8]{1,0,2:T(8,128)} %copy-done.2, f32[8,512]{1,0:T(8,128)S(1)} %get-tuple-element.16, pred[512,512]{0,1:T(8,128)(4,1)S(1)} %get-tuple-element.39, bf16[512,256]{1,0:T(8,128)(2,1)} %collective-permute-done.5), kind=kOutput, calls=%fused_computation.23 | convolution fusion | flops 547356672 | bytes 10895360 | tf_op jit(solution)/shard_map/hts,sd->htd/dot_general | solution.py:245
  519.7 3.8 fusion.28
  (122 shorter events, 74.7 us)
Async XLA Ops:
  7.2 143.1 %copy-start = (bf16[1024,1536]{1,0:T(8,128)(2,1)S(1)}, bf16[1024,1536]{1,0:T(8,128)(2,1)}, u32[]{:S(2)}) copy-start(bf16[1024,1536]{1,0:T(8,128)(2,1)} %param.14) | copy-start | bytes 9437188
  7.2 52.6 %all-gather.5.cloned.1.call-start = ((), (), s32[]{:S(2)}) async-start(), calls=%async_computation.2 | async-start | bytes 1474560 | tf_op jit(solution)/shard_map/all_gather | solution.py:187
  19.8 12.4 %copy-start.8 = (f32[512,8]{0,1:T(8,128)S(1)}, f32[512,8]{0,1:T(8,128)}, u32[]{:S(2)}) copy-start(f32[512,8]{0,1:T(8,128)} %param.12) | copy-start | bytes 49156
  29.2 121.0 %all-gather.7.cloned.1.call-start = ((), (), s32[]{:S(2)}) async-start(), calls=%async_computation.3 | async-start | bytes 5242880 | tf_op jit(solution)/shard_map/all_gather | solution.py:265
  70.9 233.5 %all-gather.9.cloned.1.call-start = ((), (), s32[]{:S(2)}) async-start(), calls=%async_computation.4 | async-start | bytes 7864320 | tf_op jit(solution)/shard_map/all_gather | solution.py:279
  159.6 2.7 copy-start.5
  162.5 6.3 %collective-permute-start.1 = (bf16[2,512,1536]{2,1,0:T(8,128)(2,1)S(1)}, bf16[2,512,1536]{2,1,0:T(8,128)(2,1)}, u32[]{:S(2)}, u32[]{:S(2)}) collective-permute-start(bf16[2,512,1536]{2,1,0:T(8,128)(2,1)S(1)} %dynamic-slice_bitcast_fusion), channel_id=1, source_target_pairs={{0,4},{4,0},{8,12},{12,8},{1,5},{5,1},{9,13},{13,9},{2,6},{6,2},{1... | collective-permute-start | bytes 9437192 | tf_op jit(solution)/shard_map/ppermute | solution.py:219
  163.4 73.0 %collective-permute-start = (bf16[512,1536]{1,0:T(8,128)(2,1)}, bf16[512,1536]{1,0:T(8,128)(2,1)}, u32[]{:S(2)}, u32[]{:S(2)}) collective-permute-start(bf16[512,1536]{1,0:T(8,128)(2,1)} %param.13), channel_id=1, source_target_pairs={{0,0},{1,4},{2,8},{3,12},{4,1},{5,5},{6,9},{7,13},{8,2},{9,6},{10,... | collective-permute-start | bytes 4718600 | tf_op jit(solution)/shard_map/ppermute | solution.py:262
  165.4 10.4 %copy-start.12 = (bf16[1536]{0:T(1024)(128)(2,1)S(1)}, bf16[1536]{0:T(1024)(128)(2,1)}, u32[]{:S(2)}) copy-start(bf16[1536]{0:T(1024)(128)(2,1)} %param.15) | copy-start | bytes 9220
  172.6 2.7 copy-start.3
  175.5 60.9 %collective-permute-start.2 = (bf16[512,1536]{1,0:T(8,128)(2,1)S(1)}, bf16[512,1536]{1,0:T(8,128)(2,1)}, u32[]{:S(2)}, u32[]{:S(2)}) collective-permute-start(bf16[512,1536]{1,0:T(8,128)(2,1)S(1)} %fusion.34), channel_id=1, source_target_pairs={{0,8},{4,12},{8,0},{12,4},{1,9},{5,13},{9,1},{13,5},{2,10},{6,14},... | collective-permute-start | bytes 4718600 | tf_op jit(solution)/shard_map/ppermute | solution.py:223
  255.5 116.7 %reduce-scatter.3.cloned.1.call-start = ((), (), s32[]{:S(2)}) async-start(), calls=%async_computation.5 | async-start | bytes 1310720 | tf_op jit(solution)/shard_map/reduce_scatter | solution.py:287
  255.6 54.6 %copy-start.13 = (bf16[1536,1024]{1,0:T(8,128)(2,1)S(1)}, bf16[1536,1024]{1,0:T(8,128)(2,1)}, u32[]{:S(2)}) copy-start(bf16[1536,1024]{1,0:T(8,128)(2,1)} %param.16) | copy-start | bytes 9437188
  310.2 182.3 %reduce-scatter.5.cloned.1.call-start = ((), (), s32[]{:S(2)}) async-start(), calls=%async_computation.6 | async-start | bytes 5242880 | tf_op jit(solution)/shard_map/reduce_scatter | solution.py:284
  321.4 47.4 %collective-permute-start.3 = (bf16[512,1536]{1,0:T(8,128)(2,1)}, bf16[512,1536]{1,0:T(8,128)(2,1)S(1)}, u32[]{:S(2)}, u32[]{:S(2)}) collective-permute-start(bf16[512,1536]{1,0:T(8,128)(2,1)} %get-tuple-element.25), channel_id=1, source_target_pairs={{0,0},{1,4},{2,8},{3,12},{4,1},{5,5},{6,9},{7,13},{8,2},{9,6},{10,... | collective-permute-start | bytes 4718600 | tf_op jit(solution)/shard_map/ppermute | solution.py:269
  368.8 126.6 %copy-start.7 = (bf16[512,1536]{1,0:T(8,128)(2,1)}, bf16[512,1536]{1,0:T(8,128)(2,1)S(1)}, u32[]{:S(2)}) copy-start(bf16[512,1536]{1,0:T(8,128)(2,1)S(1)} %collective-permute-done.3) | copy-start | bytes 4718596
  372.3 123.2 %collective-permute-start.4 = (bf16[512,256]{1,0:T(8,128)(2,1)}, bf16[512,256]{1,0:T(8,128)(2,1)S(1)}, u32[]{:S(2)}, u32[]{:S(2)}) collective-permute-start(bf16[512,256]{1,0:T(8,128)(2,1)} %reduce-scatter.3.cloned.1.call-done), channel_id=1, source_target_pairs={{0,1},{1,2},{2,3},{4,5},{5,6},{6,7},{8,9},{9,10},{10,11},{12,13},{... | collective-permute-start | bytes 786440 | tf_op jit(solution)/shard_map/ppermute | solution.py:16
  374.2 122.9 %collective-permute-start.6 = (bf16[512,256]{1,0:T(8,128)(2,1)}, bf16[512,256]{1,0:T(8,128)(2,1)S(1)}, u32[]{:S(2)}, u32[]{:S(2)}) collective-permute-start(bf16[512,256]{1,0:T(8,128)(2,1)} %reduce-scatter.3.cloned.1.call-done), channel_id=1, source_target_pairs={{0,3},{4,7},{8,11},{12,15},{16,19},{20,23},{24,27},{28,31}} | collective-permute-start | bytes 786440 | tf_op jit(solution)/shard_map/ppermute | solution.py:16
  374.9 123.9 %collective-permute-start.5 = (bf16[512,256]{1,0:T(8,128)(2,1)}, bf16[512,256]{1,0:T(8,128)(2,1)}, u32[]{:S(2)}, u32[]{:S(2)}) collective-permute-start(bf16[512,256]{1,0:T(8,128)(2,1)} %reduce-scatter.3.cloned.1.call-done), channel_id=1, source_target_pairs={{0,2},{1,3},{4,6},{5,7},{8,10},{9,11},{12,14},{13,15},{16,18},{17,... | collective-permute-start | bytes 786440 | tf_op jit(solution)/shard_map/ppermute | solution.py:16
  492.5 3.0 copy-start.4
  501.3 4.4 copy-start.2
  507.7 2.1 copy-start.9
  514.1 5.6 %copy-start.11 = (bf16[512,256]{1,0:T(8,128)(2,1)S(1)}, bf16[512,256]{1,0:T(8,128)(2,1)}, u32[]{:S(2)}) copy-start(bf16[512,256]{1,0:T(8,128)(2,1)} %copy-done.10) | copy-start | bytes 786436
  519.7 8.7 %copy-start.1 = (bf16[1024,1536]{1,0:T(8,128)(2,1)S(1)}, bf16[1024,1536]{1,0:T(8,128)(2,1)}, u32[]{:S(2)}) copy-start(bf16[1024,1536]{1,0:T(8,128)(2,1)} %param.14) | copy-start | bytes 9437188
  (2 other events, 2.4 us)
Sparse Core Ops, SparseCore 0:
  29.4 30.4 all-gather.4
  71.0 79.2 all-gather.6
  255.6 48.7 all-gather.8
  310.3 61.9 reduce-scatter.2
  374.4 118.0 reduce-scatter.4

commit v6 on v5

--- a/solution.py
+++ b/solution.py
@@ -184,7 +184,8 @@
     pad_rows = 16
     total_rows = jnp.broadcast_to(decay_total[:, None, None], (heads_here, pad_rows, DH))
     packed = jnp.concatenate([state, total_rows], axis=1).astype(jnp.bfloat16)
-    gathered = lax.all_gather(packed[None], "seq", axis=0, tiled=True).astype(jnp.float32)
+    gathered = lax.all_gather(packed[None], "seq", axis=0, tiled=True)
+    gathered = gathered.astype(jnp.float32)
     states = gathered[:, :, :DH, :]
     totals = gathered[:, :, DH, 0]
     position = lax.axis_index("seq")
@@ -248,7 +249,11 @@
     return (new_max, row_total, weighted)
 
 
-def shards_fast(
+def shards_fast(*args):
+    return shards_fast_body(*args)
+
+
+def shards_fast_body(
     lin_query, lin_key, lin_value, log_decay, stream, out_weight, norm_gain, query_weight, kv_weight
 ):
     n_heads = lax.axis_size("heads")
@@ -259,18 +264,26 @@
     mine_a = lax.axis_index("heads")
     mine_b = lax.axis_index("seq")
     swap = [(x * n_seq + y, y * n_seq + x) for x in range(n_heads) for y in range(n_seq)]
-    stream_t = lax.ppermute(stream, ("heads", "seq"), swap)
+    gain_rows = jnp.broadcast_to(norm_gain[None, :], (16, norm_gain.shape[0]))
+    packed = lax.ppermute(
+        jnp.concatenate([stream, gain_rows], axis=0), ("heads", "seq"), swap
+    )
+    stream_t = packed[:tok_rows]
+    gain_b = packed[tok_rows]
 
     lin_out = lightning_local(lin_query, lin_key, lin_value, log_decay)
-    lin_all = lax.all_gather(lin_out, "seq", axis=0, tiled=True)
-    part = jnp.dot(lin_all, out_weight, preferred_element_type=jnp.float32).astype(jnp.bfloat16)
-    own_sum = heads_reduce_scatter(part, n_heads)
+    halves = []
+    half_rows = tok_rows // 2
+    for half in range(2):
+        lin_all = lax.all_gather(
+            lin_out[half * half_rows : (half + 1) * half_rows], "seq", axis=0, tiled=True
+        )
+        part = jnp.dot(lin_all, out_weight, preferred_element_type=jnp.float32)
+        halves.append(heads_reduce_scatter(part.astype(jnp.bfloat16), n_heads))
+    own_sum = jnp.concatenate(halves, axis=0)
     mixed_sum = stream_t.astype(jnp.float32) + own_sum
     stream_next = lax.ppermute(mixed_sum.astype(jnp.bfloat16), ("heads", "seq"), swap)
     total_sq = lax.psum(jnp.sum(mixed_sum * mixed_sum, axis=1), "seq")
-    cols = mixed_sum.shape[1]
-    gain_all = lax.all_gather(norm_gain, "heads", axis=0, tiled=True)
-    gain_b = lax.dynamic_slice_in_dim(gain_all, mine_b * cols, cols)
     normed = (
         mixed_sum
         * lax.rsqrt(total_sq / D + 1e-05)[:, None]

time: 540 us -> 546 us (1.011)
  blocking collectives: 73.8 us -> 16 us
  waiting for transfers between devices: 301 us -> 350 us
  local copies, waits for them, and re-layouts: 34.5 us -> 40.8 us
    all_gather x1 -> x0, blocking collectives: 60.3 us -> none  [shards_fast(): gain_all = lax.all_gather(norm_gain, 'heads', axis=0, tiled=True)]
    ppermute x2, waiting for transfers between devices: 42.9 us -> 69.5 us  [the longest x1 41.1 us: shards_fast_body(): lax.ppermute(mixed_sum.astype(jnp.bfloat16), ('heads', 'seq'), swap)]
    ppermute x1 -> x2, waiting for transfers between devices: 0.01 us -> 22.3 us  [heads_reduce_scatter(): lax.ppermute(send2.astype(jnp.bfloat16), 'heads', [(i, i ^ 2) for i in ra...]
    all_gather x3 -> x4, waiting for transfers between devices: 135 us -> 138 us  [the longest x2 79.6 us: shards_fast_body(): lax.all_gather(lin_out[half * half_rows:(half + 1) * half_rows], 'seq', a...]
    dot_general x3 -> x4, matrix products: 26.2 us -> 27.6 us  [the longest x1 11.1 us: shards_fast_body(): jnp.dot(normed_all, query_weight, preferred_element_type=jnp.float32)]
    unnamed x38 -> x46, local copies, waits for them, and re-layouts: 23.4 us -> 22.5 us
  transfers between devices with their start and end apart: 12 -> 15, of which waited for: 7 -> 9; matrix products, arithmetic and copies ran while one was open for 9% -> 12% of each run, Pallas kernels for 0% -> 0%
where the time goes in v6:
time: 546 us; the launch traced here: 541 us
  waiting for transfers between devices  350 us (64%)
  matrix products  72.9 us (13%)
  local copies, waits for them, and re-layouts  40.8 us (7%)
  other arithmetic  32.7 us (6%)
  blocking collectives  16 us (3%)
  between operations  15 us (3%)
  starting transfers between devices  14.2 us (3%)
    reduce_scatter x1, waiting for transfers between devices, shards_fast_body(): lax.psum_scatter(q_part.astype(jnp.bfloat16), 'seq', scatter_dimension=0,...  116 us
    all_gather x2, waiting for transfers between devices, shards_fast_body(): lax.all_gather(lin_out[half * half_rows:(half + 1) * half_rows], 'seq', a...  79.6 us
    all_gather x1, waiting for transfers between devices, shards_fast_body(): normed_all = lax.all_gather(normed, 'heads', axis=0, tiled=True)  51.8 us
    ppermute x1, waiting for transfers between devices, shards_fast_body(): lax.ppermute(mixed_sum.astype(jnp.bfloat16), ('heads', 'seq'), swap)  41.1 us
    ppermute x1, waiting for transfers between devices, shards_fast_body(): lax.ppermute(jnp.concatenate([stream, gain_rows], axis=0), ('heads', 'seq...  28.5 us
    unnamed x46, local copies, waits for them, and re-layouts  22.5 us
    ppermute x2, waiting for transfers between devices, heads_reduce_scatter(): lax.ppermute(send2.astype(jnp.bfloat16), 'heads', [(i, i ^ 2) for i in ra...  22.3 us
    psum x1, blocking collectives, shards_fast_body(): total_sq = lax.psum(jnp.sum(mixed_sum * mixed_sum, axis=1), 'seq')  16 us
  transfers between devices with their start and end apart: 15, of which 9 were waited for; matrix products, arithmetic and copies ran while one was open for 12% of the time, Pallas kernels for 0%

profile of v6, /device:TPU:21, one launch (start us, length us, event | category | flops | bytes accessed | tf_op | source)
XLA Modules:
  0.0 541.1 jit_solution(9941081780722759265)
XLA Ops:
  37.7 3.4 fusion.34
  41.0 4.3 fusion.38
  45.4 3.3 fusion.36
  48.7 4.5 fusion.37
  53.2 6.6 %all-gather.5.cloned.1.call-done = bf16[4,8,144,128]{3,2,1,0:T(8,128)(2,1)} async-done(((bf16[1,8,144,128]{3,2,1,0:T(8,128)(2,1)}), bf16[4,8,144,128]{3,2,1,0:T(8,128)(2,1)}) %all-gather.5.cloned.1.call-update) | async-done | bytes 1179664 | tf_op jit(solution)/shard_map/all_gather | solution.py:187
  62.6 4.5 multiply_reduce_fusion.2
  73.3 42.2 %all-gather.7.cloned.1.call-done = bf16[1024,1024]{0,1:T(8,128)(2,1)} async-done(((bf16[256,1024]{0,1:T(8,128)(2,1)}), bf16[1024,1024]{0,1:T(8,128)(2,1)}) %all-gather.7.cloned.1.call-update) | async-done | bytes 2097168 | tf_op jit(solution)/shard_map/all_gather | solution.py:278
  115.5 5.4 convolution_convert_fusion.2
  124.8 37.4 %all-gather.9.cloned.1.call-done = bf16[1024,1024]{0,1:T(8,128)(2,1)} async-done(((bf16[256,1024]{0,1:T(8,128)(2,1)}), bf16[1024,1024]{0,1:T(8,128)(2,1)}) %all-gather.9.cloned.1.call-update) | async-done | bytes 2097168 | tf_op jit(solution)/shard_map/all_gather | solution.py:278
  162.2 5.4 convolution_convert_fusion.1
  183.2 28.5 %collective-permute-done = bf16[528,1536]{1,0:T(8,128)(2,1)} collective-permute-done((bf16[528,1536]{1,0:T(8,128)(2,1)}, bf16[528,1536]{1,0:T(8,128)(2,1)}, u32[]{:S(2)}, u32[]{:S(2)}) %collective-permute-start) | collective-permute-done | bytes 1622048 | tf_op jit(solution)/shard_map/ppermute | solution.py:268
  214.3 22.3 %collective-permute-done.4 = bf16[256,1536]{1,0:T(8,128)(2,1)} collective-permute-done((bf16[256,1536]{1,0:T(8,128)(2,1)}, bf16[256,1536]{1,0:T(8,128)(2,1)}, u32[]{:S(2)}, u32[]{:S(2)}) %collective-permute-start.4) | collective-permute-done | bytes 786464 | tf_op jit(solution)/shard_map/ppermute | solution.py:224
  239.8 16.0 %psum.7 = f32[512]{0:T(512)S(1)} all-reduce(f32[512]{0:T(512)S(1)} %multiply_reduce_fusion), channel_id=1, replica_groups=mesh['groups'=2,'heads'=4,'seq'=4] {'seq'}, use_global_device_ids=true, to_apply=%region_11.12 | all-reduce | flops 512 | bytes 4096 | tf_op jit(solution)/shard_map/psum | solution.py:286
  255.8 3.6 multiply_convert_fusion
  259.5 51.8 %all-gather.11.cloned.1.call-done = bf16[2048,1536]{1,0:T(8,128)(2,1)} async-done(((bf16[512,1536]{1,0:T(8,128)(2,1)}), bf16[2048,1536]{1,0:T(8,128)(2,1)}) %all-gather.11.cloned.1.call-update) | async-done | bytes 6291472 | tf_op jit(solution)/shard_map/all_gather | solution.py:292
  311.3 5.7 %convolution_convert_fusion.3 = bf16[2048,256]{1,0:T(8,128)(2,1)} fusion(bf16[2048,1536]{1,0:T(8,128)(2,1)} %all-gather.11.cloned.1.call-done, bf16[4,1536,256]{2,1,0:T(8,128)(2,1)} %param.17, s32[]{:T(128)S(6)} %select_n.105), kind=kOutput, calls=%fused_computation.36 | convolution fusion | flops 1611137024 | bytes 8126468 | tf_op jit(solution)/shard_map/dot_general | solution.py:296
  317.1 11.1 %convolution_convert_fusion = bf16[2048,1024]{1,0:T(8,128)(2,1)} fusion(bf16[2048,1536]{1,0:T(8,128)(2,1)} %all-gather.11.cloned.1.call-done, bf16[1536,1024]{1,0:T(8,128)(2,1)S(1)} %copy-done.18), kind=kOutput, calls=%fused_computation.28 | convolution fusion | flops 6444548096 | bytes 13631488 | tf_op jit(solution)/shard_map/dot_general | solution.py:295
  329.7 3.5 collective-permute-start.5
  334.4 41.1 %collective-permute-done.5 = bf16[512,1536]{1,0:T(8,128)(2,1)} collective-permute-done((bf16[512,1536]{1,0:T(8,128)(2,1)S(1)}, bf16[512,1536]{1,0:T(8,128)(2,1)}, u32[]{:S(2)}, u32[]{:S(2)}) %collective-permute-start.5) | collective-permute-done | bytes 1572896 | tf_op jit(solution)/shard_map/ppermute | solution.py:285
  375.4 3.2 reduce-scatter.3.cloned.1.call-done
  382.5 116.3 %reduce-scatter.5.cloned.1.call-done = bf16[512,1024]{1,0:T(8,128)(2,1)} async-done(((bf16[2048,1024]{1,0:T(8,128)(2,1)}), bf16[512,1024]{1,0:T(8,128)(2,1)}) %reduce-scatter.5.cloned.1.call-update) | async-done | bytes 1048592 | tf_op jit(solution)/shard_map/reduce_scatter | solution.py:297
  498.9 2.9 fusion
  519.6 5.6 %fusion.14 = f32[8,512,128]{1,2,0:T(8,128)S(1)} fusion(f32[512,512,8]{1,0,2:T(8,128)} %copy-done.2, f32[8,512]{1,0:T(8,128)S(1)} %get-tuple-element.16, pred[512,512]{0,1:T(8,128)(4,1)S(1)} %get-tuple-element.39, bf16[512,256]{1,0:T(8,128)(2,1)S(1)} %collective-permute-done.7), kind=kOutput, calls=%fused_computation.21 | convolution fusion | flops 547356672 | bytes 10895360 | tf_op jit(solution)/shard_map/hts,sd->htd/dot_general | solution.py:246
  525.2 3.8 fusion.27
  (145 shorter events, 93.7 us)
Async XLA Ops:
  7.2 108.4 %copy-start = (bf16[1024,1536]{1,0:T(8,128)(2,1)S(1)}, bf16[1024,1536]{1,0:T(8,128)(2,1)}, u32[]{:S(2)}) copy-start(bf16[1024,1536]{1,0:T(8,128)(2,1)} %param.14) | copy-start | bytes 9437188
  7.2 52.6 %all-gather.5.cloned.1.call-start = ((), (), s32[]{:S(2)}) async-start(), calls=%async_computation.2 | async-start | bytes 1474560 | tf_op jit(solution)/shard_map/all_gather | solution.py:187
  23.9 8.2 %copy-start.13 = (f32[512,8]{0,1:T(8,128)S(1)}, f32[512,8]{0,1:T(8,128)}, u32[]{:S(2)}) copy-start(f32[512,8]{0,1:T(8,128)} %param.12) | copy-start | bytes 49156
  29.2 86.3 %all-gather.7.cloned.1.call-start = ((), (), s32[]{:S(2)}) async-start(), calls=%async_computation.3 | async-start | bytes 2621440 | tf_op jit(solution)/shard_map/all_gather | solution.py:278
  71.0 91.2 %all-gather.9.cloned.1.call-start = ((), (), s32[]{:S(2)}) async-start(), calls=%async_computation.4 | async-start | bytes 2621440 | tf_op jit(solution)/shard_map/all_gather | solution.py:278
  73.1 238.3 %all-gather.11.cloned.1.call-start = ((), (), s32[]{:S(2)}) async-start(), calls=%async_computation.5 | async-start | bytes 7864320 | tf_op jit(solution)/shard_map/all_gather | solution.py:292
  123.9 50.4 %collective-permute-start.1 = (bf16[2,256,1536]{2,1,0:T(8,128)(2,1)}, bf16[2,256,1536]{2,1,0:T(8,128)(2,1)}, u32[]{:S(2)}, u32[]{:S(2)}) collective-permute-start(bf16[2,256,1536]{2,1,0:T(8,128)(2,1)} %dynamic-slice_bitcast_fusion.1), channel_id=1, source_target_pairs={{0,4},{4,0},{8,12},{12,8},{1,5},{5,1},{9,13},{13,9},{2,6},{6,2},{1... | collective-permute-start | bytes 4718600 | tf_op jit(solution)/shard_map/ppermute | solution.py:220
  167.5 4.0 copy-start.8
  168.8 9.8 %collective-permute-start.3 = (bf16[2,256,1536]{2,1,0:T(8,128)(2,1)}, bf16[2,256,1536]{2,1,0:T(8,128)(2,1)}, u32[]{:S(2)}, u32[]{:S(2)}) collective-permute-start(bf16[2,256,1536]{2,1,0:T(8,128)(2,1)} %dynamic-slice_bitcast_fusion), channel_id=1, source_target_pairs={{0,4},{4,0},{8,12},{12,8},{1,5},{5,1},{9,13},{13,9},{2,6},{6,2},{1... | collective-permute-start | bytes 4718600 | tf_op jit(solution)/shard_map/ppermute | solution.py:220
  171.5 40.2 %collective-permute-start = (bf16[528,1536]{1,0:T(8,128)(2,1)}, bf16[528,1536]{1,0:T(8,128)(2,1)}, u32[]{:S(2)}, u32[]{:S(2)}) collective-permute-start(bf16[528,1536]{1,0:T(8,128)(2,1)} %pad_maximum_fusion), channel_id=1, source_target_pairs={{0,0},{1,4},{2,8},{3,12},{4,1},{5,5},{6,9},{7,13},{8,2},{9,6},{10,... | collective-permute-start | bytes 4866056 | tf_op jit(solution)/shard_map/ppermute | solution.py:268
  174.4 4.2 copy-start.9
  178.0 34.5 %collective-permute-start.2 = (bf16[256,1536]{1,0:T(8,128)(2,1)}, bf16[256,1536]{1,0:T(8,128)(2,1)}, u32[]{:S(2)}, u32[]{:S(2)}) collective-permute-start(bf16[256,1536]{1,0:T(8,128)(2,1)} %fusion.66), channel_id=1, source_target_pairs={{0,8},{4,12},{8,0},{12,4},{1,9},{5,13},{9,1},{13,5},{2,10},{6,14},... | collective-permute-start | bytes 2359304 | tf_op jit(solution)/shard_map/ppermute | solution.py:224
  182.3 54.2 %collective-permute-start.4 = (bf16[256,1536]{1,0:T(8,128)(2,1)}, bf16[256,1536]{1,0:T(8,128)(2,1)}, u32[]{:S(2)}, u32[]{:S(2)}) collective-permute-start(bf16[256,1536]{1,0:T(8,128)(2,1)} %fusion.67), channel_id=1, source_target_pairs={{0,8},{4,12},{8,0},{12,4},{1,9},{5,13},{9,1},{13,5},{2,10},{6,14},... | collective-permute-start | bytes 2359304 | tf_op jit(solution)/shard_map/ppermute | solution.py:224
  183.2 53.4 %copy-start.6 = (f32[2,256,1536]{2,1,0:T(8,128)S(1)}, f32[2,256,1536]{2,1,0:T(8,128)}, u32[]{:S(2)}) copy-start(f32[2,256,1536]{2,1,0:T(8,128)} %copy-done.5) | copy-start | bytes 9437188
  259.5 119.2 %reduce-scatter.3.cloned.1.call-start = ((), (), s32[]{:S(2)}) async-start(), calls=%async_computation.6 | async-start | bytes 1310720 | tf_op jit(solution)/shard_map/reduce_scatter | solution.py:300
  259.5 57.6 %copy-start.18 = (bf16[1536,1024]{1,0:T(8,128)(2,1)S(1)}, bf16[1536,1024]{1,0:T(8,128)(2,1)}, u32[]{:S(2)}) copy-start(bf16[1536,1024]{1,0:T(8,128)(2,1)} %param.16) | copy-start | bytes 9437188
  317.1 181.8 %reduce-scatter.5.cloned.1.call-start = ((), (), s32[]{:S(2)}) async-start(), calls=%async_computation.7 | async-start | bytes 5242880 | tf_op jit(solution)/shard_map/reduce_scatter | solution.py:297
  329.7 45.7 %collective-permute-start.5 = (bf16[512,1536]{1,0:T(8,128)(2,1)S(1)}, bf16[512,1536]{1,0:T(8,128)(2,1)}, u32[]{:S(2)}, u32[]{:S(2)}) collective-permute-start(bf16[512,1536]{1,0:T(8,128)(2,1)S(1)} %copy-done.11), channel_id=1, source_target_pairs={{0,0},{1,4},{2,8},{3,12},{4,1},{5,5},{6,9},{7,13},{8,2},{9,6},{10,... | collective-permute-start | bytes 4718600 | tf_op jit(solution)/shard_map/ppermute | solution.py:285
  378.6 123.2 %collective-permute-start.6 = (bf16[512,256]{1,0:T(8,128)(2,1)}, bf16[512,256]{1,0:T(8,128)(2,1)S(1)}, u32[]{:S(2)}, u32[]{:S(2)}) collective-permute-start(bf16[512,256]{1,0:T(8,128)(2,1)} %reduce-scatter.3.cloned.1.call-done), channel_id=1, source_target_pairs={{0,1},{1,2},{2,3},{4,5},{5,6},{6,7},{8,9},{9,10},{10,11},{12,13},{... | collective-permute-start | bytes 786440 | tf_op jit(solution)/shard_map/ppermute | solution.py:16
  380.6 122.9 %collective-permute-start.8 = (bf16[512,256]{1,0:T(8,128)(2,1)}, bf16[512,256]{1,0:T(8,128)(2,1)S(1)}, u32[]{:S(2)}, u32[]{:S(2)}) collective-permute-start(bf16[512,256]{1,0:T(8,128)(2,1)} %reduce-scatter.3.cloned.1.call-done), channel_id=1, source_target_pairs={{0,3},{4,7},{8,11},{12,15},{16,19},{20,23},{24,27},{28,31}} | collective-permute-start | bytes 786440 | tf_op jit(solution)/shard_map/ppermute | solution.py:16
  381.2 123.9 %collective-permute-start.7 = (bf16[512,256]{1,0:T(8,128)(2,1)}, bf16[512,256]{1,0:T(8,128)(2,1)S(1)}, u32[]{:S(2)}, u32[]{:S(2)}) collective-permute-start(bf16[512,256]{1,0:T(8,128)(2,1)} %reduce-scatter.3.cloned.1.call-done), channel_id=1, source_target_pairs={{0,2},{1,3},{4,6},{5,7},{8,10},{9,11},{12,14},{13,15},{16,18},{17,... | collective-permute-start | bytes 786440 | tf_op jit(solution)/shard_map/ppermute | solution.py:16
  506.8 4.4 copy-start.2
  519.6 5.6 %copy-start.16 = (bf16[512,256]{1,0:T(8,128)(2,1)S(1)}, bf16[512,256]{1,0:T(8,128)(2,1)}, u32[]{:S(2)}) copy-start(bf16[512,256]{1,0:T(8,128)(2,1)} %copy-done.15) | copy-start | bytes 786436
  525.2 8.7 %copy-start.1 = (bf16[1024,1536]{1,0:T(8,128)(2,1)S(1)}, bf16[1024,1536]{1,0:T(8,128)(2,1)}, u32[]{:S(2)}) copy-start(bf16[1024,1536]{1,0:T(8,128)(2,1)} %param.14) | copy-start | bytes 9437188
  (10 other events, 20.8 us)
Sparse Core Ops, SparseCore 0:
  29.4 30.4 all-gather.4
  71.1 44.4 all-gather.6
  117.7 44.4 all-gather.8
  259.6 51.7 all-gather.10
  317.2 61.4 reduce-scatter.2
  380.8 118.0 reduce-scatter.4

commit v7 on v6

--- a/solution.py
+++ b/solution.py
@@ -294,9 +294,8 @@
     kv_mine = lax.dynamic_index_in_dim(kv_weight, kv_group, 0, keepdims=False)
     q_part = jnp.dot(normed_all, query_weight, preferred_element_type=jnp.float32)
     kv_part = jnp.dot(normed_all, kv_mine, preferred_element_type=jnp.float32)
-    queries = lax.psum_scatter(
-        q_part.astype(jnp.bfloat16), "seq", scatter_dimension=0, tiled=True
-    ).reshape(tok_rows, heads_here, DH)
+    queries = lax.psum_scatter(q_part.astype(jnp.bfloat16), "seq", scatter_dimension=0, tiled=True)
+    queries = queries.reshape(tok_rows, heads_here, DH)
     kv_own = lax.psum_scatter(kv_part.astype(jnp.bfloat16), "seq", scatter_dimension=0, tiled=True)
     query_pos = mine_b * tok_rows + jnp.arange(tok_rows)
     state = (

time: 546 us -> 546 us (level)
  no operation moved by 1% of the time
where the time goes in v7:
time: 546 us; the launch traced here: 541 us
  waiting for transfers between devices  350 us (64%)
  matrix products  72.9 us (13%)
  local copies, waits for them, and re-layouts  40.8 us (7%)
  other arithmetic  32.7 us (6%)
  blocking collectives  16 us (3%)
  between operations  15 us (3%)
  starting transfers between devices  14.2 us (3%)
    reduce_scatter x1, waiting for transfers between devices, shards_fast_body(): lax.psum_scatter(q_part.astype(jnp.bfloat16), 'seq', scatter_dimension=0,...  116 us
    all_gather x2, waiting for transfers between devices, shards_fast_body(): lax.all_gather(lin_out[half * half_rows:(half + 1) * half_rows], 'seq', a...  79.6 us
    all_gather x1, waiting for transfers between devices, shards_fast_body(): normed_all = lax.all_gather(normed, 'heads', axis=0, tiled=True)  51.8 us
    ppermute x1, waiting for transfers between devices, shards_fast_body(): lax.ppermute(mixed_sum.astype(jnp.bfloat16), ('heads', 'seq'), swap)  41.1 us
    ppermute x1, waiting for transfers between devices, shards_fast_body(): lax.ppermute(jnp.concatenate([stream, gain_rows], axis=0), ('heads', 'seq...  28.5 us
    unnamed x46, local copies, waits for them, and re-layouts  22.5 us
    ppermute x2, waiting for transfers between devices, heads_reduce_scatter(): lax.ppermute(send2.astype(jnp.bfloat16), 'heads', [(i, i ^ 2) for i in ra...  22.3 us
    psum x1, blocking collectives, shards_fast_body(): total_sq = lax.psum(jnp.sum(mixed_sum * mixed_sum, axis=1), 'seq')  16 us
  transfers between devices with their start and end apart: 15, of which 9 were waited for; matrix products, arithmetic and copies ran while one was open for 12% of the time, Pallas kernels for 0%

profile of v7, /device:TPU:21, one launch (start us, length us, event | category | flops | bytes accessed | tf_op | source)
XLA Modules:
  0.0 541.1 jit_solution(9941081780722759265)
XLA Ops:
  37.7 3.4 fusion.34
  41.0 4.3 fusion.38
  45.4 3.3 fusion.36
  48.7 4.5 fusion.37
  53.2 6.6 %all-gather.5.cloned.1.call-done = bf16[4,8,144,128]{3,2,1,0:T(8,128)(2,1)} async-done(((bf16[1,8,144,128]{3,2,1,0:T(8,128)(2,1)}), bf16[4,8,144,128]{3,2,1,0:T(8,128)(2,1)}) %all-gather.5.cloned.1.call-update) | async-done | bytes 1179664 | tf_op jit(solution)/shard_map/all_gather | solution.py:187
  62.6 4.5 multiply_reduce_fusion.2
  73.3 42.2 %all-gather.7.cloned.1.call-done = bf16[1024,1024]{0,1:T(8,128)(2,1)} async-done(((bf16[256,1024]{0,1:T(8,128)(2,1)}), bf16[1024,1024]{0,1:T(8,128)(2,1)}) %all-gather.7.cloned.1.call-update) | async-done | bytes 2097168 | tf_op jit(solution)/shard_map/all_gather | solution.py:278
  115.5 5.4 convolution_convert_fusion.2
  124.8 37.4 %all-gather.9.cloned.1.call-done = bf16[1024,1024]{0,1:T(8,128)(2,1)} async-done(((bf16[256,1024]{0,1:T(8,128)(2,1)}), bf16[1024,1024]{0,1:T(8,128)(2,1)}) %all-gather.9.cloned.1.call-update) | async-done | bytes 2097168 | tf_op jit(solution)/shard_map/all_gather | solution.py:278
  162.2 5.4 convolution_convert_fusion.1
  183.2 28.5 %collective-permute-done = bf16[528,1536]{1,0:T(8,128)(2,1)} collective-permute-done((bf16[528,1536]{1,0:T(8,128)(2,1)}, bf16[528,1536]{1,0:T(8,128)(2,1)}, u32[]{:S(2)}, u32[]{:S(2)}) %collective-permute-start) | collective-permute-done | bytes 1622048 | tf_op jit(solution)/shard_map/ppermute | solution.py:268
  214.3 22.3 %collective-permute-done.4 = bf16[256,1536]{1,0:T(8,128)(2,1)} collective-permute-done((bf16[256,1536]{1,0:T(8,128)(2,1)}, bf16[256,1536]{1,0:T(8,128)(2,1)}, u32[]{:S(2)}, u32[]{:S(2)}) %collective-permute-start.4) | collective-permute-done | bytes 786464 | tf_op jit(solution)/shard_map/ppermute | solution.py:224
  239.8 16.0 %psum.7 = f32[512]{0:T(512)S(1)} all-reduce(f32[512]{0:T(512)S(1)} %multiply_reduce_fusion), channel_id=1, replica_groups=mesh['groups'=2,'heads'=4,'seq'=4] {'seq'}, use_global_device_ids=true, to_apply=%region_11.12 | all-reduce | flops 512 | bytes 4096 | tf_op jit(solution)/shard_map/psum | solution.py:286
  255.8 3.6 multiply_convert_fusion
  259.5 51.8 %all-gather.11.cloned.1.call-done = bf16[2048,1536]{1,0:T(8,128)(2,1)} async-done(((bf16[512,1536]{1,0:T(8,128)(2,1)}), bf16[2048,1536]{1,0:T(8,128)(2,1)}) %all-gather.11.cloned.1.call-update) | async-done | bytes 6291472 | tf_op jit(solution)/shard_map/all_gather | solution.py:292
  311.3 5.7 %convolution_convert_fusion.3 = bf16[2048,256]{1,0:T(8,128)(2,1)} fusion(bf16[2048,1536]{1,0:T(8,128)(2,1)} %all-gather.11.cloned.1.call-done, bf16[4,1536,256]{2,1,0:T(8,128)(2,1)} %param.17, s32[]{:T(128)S(6)} %select_n.105), kind=kOutput, calls=%fused_computation.36 | convolution fusion | flops 1611137024 | bytes 8126468 | tf_op jit(solution)/shard_map/dot_general | solution.py:296
  317.1 11.1 %convolution_convert_fusion = bf16[2048,1024]{1,0:T(8,128)(2,1)} fusion(bf16[2048,1536]{1,0:T(8,128)(2,1)} %all-gather.11.cloned.1.call-done, bf16[1536,1024]{1,0:T(8,128)(2,1)S(1)} %copy-done.18), kind=kOutput, calls=%fused_computation.28 | convolution fusion | flops 6444548096 | bytes 13631488 | tf_op jit(solution)/shard_map/dot_general | solution.py:295
  329.7 3.5 collective-permute-start.5
  334.4 41.1 %collective-permute-done.5 = bf16[512,1536]{1,0:T(8,128)(2,1)} collective-permute-done((bf16[512,1536]{1,0:T(8,128)(2,1)S(1)}, bf16[512,1536]{1,0:T(8,128)(2,1)}, u32[]{:S(2)}, u32[]{:S(2)}) %collective-permute-start.5) | collective-permute-done | bytes 1572896 | tf_op jit(solution)/shard_map/ppermute | solution.py:285
  375.4 3.2 reduce-scatter.3.cloned.1.call-done
  382.5 116.3 %reduce-scatter.5.cloned.1.call-done = bf16[512,1024]{1,0:T(8,128)(2,1)} async-done(((bf16[2048,1024]{1,0:T(8,128)(2,1)}), bf16[512,1024]{1,0:T(8,128)(2,1)}) %reduce-scatter.5.cloned.1.call-update) | async-done | bytes 1048592 | tf_op jit(solution)/shard_map/reduce_scatter | solution.py:297
  498.9 2.9 fusion
  519.6 5.6 %fusion.14 = f32[8,512,128]{1,2,0:T(8,128)S(1)} fusion(f32[512,512,8]{1,0,2:T(8,128)} %copy-done.2, f32[8,512]{1,0:T(8,128)S(1)} %get-tuple-element.16, pred[512,512]{0,1:T(8,128)(4,1)S(1)} %get-tuple-element.39, bf16[512,256]{1,0:T(8,128)(2,1)S(1)} %collective-permute-done.7), kind=kOutput, calls=%fused_computation.21 | convolution fusion | flops 547356672 | bytes 10895360 | tf_op jit(solution)/shard_map/hts,sd->htd/dot_general | solution.py:246
  525.2 3.8 fusion.27
  (145 shorter events, 93.7 us)
Async XLA Ops:
  7.2 108.4 %copy-start = (bf16[1024,1536]{1,0:T(8,128)(2,1)S(1)}, bf16[1024,1536]{1,0:T(8,128)(2,1)}, u32[]{:S(2)}) copy-start(bf16[1024,1536]{1,0:T(8,128)(2,1)} %param.14) | copy-start | bytes 9437188
  7.2 52.6 %all-gather.5.cloned.1.call-start = ((), (), s32[]{:S(2)}) async-start(), calls=%async_computation.2 | async-start | bytes 1474560 | tf_op jit(solution)/shard_map/all_gather | solution.py:187
  23.9 8.2 %copy-start.13 = (f32[512,8]{0,1:T(8,128)S(1)}, f32[512,8]{0,1:T(8,128)}, u32[]{:S(2)}) copy-start(f32[512,8]{0,1:T(8,128)} %param.12) | copy-start | bytes 49156
  29.2 86.3 %all-gather.7.cloned.1.call-start = ((), (), s32[]{:S(2)}) async-start(), calls=%async_computation.3 | async-start | bytes 2621440 | tf_op jit(solution)/shard_map/all_gather | solution.py:278
  71.0 91.2 %all-gather.9.cloned.1.call-start = ((), (), s32[]{:S(2)}) async-start(), calls=%async_computation.4 | async-start | bytes 2621440 | tf_op jit(solution)/shard_map/all_gather | solution.py:278
  73.1 238.3 %all-gather.11.cloned.1.call-start = ((), (), s32[]{:S(2)}) async-start(), calls=%async_computation.5 | async-start | bytes 7864320 | tf_op jit(solution)/shard_map/all_gather | solution.py:292
  123.9 50.4 %collective-permute-start.1 = (bf16[2,256,1536]{2,1,0:T(8,128)(2,1)}, bf16[2,256,1536]{2,1,0:T(8,128)(2,1)}, u32[]{:S(2)}, u32[]{:S(2)}) collective-permute-start(bf16[2,256,1536]{2,1,0:T(8,128)(2,1)} %dynamic-slice_bitcast_fusion.1), channel_id=1, source_target_pairs={{0,4},{4,0},{8,12},{12,8},{1,5},{5,1},{9,13},{13,9},{2,6},{6,2},{1... | collective-permute-start | bytes 4718600 | tf_op jit(solution)/shard_map/ppermute | solution.py:220
  167.5 4.0 copy-start.8
  168.8 9.8 %collective-permute-start.3 = (bf16[2,256,1536]{2,1,0:T(8,128)(2,1)}, bf16[2,256,1536]{2,1,0:T(8,128)(2,1)}, u32[]{:S(2)}, u32[]{:S(2)}) collective-permute-start(bf16[2,256,1536]{2,1,0:T(8,128)(2,1)} %dynamic-slice_bitcast_fusion), channel_id=1, source_target_pairs={{0,4},{4,0},{8,12},{12,8},{1,5},{5,1},{9,13},{13,9},{2,6},{6,2},{1... | collective-permute-start | bytes 4718600 | tf_op jit(solution)/shard_map/ppermute | solution.py:220
  171.5 40.2 %collective-permute-start = (bf16[528,1536]{1,0:T(8,128)(2,1)}, bf16[528,1536]{1,0:T(8,128)(2,1)}, u32[]{:S(2)}, u32[]{:S(2)}) collective-permute-start(bf16[528,1536]{1,0:T(8,128)(2,1)} %pad_maximum_fusion), channel_id=1, source_target_pairs={{0,0},{1,4},{2,8},{3,12},{4,1},{5,5},{6,9},{7,13},{8,2},{9,6},{10,... | collective-permute-start | bytes 4866056 | tf_op jit(solution)/shard_map/ppermute | solution.py:268
  174.4 4.2 copy-start.9
  178.0 34.5 %collective-permute-start.2 = (bf16[256,1536]{1,0:T(8,128)(2,1)}, bf16[256,1536]{1,0:T(8,128)(2,1)}, u32[]{:S(2)}, u32[]{:S(2)}) collective-permute-start(bf16[256,1536]{1,0:T(8,128)(2,1)} %fusion.66), channel_id=1, source_target_pairs={{0,8},{4,12},{8,0},{12,4},{1,9},{5,13},{9,1},{13,5},{2,10},{6,14},... | collective-permute-start | bytes 2359304 | tf_op jit(solution)/shard_map/ppermute | solution.py:224
  182.3 54.2 %collective-permute-start.4 = (bf16[256,1536]{1,0:T(8,128)(2,1)}, bf16[256,1536]{1,0:T(8,128)(2,1)}, u32[]{:S(2)}, u32[]{:S(2)}) collective-permute-start(bf16[256,1536]{1,0:T(8,128)(2,1)} %fusion.67), channel_id=1, source_target_pairs={{0,8},{4,12},{8,0},{12,4},{1,9},{5,13},{9,1},{13,5},{2,10},{6,14},... | collective-permute-start | bytes 2359304 | tf_op jit(solution)/shard_map/ppermute | solution.py:224
  183.2 53.4 %copy-start.6 = (f32[2,256,1536]{2,1,0:T(8,128)S(1)}, f32[2,256,1536]{2,1,0:T(8,128)}, u32[]{:S(2)}) copy-start(f32[2,256,1536]{2,1,0:T(8,128)} %copy-done.5) | copy-start | bytes 9437188
  259.5 119.2 %reduce-scatter.3.cloned.1.call-start = ((), (), s32[]{:S(2)}) async-start(), calls=%async_computation.6 | async-start | bytes 1310720 | tf_op jit(solution)/shard_map/reduce_scatter | solution.py:299
  259.5 57.6 %copy-start.18 = (bf16[1536,1024]{1,0:T(8,128)(2,1)S(1)}, bf16[1536,1024]{1,0:T(8,128)(2,1)}, u32[]{:S(2)}) copy-start(bf16[1536,1024]{1,0:T(8,128)(2,1)} %param.16) | copy-start | bytes 9437188
  317.1 181.8 %reduce-scatter.5.cloned.1.call-start = ((), (), s32[]{:S(2)}) async-start(), calls=%async_computation.7 | async-start | bytes 5242880 | tf_op jit(solution)/shard_map/reduce_scatter | solution.py:297
  329.7 45.7 %collective-permute-start.5 = (bf16[512,1536]{1,0:T(8,128)(2,1)S(1)}, bf16[512,1536]{1,0:T(8,128)(2,1)}, u32[]{:S(2)}, u32[]{:S(2)}) collective-permute-start(bf16[512,1536]{1,0:T(8,128)(2,1)S(1)} %copy-done.11), channel_id=1, source_target_pairs={{0,0},{1,4},{2,8},{3,12},{4,1},{5,5},{6,9},{7,13},{8,2},{9,6},{10,... | collective-permute-start | bytes 4718600 | tf_op jit(solution)/shard_map/ppermute | solution.py:285
  378.6 123.2 %collective-permute-start.6 = (bf16[512,256]{1,0:T(8,128)(2,1)}, bf16[512,256]{1,0:T(8,128)(2,1)S(1)}, u32[]{:S(2)}, u32[]{:S(2)}) collective-permute-start(bf16[512,256]{1,0:T(8,128)(2,1)} %reduce-scatter.3.cloned.1.call-done), channel_id=1, source_target_pairs={{0,1},{1,2},{2,3},{4,5},{5,6},{6,7},{8,9},{9,10},{10,11},{12,13},{... | collective-permute-start | bytes 786440 | tf_op jit(solution)/shard_map/ppermute | solution.py:16
  380.6 122.9 %collective-permute-start.8 = (bf16[512,256]{1,0:T(8,128)(2,1)}, bf16[512,256]{1,0:T(8,128)(2,1)S(1)}, u32[]{:S(2)}, u32[]{:S(2)}) collective-permute-start(bf16[512,256]{1,0:T(8,128)(2,1)} %reduce-scatter.3.cloned.1.call-done), channel_id=1, source_target_pairs={{0,3},{4,7},{8,11},{12,15},{16,19},{20,23},{24,27},{28,31}} | collective-permute-start | bytes 786440 | tf_op jit(solution)/shard_map/ppermute | solution.py:16
  381.2 123.9 %collective-permute-start.7 = (bf16[512,256]{1,0:T(8,128)(2,1)}, bf16[512,256]{1,0:T(8,128)(2,1)S(1)}, u32[]{:S(2)}, u32[]{:S(2)}) collective-permute-start(bf16[512,256]{1,0:T(8,128)(2,1)} %reduce-scatter.3.cloned.1.call-done), channel_id=1, source_target_pairs={{0,2},{1,3},{4,6},{5,7},{8,10},{9,11},{12,14},{13,15},{16,18},{17,... | collective-permute-start | bytes 786440 | tf_op jit(solution)/shard_map/ppermute | solution.py:16
  506.8 4.4 copy-start.2
  519.6 5.6 %copy-start.16 = (bf16[512,256]{1,0:T(8,128)(2,1)S(1)}, bf16[512,256]{1,0:T(8,128)(2,1)}, u32[]{:S(2)}) copy-start(bf16[512,256]{1,0:T(8,128)(2,1)} %copy-done.15) | copy-start | bytes 786436
  525.2 8.7 %copy-start.1 = (bf16[1024,1536]{1,0:T(8,128)(2,1)S(1)}, bf16[1024,1536]{1,0:T(8,128)(2,1)}, u32[]{:S(2)}) copy-start(bf16[1024,1536]{1,0:T(8,128)(2,1)} %param.14) | copy-start | bytes 9437188
  (10 other events, 20.8 us)
Sparse Core Ops, SparseCore 0:
  29.4 30.4 all-gather.4
  71.1 44.4 all-gather.6
  117.7 44.4 all-gather.8
  259.6 51.7 all-gather.10
  317.2 61.4 reduce-scatter.2
  380.8 118.0 reduce-scatter.4

commit v8 on v7

--- a/solution.py
+++ b/solution.py
@@ -260,7 +260,6 @@
     n_seq = lax.axis_size("seq")
     tok_rows = lin_query.shape[0]
     heads_here = log_decay.shape[1]
-    head_width = heads_here * DH
     mine_a = lax.axis_index("heads")
     mine_b = lax.axis_index("seq")
     swap = [(x * n_seq + y, y * n_seq + x) for x in range(n_heads) for y in range(n_seq)]
@@ -282,7 +281,10 @@
         halves.append(heads_reduce_scatter(part.astype(jnp.bfloat16), n_heads))
     own_sum = jnp.concatenate(halves, axis=0)
     mixed_sum = stream_t.astype(jnp.float32) + own_sum
-    stream_next = lax.ppermute(mixed_sum.astype(jnp.bfloat16), ("heads", "seq"), swap)
+    next_t = mixed_sum.astype(jnp.bfloat16)
+    next_early = lax.ppermute(next_t[:half_rows], ("heads", "seq"), swap)
+    next_late = lax.ppermute(next_t[half_rows:], ("heads", "seq"), swap)
+    stream_next = jnp.concatenate([next_early, next_late], axis=0)
     total_sq = lax.psum(jnp.sum(mixed_sum * mixed_sum, axis=1), "seq")
     normed = (
         mixed_sum
@@ -294,26 +296,35 @@
     kv_mine = lax.dynamic_index_in_dim(kv_weight, kv_group, 0, keepdims=False)
     q_part = jnp.dot(normed_all, query_weight, preferred_element_type=jnp.float32)
     kv_part = jnp.dot(normed_all, kv_mine, preferred_element_type=jnp.float32)
-    queries = lax.psum_scatter(q_part.astype(jnp.bfloat16), "seq", scatter_dimension=0, tiled=True)
-    queries = queries.reshape(tok_rows, heads_here, DH)
     kv_own = lax.psum_scatter(kv_part.astype(jnp.bfloat16), "seq", scatter_dimension=0, tiled=True)
+    earlier_kv = [from_behind(kv_own, "seq", dist) for dist in range(1, n_seq)]
     query_pos = mine_b * tok_rows + jnp.arange(tok_rows)
-    state = (
-        jnp.full((heads_here, tok_rows), -1e30, jnp.float32),
-        jnp.zeros((heads_here, tok_rows), jnp.float32),
-        jnp.zeros((heads_here, tok_rows, DH), jnp.float32),
-    )
-    earlier_kv = [from_behind(kv_own, "seq", dist) for dist in range(1, n_seq)]
-    state = attend_block(queries, query_pos, state, kv_own, mine_b * tok_rows)
-    for dist in range(1, n_seq):
-        key_start = (mine_b - dist) * tok_rows
-        state = attend_block(queries, query_pos, state, earlier_kv[dist - 1], key_start)
-    _, row_total, weighted = state
-    attended = (
-        jnp.transpose(weighted / row_total[:, :, None], (1, 0, 2))
-        .reshape(tok_rows, head_width)
-        .astype(jnp.bfloat16)
-    )
+    q_groups = 2 if heads_here % 2 == 0 else 1
+    group_heads = heads_here // q_groups
+    group_width = group_heads * DH
+    pieces = []
+    for group in range(q_groups):
+        q_cols = q_part[:, group * group_width : (group + 1) * group_width]
+        queries = lax.psum_scatter(
+            q_cols.astype(jnp.bfloat16), "seq", scatter_dimension=0, tiled=True
+        )
+        queries = queries.reshape(tok_rows, group_heads, DH)
+        state = (
+            jnp.full((group_heads, tok_rows), -1e30, jnp.float32),
+            jnp.zeros((group_heads, tok_rows), jnp.float32),
+            jnp.zeros((group_heads, tok_rows, DH), jnp.float32),
+        )
+        state = attend_block(queries, query_pos, state, kv_own, mine_b * tok_rows)
+        for dist in range(1, n_seq):
+            key_start = (mine_b - dist) * tok_rows
+            state = attend_block(queries, query_pos, state, earlier_kv[dist - 1], key_start)
+        _, row_total, weighted = state
+        pieces.append(
+            jnp.transpose(weighted / row_total[:, :, None], (1, 0, 2))
+            .reshape(tok_rows, group_width)
+            .astype(jnp.bfloat16)
+        )
+    attended = jnp.concatenate(pieces, axis=1)
     return (stream_next, attended)
 
 

time: 546 us -> 559 us (1.024)
  matrix products: 72.9 us -> 90 us
  waiting for transfers between devices: 350 us -> 339 us
    reduce_scatter x1 -> x2, waiting for transfers between devices: 116 us -> 57.9 us  [shards_fast_body(): lax.psum_scatter(q_cols.astype(jnp.bfloat16), 'seq', scatter_dimension=0,...]
    ppermute x3, waiting for transfers between devices: 0.01 us -> 51.9 us  [from_behind(): lax.ppermute(value, axis, [(source, source + steps) for source in range(l...]
    dot_general x4 -> x8, matrix products: 7.79 us -> 30.4 us  [attend_block(): jnp.einsum('thd,sd->hts', queries, key_part, preferred_element_type=jnp.f...]
    unnamed x46 -> x58, local copies, waits for them, and re-layouts: 22.5 us -> 19.5 us
    dot_general x4 -> x8, matrix products: 13.7 us -> 10.7 us  [attend_block(): jnp.einsum('hts,sd->htd', prob_bf16, value_part, preferred_element_type=j...]
    ppermute x1 -> x2, waiting for transfers between devices: 41.1 us -> 39 us  [the longest x1 22.4 us: shards_fast_body(): next_early = lax.ppermute(next_t[:half_rows], ('heads', 'seq'), swap)]
  transfers between devices with their start and end apart: 15 -> 17, of which waited for: 9 -> 11; matrix products, arithmetic and copies ran while one was open for 12% -> 14% of each run, Pallas kernels for 0% -> 0%
where the time goes in v8:
time: 559 us; the launch traced here: 554 us
  waiting for transfers between devices  339 us (61%)
  matrix products  90 us (16%)
  local copies, waits for them, and re-layouts  43.2 us (8%)
  other arithmetic  36 us (6%)
  starting transfers between devices  16.3 us (3%)
  blocking collectives  15 us (3%)
  between operations  14.9 us (3%)
    all_gather x2, waiting for transfers between devices, shards_fast_body(): lax.all_gather(lin_out[half * half_rows:(half + 1) * half_rows], 'seq', a...  79 us
    reduce_scatter x2, waiting for transfers between devices, shards_fast_body(): lax.psum_scatter(q_cols.astype(jnp.bfloat16), 'seq', scatter_dimension=0,...  57.9 us
    ppermute x3, waiting for transfers between devices, from_behind(): lax.ppermute(value, axis, [(source, source + steps) for source in range(l...  51.9 us
    all_gather x1, waiting for transfers between devices, shards_fast_body(): normed_all = lax.all_gather(normed, 'heads', axis=0, tiled=True)  50.8 us
    dot_general x8, matrix products, attend_block(): jnp.einsum('thd,sd->hts', queries, key_part, preferred_element_type=jnp.f...  30.4 us
    ppermute x1, waiting for transfers between devices, shards_fast_body(): lax.ppermute(jnp.concatenate([stream, gain_rows], axis=0), ('heads', 'seq...  25.7 us
    ppermute x2, waiting for transfers between devices, heads_reduce_scatter(): lax.ppermute(send2.astype(jnp.bfloat16), 'heads', [(i, i ^ 2) for i in ra...  25.6 us
    ppermute x1, waiting for transfers between devices, shards_fast_body(): next_early = lax.ppermute(next_t[:half_rows], ('heads', 'seq'), swap)  22.4 us
  transfers between devices with their start and end apart: 17, of which 11 were waited for; matrix products, arithmetic and copies ran while one was open for 14% of the time, Pallas kernels for 0%

profile of v8, /device:TPU:21, one launch (start us, length us, event | category | flops | bytes accessed | tf_op | source)
XLA Modules:
  0.0 553.9 jit_solution(8208205220153308740)
XLA Ops:
  40.8 4.3 fusion.79
  48.4 4.5 fusion.78
  52.9 6.9 %all-gather.5.cloned.1.call-done = bf16[4,8,144,128]{3,2,1,0:T(8,128)(2,1)} async-done(((bf16[1,8,144,128]{3,2,1,0:T(8,128)(2,1)}), bf16[4,8,144,128]{3,2,1,0:T(8,128)(2,1)}) %all-gather.5.cloned.1.call-update) | async-done | bytes 1179664 | tf_op jit(solution)/shard_map/all_gather | solution.py:187
  62.6 4.5 multiply_reduce_fusion.2
  73.4 42.2 %all-gather.9.cloned.1.call-done = bf16[1024,1024]{0,1:T(8,128)(2,1)} async-done(((bf16[256,1024]{0,1:T(8,128)(2,1)}), bf16[1024,1024]{0,1:T(8,128)(2,1)}) %all-gather.9.cloned.1.call-update) | async-done | bytes 2097168 | tf_op jit(solution)/shard_map/all_gather | solution.py:277
  115.6 5.4 convolution_convert_fusion.1
  124.7 36.9 %all-gather.7.cloned.1.call-done = bf16[1024,1024]{0,1:T(8,128)(2,1)} async-done(((bf16[256,1024]{0,1:T(8,128)(2,1)}), bf16[1024,1024]{0,1:T(8,128)(2,1)}) %all-gather.7.cloned.1.call-update) | async-done | bytes 2097168 | tf_op jit(solution)/shard_map/all_gather | solution.py:277
  161.6 5.4 convolution_convert_fusion.2
  184.7 25.7 %collective-permute-done = bf16[528,1536]{1,0:T(8,128)(2,1)} collective-permute-done((bf16[528,1536]{1,0:T(8,128)(2,1)}, bf16[528,1536]{1,0:T(8,128)(2,1)}, u32[]{:S(2)}, u32[]{:S(2)}) %collective-permute-start) | collective-permute-done | bytes 1622048 | tf_op jit(solution)/shard_map/ppermute | solution.py:267
  213.0 25.6 %collective-permute-done.2 = bf16[256,1536]{1,0:T(8,128)(2,1)} collective-permute-done((bf16[256,1536]{1,0:T(8,128)(2,1)}, bf16[256,1536]{1,0:T(8,128)(2,1)}, u32[]{:S(2)}, u32[]{:S(2)}) %collective-permute-start.2) | collective-permute-done | bytes 786464 | tf_op jit(solution)/shard_map/ppermute | solution.py:224
  241.8 15.0 %psum.7 = f32[512]{0:T(512)S(1)} all-reduce(f32[512]{0:T(512)S(1)} %multiply_reduce_fusion), channel_id=1, replica_groups=mesh['groups'=2,'heads'=4,'seq'=4] {'seq'}, use_global_device_ids=true, to_apply=%region_11.12 | all-reduce | flops 512 | bytes 4096 | tf_op jit(solution)/shard_map/psum | solution.py:288
  256.8 3.6 multiply_convert_fusion
  260.5 50.8 %all-gather.11.cloned.1.call-done = bf16[2048,1536]{1,0:T(8,128)(2,1)} async-done(((bf16[512,1536]{1,0:T(8,128)(2,1)}), bf16[2048,1536]{1,0:T(8,128)(2,1)}) %all-gather.11.cloned.1.call-update) | async-done | bytes 6291472 | tf_op jit(solution)/shard_map/all_gather | solution.py:294
  311.3 5.7 %convolution_convert_fusion.3 = bf16[2048,256]{1,0:T(8,128)(2,1)} fusion(bf16[2048,1536]{1,0:T(8,128)(2,1)} %all-gather.11.cloned.1.call-done, bf16[4,1536,256]{2,1,0:T(8,128)(2,1)} %param.17, s32[]{:T(128)S(6)} %select_n.129), kind=kOutput, calls=%fused_computation.48 | convolution fusion | flops 1611137024 | bytes 8126468 | tf_op jit(solution)/shard_map/dot_general | solution.py:298
  317.1 8.7 %convolution_convert_fusion = bf16[2048,1024]{1,0:T(8,128)(2,1)S(1)} fusion(bf16[2048,1536]{1,0:T(8,128)(2,1)} %all-gather.11.cloned.1.call-done, bf16[1536,1024]{1,0:T(8,128)(2,1)S(1)} %copy-done.16), kind=kOutput, calls=%fused_computation.16 | convolution fusion | flops 6444548096 | bytes 13631488 | tf_op jit(solution)/shard_map/dot_general | solution.py:297
  336.5 22.4 %collective-permute-done.5 = bf16[256,1536]{1,0:T(8,128)(2,1)S(1)} collective-permute-done((bf16[256,1536]{1,0:T(8,128)(2,1)S(1)}, bf16[256,1536]{1,0:T(8,128)(2,1)S(1)}, u32[]{:S(2)}, u32[]{:S(2)}) %collective-permute-start.5) | collective-permute-done | bytes 786464 | tf_op jit(solution)/shard_map/ppermute | solution.py:285
  358.8 16.6 %collective-permute-done.6 = bf16[256,1536]{1,0:T(8,128)(2,1)} collective-permute-done((bf16[256,1536]{1,0:T(8,128)(2,1)S(1)}, bf16[256,1536]{1,0:T(8,128)(2,1)}, u32[]{:S(2)}, u32[]{:S(2)}) %collective-permute-start.6) | collective-permute-done | bytes 786464 | tf_op jit(solution)/shard_map/ppermute | solution.py:286
  383.0 57.9 %reduce-scatter.6.cloned.1.call-done = bf16[512,512]{1,0:T(8,128)(2,1)} async-done(((bf16[2048,512]{1,0:T(8,128)(2,1)}), bf16[512,512]{1,0:T(8,128)(2,1)}) %reduce-scatter.6.cloned.1.call-update) | async-done | bytes 524304 | tf_op jit(solution)/shard_map/reduce_scatter | solution.py:308
  440.9 4.0 fusion
  444.9 51.9 %collective-permute-done.7 = bf16[512,256]{1,0:T(8,128)(2,1)S(1)} collective-permute-done((bf16[512,256]{1,0:T(8,128)(2,1)}, bf16[512,256]{1,0:T(8,128)(2,1)S(1)}, u32[]{:S(2)}, u32[]{:S(2)}) %collective-permute-start.7) | collective-permute-done | bytes 262176 | tf_op jit(solution)/shard_map/ppermute | solution.py:16
  505.3 6.3 %fusion.14 = (f32[4,512]{1,0:T(4,128)S(1)}, f32[4,512]{1,0:T(4,128)S(1)}, f32[512,512,4]{1,0,2:T(8,128)}) fusion(f32[512,512,4]{1,0,2:T(8,128)} %get-tuple-element.55, f32[4,512]{1,0:T(4,128)S(1)} %get-tuple-element.19, pred[512,512]{0,1:T(8,128)(4,1)S(1)} %get-tuple-element.49, bf16[512,256]{1,0:T(8,128)(2,1)S(1)} %collective-permute-done.9, ...), kind=kOutput, calls=%fused_computation.38 | convolution fusion | flops 276819968 | bytes 9330688 | tf_op jit(solution)/shard_map/thd,sd->hts/dot_general | solution.py:235
  511.7 3.8 fusion.12
  515.5 3.9 fusion.10
  519.4 3.9 fusion.8
  (178 shorter events, 123.1 us)
Async XLA Ops:
  7.2 108.4 %copy-start = (bf16[1024,1536]{1,0:T(8,128)(2,1)S(1)}, bf16[1024,1536]{1,0:T(8,128)(2,1)}, u32[]{:S(2)}) copy-start(bf16[1024,1536]{1,0:T(8,128)(2,1)} %param.14) | copy-start | bytes 9437188
  7.2 52.7 %all-gather.5.cloned.1.call-start = ((), (), s32[]{:S(2)}) async-start(), calls=%async_computation.3 | async-start | bytes 1474560 | tf_op jit(solution)/shard_map/all_gather | solution.py:187
  17.6 12.0 %copy-start.14 = (f32[512,8]{0,1:T(8,128)S(1)}, f32[512,8]{0,1:T(8,128)}, u32[]{:S(2)}) copy-start(f32[512,8]{0,1:T(8,128)} %param.12) | copy-start | bytes 49156
  29.3 86.3 %all-gather.9.cloned.1.call-start = ((), (), s32[]{:S(2)}) async-start(), calls=%async_computation.5 | async-start | bytes 2621440 | tf_op jit(solution)/shard_map/all_gather | solution.py:277
  71.0 90.6 %all-gather.7.cloned.1.call-start = ((), (), s32[]{:S(2)}) async-start(), calls=%async_computation.4 | async-start | bytes 2621440 | tf_op jit(solution)/shard_map/all_gather | solution.py:277
  73.1 238.2 %all-gather.11.cloned.1.call-start = ((), (), s32[]{:S(2)}) async-start(), calls=%async_computation.6 | async-start | bytes 7864320 | tf_op jit(solution)/shard_map/all_gather | solution.py:294
  123.9 46.9 %copy-start.15 = (bf16[1536]{0:T(1024)(128)(2,1)S(1)}, bf16[1536]{0:T(1024)(128)(2,1)}, u32[]{:S(2)}) copy-start(bf16[1536]{0:T(1024)(128)(2,1)} %param.15) | copy-start | bytes 9220
  123.9 50.3 %collective-permute-start.3 = (bf16[2,256,1536]{2,1,0:T(8,128)(2,1)}, bf16[2,256,1536]{2,1,0:T(8,128)(2,1)}, u32[]{:S(2)}, u32[]{:S(2)}) collective-permute-start(bf16[2,256,1536]{2,1,0:T(8,128)(2,1)} %dynamic-slice_bitcast_fusion), channel_id=1, source_target_pairs={{0,4},{4,0},{8,12},{12,8},{1,5},{5,1},{9,13},{13,9},{2,6},{6,2},{1... | collective-permute-start | bytes 4718600 | tf_op jit(solution)/shard_map/ppermute | solution.py:220
  169.9 9.5 %collective-permute-start.1 = (bf16[2,256,1536]{2,1,0:T(8,128)(2,1)}, bf16[2,256,1536]{2,1,0:T(8,128)(2,1)}, u32[]{:S(2)}, u32[]{:S(2)}) collective-permute-start(bf16[2,256,1536]{2,1,0:T(8,128)(2,1)} %dynamic-slice_bitcast_fusion.1), channel_id=1, source_target_pairs={{0,4},{4,0},{8,12},{12,8},{1,5},{5,1},{9,13},{13,9},{2,6},{6,2},{1... | collective-permute-start | bytes 4718600 | tf_op jit(solution)/shard_map/ppermute | solution.py:220
  172.2 38.3 %collective-permute-start = (bf16[528,1536]{1,0:T(8,128)(2,1)}, bf16[528,1536]{1,0:T(8,128)(2,1)}, u32[]{:S(2)}, u32[]{:S(2)}) collective-permute-start(bf16[528,1536]{1,0:T(8,128)(2,1)} %pad_maximum_fusion), channel_id=1, source_target_pairs={{0,0},{1,4},{2,8},{3,12},{4,1},{5,5},{6,9},{7,13},{8,2},{9,6},{10,... | collective-permute-start | bytes 4866056 | tf_op jit(solution)/shard_map/ppermute | solution.py:267
  177.6 33.6 %collective-permute-start.4 = (bf16[256,1536]{1,0:T(8,128)(2,1)}, bf16[256,1536]{1,0:T(8,128)(2,1)}, u32[]{:S(2)}, u32[]{:S(2)}) collective-permute-start(bf16[256,1536]{1,0:T(8,128)(2,1)} %fusion.146), channel_id=1, source_target_pairs={{0,8},{4,12},{8,0},{12,4},{1,9},{5,13},{9,1},{13,5},{2,10},{6,14},... | collective-permute-start | bytes 2359304 | tf_op jit(solution)/shard_map/ppermute | solution.py:224
  184.4 54.2 %collective-permute-start.2 = (bf16[256,1536]{1,0:T(8,128)(2,1)}, bf16[256,1536]{1,0:T(8,128)(2,1)}, u32[]{:S(2)}, u32[]{:S(2)}) collective-permute-start(bf16[256,1536]{1,0:T(8,128)(2,1)} %fusion.145), channel_id=1, source_target_pairs={{0,8},{4,12},{8,0},{12,4},{1,9},{5,13},{9,1},{13,5},{2,10},{6,14},... | collective-permute-start | bytes 2359304 | tf_op jit(solution)/shard_map/ppermute | solution.py:224
  184.7 53.9 %copy-start.4 = (f32[2,256,1536]{2,1,0:T(8,128)S(1)}, f32[2,256,1536]{2,1,0:T(8,128)}, u32[]{:S(2)}) copy-start(f32[2,256,1536]{2,1,0:T(8,128)} %copy-done.3) | copy-start | bytes 9437188
  260.4 118.2 %reduce-scatter.4.cloned.1.call-start = ((), (), s32[]{:S(2)}) async-start(), calls=%async_computation.7 | async-start | bytes 1310720 | tf_op jit(solution)/shard_map/reduce_scatter | solution.py:299
  260.5 56.6 %copy-start.16 = (bf16[1536,1024]{1,0:T(8,128)(2,1)S(1)}, bf16[1536,1024]{1,0:T(8,128)(2,1)}, u32[]{:S(2)}) copy-start(bf16[1536,1024]{1,0:T(8,128)(2,1)} %param.16) | copy-start | bytes 9437188
  317.1 123.8 %reduce-scatter.6.cloned.1.call-start = ((), (), s32[]{:S(2)}) async-start(), calls=%async_computation.8 | async-start | bytes 2621440 | tf_op jit(solution)/shard_map/reduce_scatter | solution.py:308
  328.2 177.1 %reduce-scatter.8.cloned.1.call-start = ((), (), s32[]{:S(2)}) async-start(), calls=%async_computation.9 | async-start | bytes 2621440 | tf_op jit(solution)/shard_map/reduce_scatter | solution.py:308
  329.7 29.2 %collective-permute-start.5 = (bf16[256,1536]{1,0:T(8,128)(2,1)S(1)}, bf16[256,1536]{1,0:T(8,128)(2,1)S(1)}, u32[]{:S(2)}, u32[]{:S(2)}) collective-permute-start(bf16[256,1536]{1,0:T(8,128)(2,1)S(1)} %get-tuple-element.30), channel_id=1, source_target_pairs={{0,0},{1,4},{2,8},{3,12},{4,1},{5,5},{6,9},{7,13},{8,2},{9,6},{10,... | collective-permute-start | bytes 2359304 | tf_op jit(solution)/shard_map/ppermute | solution.py:285
  332.9 42.5 %collective-permute-start.6 = (bf16[256,1536]{1,0:T(8,128)(2,1)S(1)}, bf16[256,1536]{1,0:T(8,128)(2,1)}, u32[]{:S(2)}, u32[]{:S(2)}) collective-permute-start(bf16[256,1536]{1,0:T(8,128)(2,1)S(1)} %get-tuple-element.31), channel_id=1, source_target_pairs={{0,0},{1,4},{2,8},{3,12},{4,1},{5,5},{6,9},{7,13},{8,2},{9,6},{10,... | collective-permute-start | bytes 2359304 | tf_op jit(solution)/shard_map/ppermute | solution.py:286
  378.7 123.8 %collective-permute-start.9 = (bf16[512,256]{1,0:T(8,128)(2,1)}, bf16[512,256]{1,0:T(8,128)(2,1)S(1)}, u32[]{:S(2)}, u32[]{:S(2)}) collective-permute-start(bf16[512,256]{1,0:T(8,128)(2,1)} %reduce-scatter.4.cloned.1.call-done), channel_id=1, source_target_pairs={{0,3},{4,7},{8,11},{12,15},{16,19},{20,23},{24,27},{28,31}} | collective-permute-start | bytes 786440 | tf_op jit(solution)/shard_map/ppermute | solution.py:16
  379.3 120.3 %collective-permute-start.8 = (bf16[512,256]{1,0:T(8,128)(2,1)}, bf16[512,256]{1,0:T(8,128)(2,1)S(1)}, u32[]{:S(2)}, u32[]{:S(2)}) collective-permute-start(bf16[512,256]{1,0:T(8,128)(2,1)} %reduce-scatter.4.cloned.1.call-done), channel_id=1, source_target_pairs={{0,2},{1,3},{4,6},{5,7},{8,10},{9,11},{12,14},{13,15},{16,18},{17,... | collective-permute-start | bytes 786440 | tf_op jit(solution)/shard_map/ppermute | solution.py:16
  380.6 116.2 %collective-permute-start.7 = (bf16[512,256]{1,0:T(8,128)(2,1)}, bf16[512,256]{1,0:T(8,128)(2,1)S(1)}, u32[]{:S(2)}, u32[]{:S(2)}) collective-permute-start(bf16[512,256]{1,0:T(8,128)(2,1)} %reduce-scatter.4.cloned.1.call-done), channel_id=1, source_target_pairs={{0,1},{1,2},{2,3},{4,5},{5,6},{6,7},{8,9},{9,10},{10,11},{12,13},{... | collective-permute-start | bytes 786440 | tf_op jit(solution)/shard_map/ppermute | solution.py:16
  440.9 55.9 %copy-start.18 = (bf16[512,512]{1,0:T(8,128)(2,1)S(1)}, bf16[512,512]{1,0:T(8,128)(2,1)}, u32[]{:S(2)}) copy-start(bf16[512,512]{1,0:T(8,128)(2,1)} %reduce-scatter.6.cloned.1.call-done) | copy-start | bytes 1572868
  496.8 30.2 %copy-start.20 = (bf16[512,256]{1,0:T(8,128)(2,1)}, bf16[512,256]{1,0:T(8,128)(2,1)S(1)}, u32[]{:S(2)}) copy-start(bf16[512,256]{1,0:T(8,128)(2,1)S(1)} %collective-permute-done.7) | copy-start | bytes 786436
  (19 other events, 68.3 us)
Sparse Core Ops, SparseCore 0:
  29.4 30.3 all-gather.4
  71.1 44.4 all-gather.8
  117.1 44.4 all-gather.6
  260.6 50.7 all-gather.10
  317.2 61.4 reduce-scatter.3
  380.8 60.0 reduce-scatter.5
  443.2 58.3 reduce-scatter.7

commit v9 on v6

--- a/solution.py
+++ b/solution.py
@@ -1,6 +1,8 @@
 import jax
 import jax.numpy as jnp
 from jax import lax
+from jax.experimental import pallas as pl
+from jax.experimental.pallas import tpu as pltpu
 from jax.sharding import PartitionSpec as P
 
 D = 6144
@@ -225,28 +227,66 @@
     return keep2 + recv2.astype(jnp.float32)
 
 
-def attend_block(queries, query_pos, state_in, kv_block, key_start):
-    old_max, row_total, weighted = state_in
-    key_count = kv_block.shape[0]
-    key_part = kv_block[:, :DH]
-    value_part = kv_block[:, DH:]
+def attention_kernel(pos_ref, q_ref, kv_ref, o_ref, s_ref):
+    position = pos_ref[0]
+    n_blk = kv_ref.shape[0]
+    rows = q_ref.shape[0]
     score_scale = float(DH) ** (-0.5)
-    scores = (
-        jnp.einsum("thd,sd->hts", queries, key_part, preferred_element_type=jnp.float32)
-        * score_scale
-    )
-    key_pos = key_start + jnp.arange(key_count)
-    allowed = ((key_pos[None, :] <= query_pos[:, None]) & (key_pos[None, :] >= 0))[None, :, :]
-    scores = jnp.where(allowed, scores, -1e30)
-    new_max = jnp.maximum(old_max, jnp.max(scores, axis=-1))
-    expos = jnp.where(allowed, jnp.exp(scores - new_max[:, :, None]), 0.0)
-    rescale = jnp.exp(old_max - new_max)
-    row_total = row_total * rescale + jnp.sum(expos, axis=-1)
-    prob_bf16 = expos.astype(jnp.bfloat16)
-    weighted = weighted * rescale[:, :, None] + jnp.einsum(
-        "hts,sd->htd", prob_bf16, value_part, preferred_element_type=jnp.float32
-    )
-    return (new_max, row_total, weighted)
+    query = q_ref[...]
+    row_id = lax.broadcasted_iota(jnp.int32, (rows, rows), 0)
+    col_id = lax.broadcasted_iota(jnp.int32, (rows, rows), 1)
+
+    def allowed_of(dist):
+        if dist == 0:
+            return col_id <= row_id
+        return jnp.broadcast_to(dist <= position, (rows, rows))
+
+    row_max = jnp.full((rows, 1), -1e30, jnp.float32)
+    for dist in range(n_blk):
+        key = kv_ref[dist, :, :DH]
+        scores = lax.dot_general(
+            query, key, (((1,), (1,)), ((), ())), preferred_element_type=jnp.float32
+        ) * score_scale
+        scores = jnp.where(allowed_of(dist), scores, -1e30)
+        s_ref[dist] = scores
+        row_max = jnp.maximum(row_max, jnp.max(scores, axis=1, keepdims=True))
+    row_total = jnp.zeros((rows, 1), jnp.float32)
+    weighted = jnp.zeros((rows, DH), jnp.float32)
+    for dist in range(n_blk):
+        expos = jnp.where(allowed_of(dist), jnp.exp(s_ref[dist] - row_max), 0.0)
+        row_total = row_total + jnp.sum(expos, axis=1, keepdims=True)
+        weighted = weighted + jnp.dot(
+            expos.astype(jnp.bfloat16), kv_ref[dist, :, DH:], preferred_element_type=jnp.float32
+        )
+    o_ref[...] = (weighted / row_total).astype(o_ref.dtype)
+
+
+def attention_pallas(queries, kv_stack, position):
+    rows, width = queries.shape
+    n_blk = kv_stack.shape[0]
+    local_heads = width // DH
+    flops = 4 * local_heads * n_blk * rows * rows * DH
+    grid_spec = pltpu.PrefetchScalarGridSpec(
+        num_scalar_prefetch=1,
+        grid=(local_heads,),
+        in_specs=[
+            pl.BlockSpec((rows, DH), lambda h, pos: (0, h)),
+            pl.BlockSpec((n_blk, rows, 2 * DH), lambda h, pos: (0, 0, 0)),
+        ],
+        out_specs=pl.BlockSpec((rows, DH), lambda h, pos: (0, h)),
+        scratch_shapes=[pltpu.VMEM((n_blk, rows, rows), jnp.float32)],
+    )
+    return pl.pallas_call(
+        attention_kernel,
+        grid_spec=grid_spec,
+        out_shape=jax.ShapeDtypeStruct((rows, width), jnp.bfloat16),
+        compiler_params=pltpu.CompilerParams(dimension_semantics=("arbitrary",)),
+        cost_estimate=pl.CostEstimate(
+            flops=flops,
+            transcendentals=local_heads * n_blk * rows * rows,
+            bytes_accessed=2 * queries.size * 2 + kv_stack.size * 2,
+        ),
+    )(jnp.reshape(position, (1,)).astype(jnp.int32), queries, kv_stack)
 
 
 def shards_fast(*args):
@@ -260,7 +300,6 @@
     n_seq = lax.axis_size("seq")
     tok_rows = lin_query.shape[0]
     heads_here = log_decay.shape[1]
-    head_width = heads_here * DH
     mine_a = lax.axis_index("heads")
     mine_b = lax.axis_index("seq")
     swap = [(x * n_seq + y, y * n_seq + x) for x in range(n_heads) for y in range(n_seq)]
@@ -296,25 +335,11 @@
     kv_part = jnp.dot(normed_all, kv_mine, preferred_element_type=jnp.float32)
     queries = lax.psum_scatter(
         q_part.astype(jnp.bfloat16), "seq", scatter_dimension=0, tiled=True
-    ).reshape(tok_rows, heads_here, DH)
+    )
     kv_own = lax.psum_scatter(kv_part.astype(jnp.bfloat16), "seq", scatter_dimension=0, tiled=True)
-    query_pos = mine_b * tok_rows + jnp.arange(tok_rows)
-    state = (
-        jnp.full((heads_here, tok_rows), -1e30, jnp.float32),
-        jnp.zeros((heads_here, tok_rows), jnp.float32),
-        jnp.zeros((heads_here, tok_rows, DH), jnp.float32),
-    )
     earlier_kv = [from_behind(kv_own, "seq", dist) for dist in range(1, n_seq)]
-    state = attend_block(queries, query_pos, state, kv_own, mine_b * tok_rows)
-    for dist in range(1, n_seq):
-        key_start = (mine_b - dist) * tok_rows
-        state = attend_block(queries, query_pos, state, earlier_kv[dist - 1], key_start)
-    _, row_total, weighted = state
-    attended = (
-        jnp.transpose(weighted / row_total[:, :, None], (1, 0, 2))
-        .reshape(tok_rows, head_width)
-        .astype(jnp.bfloat16)
-    )
+    kv_stack = jnp.stack([kv_own] + earlier_kv, axis=0)
+    attended = attention_pallas(queries, kv_stack, mine_b)
     return (stream_next, attended)
 
 

time: 546 us -> 537 us (0.984)
  Pallas kernels: 0 us -> 25.2 us
  matrix products: 72.9 us -> 51 us
  other arithmetic: 32.7 us -> 25.3 us
    reduce_scatter x1, waiting for transfers between devices: 116 us -> 11.1 us  [shards_fast_body(): lax.psum_scatter(q_part.astype(jnp.bfloat16), 'seq', scatter_dimension=0,...]
    ppermute x3, waiting for transfers between devices: 0.01 us -> 104 us  [from_behind(): lax.ppermute(value, axis, [(source, source + steps) for source in range(l...]
    reduce_scatter x1, waiting for transfers between devices: 3.23 us -> 45.4 us  [shards_fast_body(): lax.psum_scatter(kv_part.astype(jnp.bfloat16), 'seq', scatter_dimension=0...]
    ppermute x1, waiting for transfers between devices: 41.1 us -> 0.01 us  [shards_fast_body(): lax.ppermute(mixed_sum.astype(jnp.bfloat16), ('heads', 'seq'), swap)]
    pallas_call x0 -> x1, Pallas kernels: none -> 25.2 us  [attention_pallas(): pl.pallas_call(attention_kernel, grid_spec=grid_spec, out_shape=jax.Shape...]
    dot_general x8 -> x0, matrix products: 21.5 us -> none  [the longest x4 13.7 us: attend_block(): jnp.einsum('hts,sd->htd', prob_bf16, value_part, preferred_element_type=j...]
    reduce_sum x4 -> x0, other arithmetic: 8.38 us -> none  [attend_block(): row_total = row_total * rescale + jnp.sum(expos, axis=-1)]
    unnamed x46 -> x39, local copies, waits for them, and re-layouts: 22.5 us -> 21.3 us
where the time goes in v9:
time: 537 us; the launch traced here: 535 us
  waiting for transfers between devices  349 us (65%)
  matrix products  51 us (9%)
  local copies, waits for them, and re-layouts  39.6 us (7%)
  other arithmetic  25.3 us (5%)
  Pallas kernels  25.2 us (5%)
  blocking collectives  16 us (3%)
  between operations  14.5 us (3%)
  starting transfers between devices  14 us (3%)
    ppermute x3, waiting for transfers between devices, from_behind(): lax.ppermute(value, axis, [(source, source + steps) for source in range(l...  104 us
    all_gather x2, waiting for transfers between devices, shards_fast_body(): lax.all_gather(lin_out[half * half_rows:(half + 1) * half_rows], 'seq', a...  79.6 us
    all_gather x1, waiting for transfers between devices, shards_fast_body(): normed_all = lax.all_gather(normed, 'heads', axis=0, tiled=True)  51.8 us
    reduce_scatter x1, waiting for transfers between devices, shards_fast_body(): lax.psum_scatter(kv_part.astype(jnp.bfloat16), 'seq', scatter_dimension=0...  45.4 us
    ppermute x1, waiting for transfers between devices, shards_fast_body(): lax.ppermute(jnp.concatenate([stream, gain_rows], axis=0), ('heads', 'seq...  28.5 us
    pallas_call x1, Pallas kernels, attention_pallas(): pl.pallas_call(attention_kernel, grid_spec=grid_spec, out_shape=jax.Shape...  25.2 us
    ppermute x2, waiting for transfers between devices, heads_reduce_scatter(): lax.ppermute(send2.astype(jnp.bfloat16), 'heads', [(i, i ^ 2) for i in ra...  22.3 us
    unnamed x39, local copies, waits for them, and re-layouts  21.3 us
  transfers between devices with their start and end apart: 15, of which 9 were waited for; matrix products, arithmetic and copies ran while one was open for 12% of the time, Pallas kernels for 0%

profile of v9, /device:TPU:21, one launch (start us, length us, event | category | flops | bytes accessed | tf_op | source)
XLA Modules:
  0.0 535.0 jit_solution(67665126823486993)
XLA Ops:
  37.4 3.4 fusion.3
  40.8 4.3 fusion.7
  45.1 3.3 fusion.5
  48.4 4.5 fusion.6
  52.9 6.9 %all-gather.5.cloned.1.call-done = bf16[4,8,144,128]{3,2,1,0:T(8,128)(2,1)} async-done(((bf16[1,8,144,128]{3,2,1,0:T(8,128)(2,1)}), bf16[4,8,144,128]{3,2,1,0:T(8,128)(2,1)}) %all-gather.5.cloned.1.call-update) | async-done | bytes 1179664 | tf_op jit(solution)/shard_map/all_gather | solution.py:189
  62.6 4.2 multiply_reduce_fusion.2
  73.1 42.2 %all-gather.7.cloned.1.call-done = bf16[1024,1024]{0,1:T(8,128)(2,1)} async-done(((bf16[256,1024]{0,1:T(8,128)(2,1)}), bf16[1024,1024]{0,1:T(8,128)(2,1)}) %all-gather.7.cloned.1.call-update) | async-done | bytes 2097168 | tf_op jit(solution)/shard_map/all_gather | solution.py:317
  115.3 5.4 %convolution_convert_fusion.2 = bf16[1024,1536]{1,0:T(8,128)(2,1)S(1)} fusion(bf16[1024,1024]{0,1:T(8,128)(2,1)} %all-gather.7.cloned.1.call-done, bf16[1024,1536]{1,0:T(8,128)(2,1)S(1)} %copy-done), kind=kOutput, calls=%fused_computation.2 | convolution fusion | flops 3222798336 | bytes 8388608 | tf_op jit(solution)/shard_map/dot_general | solution.py:320
  124.5 37.4 %all-gather.9.cloned.1.call-done = bf16[1024,1024]{0,1:T(8,128)(2,1)} async-done(((bf16[256,1024]{0,1:T(8,128)(2,1)}), bf16[1024,1024]{0,1:T(8,128)(2,1)}) %all-gather.9.cloned.1.call-update) | async-done | bytes 2097168 | tf_op jit(solution)/shard_map/all_gather | solution.py:317
  161.9 5.4 %convolution_convert_fusion.1 = bf16[1024,1536]{1,0:T(8,128)(2,1)S(1)} fusion(bf16[1024,1024]{0,1:T(8,128)(2,1)} %all-gather.9.cloned.1.call-done, bf16[1024,1536]{1,0:T(8,128)(2,1)S(1)} %copy-done), kind=kOutput, calls=%fused_computation.1 | convolution fusion | flops 3222798336 | bytes 8388608 | tf_op jit(solution)/shard_map/dot_general | solution.py:320
  171.3 2.8 collective-permute-start
  183.0 28.5 %collective-permute-done = bf16[528,1536]{1,0:T(8,128)(2,1)} collective-permute-done((bf16[528,1536]{1,0:T(8,128)(2,1)}, bf16[528,1536]{1,0:T(8,128)(2,1)}, u32[]{:S(2)}, u32[]{:S(2)}) %collective-permute-start) | collective-permute-done | bytes 1622048 | tf_op jit(solution)/shard_map/ppermute | solution.py:307
  214.1 22.3 %collective-permute-done.4 = bf16[256,1536]{1,0:T(8,128)(2,1)} collective-permute-done((bf16[256,1536]{1,0:T(8,128)(2,1)}, bf16[256,1536]{1,0:T(8,128)(2,1)}, u32[]{:S(2)}, u32[]{:S(2)}) %collective-permute-start.4) | collective-permute-done | bytes 786464 | tf_op jit(solution)/shard_map/ppermute | solution.py:226
  239.6 16.0 %psum.7 = f32[512]{0:T(512)S(1)} all-reduce(f32[512]{0:T(512)S(1)} %multiply_reduce_fusion), channel_id=1, replica_groups=mesh['groups'=2,'heads'=4,'seq'=4] {'seq'}, use_global_device_ids=true, to_apply=%region_11.12 | all-reduce | flops 512 | bytes 4096 | tf_op jit(solution)/shard_map/psum | solution.py:325
  255.6 3.6 multiply_convert_fusion
  259.3 51.8 %all-gather.11.cloned.1.call-done = bf16[2048,1536]{1,0:T(8,128)(2,1)} async-done(((bf16[512,1536]{1,0:T(8,128)(2,1)}), bf16[2048,1536]{1,0:T(8,128)(2,1)}) %all-gather.11.cloned.1.call-update) | async-done | bytes 6291472 | tf_op jit(solution)/shard_map/all_gather | solution.py:331
  311.1 5.7 %convolution_convert_fusion.3 = bf16[2048,256]{1,0:T(8,128)(2,1)} fusion(bf16[2048,1536]{1,0:T(8,128)(2,1)} %all-gather.11.cloned.1.call-done, bf16[4,1536,256]{2,1,0:T(8,128)(2,1)} %param.17, s32[]{:T(128)S(6)} %select_n.80), kind=kOutput, calls=%fused_computation.8 | convolution fusion | flops 1611137024 | bytes 8126468 | tf_op jit(solution)/shard_map/dot_general | solution.py:335
  316.9 11.1 %convolution_convert_fusion = bf16[2048,1024]{1,0:T(8,128)(2,1)} fusion(bf16[2048,1536]{1,0:T(8,128)(2,1)} %all-gather.11.cloned.1.call-done, bf16[1536,1024]{1,0:T(8,128)(2,1)S(1)} %copy-done.15), kind=kOutput, calls=%fused_computation | convolution fusion | flops 6444548096 | bytes 13631488 | tf_op jit(solution)/shard_map/dot_general | solution.py:334
  329.4 3.5 collective-permute-start.5
  332.9 45.4 %reduce-scatter.5.cloned.1.call-done = bf16[512,256]{1,0:T(8,128)(2,1)} async-done(((bf16[2048,256]{1,0:T(8,128)(2,1)}), bf16[512,256]{1,0:T(8,128)(2,1)}) %reduce-scatter.5.cloned.1.call-update) | async-done | bytes 262160 | tf_op jit(solution)/shard_map/reduce_scatter | solution.py:339
  383.5 103.7 %collective-permute-done.6 = bf16[512,256]{1,0:T(8,128)(2,1)S(1)} collective-permute-done((bf16[512,256]{1,0:T(8,128)(2,1)}, bf16[512,256]{1,0:T(8,128)(2,1)S(1)}, u32[]{:S(2)}, u32[]{:S(2)}) %collective-permute-start.6) | collective-permute-done | bytes 262176 | tf_op jit(solution)/shard_map/ppermute | solution.py:18
  489.2 11.1 %reduce-scatter.3.cloned.1.call-done.q_ref = bf16[512,1024]{1,0:T(8,128)(2,1)} async-done(((bf16[2048,1024]{1,0:T(8,128)(2,1)}), bf16[512,1024]{1,0:T(8,128)(2,1)}) %reduce-scatter.3.cloned.1.call-update) | async-done | bytes 1048592 | tf_op jit(solution)/shard_map/reduce_scatter | solution.py:336
  500.3 25.2 %shard_map.104 = bf16[512,1024]{1,0:T(8,128)(2,1)} custom-call(s32[1]{0:T(128)} %bitcast.40.pos_ref, bf16[512,1024]{1,0:T(8,128)(2,1)} %reduce-scatter.3.cloned.1.call-done.q_ref, bf16[4,512,256]{2,1,0:T(8,128)(2,1)} %pad_maximum_fusion.1.kv_ref), custom_call_target="tpu_custom_call" | custom-call | flops 4294967296 | bytes 3145728 | tf_op jit(solution)/shard_map/pallas_call | solution.py:279
  525.5 2.7 copy.157
  (121 shorter events, 70.2 us)
Async XLA Ops:
  7.2 108.1 %copy-start = (bf16[1024,1536]{1,0:T(8,128)(2,1)S(1)}, bf16[1024,1536]{1,0:T(8,128)(2,1)}, u32[]{:S(2)}) copy-start(bf16[1024,1536]{1,0:T(8,128)(2,1)} %param.14) | copy-start | bytes 9437188
  7.2 52.6 %all-gather.5.cloned.1.call-start = ((), (), s32[]{:S(2)}) async-start(), calls=%async_computation.2 | async-start | bytes 1474560 | tf_op jit(solution)/shard_map/all_gather | solution.py:189
  26.5 5.3 copy-start.13
  29.2 86.1 %all-gather.7.cloned.1.call-start = ((), (), s32[]{:S(2)}) async-start(), calls=%async_computation.3 | async-start | bytes 2621440 | tf_op jit(solution)/shard_map/all_gather | solution.py:317
  70.7 91.2 %all-gather.9.cloned.1.call-start = ((), (), s32[]{:S(2)}) async-start(), calls=%async_computation.4 | async-start | bytes 2621440 | tf_op jit(solution)/shard_map/all_gather | solution.py:317
  72.8 238.3 %all-gather.11.cloned.1.call-start = ((), (), s32[]{:S(2)}) async-start(), calls=%async_computation.5 | async-start | bytes 7864320 | tf_op jit(solution)/shard_map/all_gather | solution.py:331
  123.7 50.4 %collective-permute-start.1 = (bf16[2,256,1536]{2,1,0:T(8,128)(2,1)}, bf16[2,256,1536]{2,1,0:T(8,128)(2,1)}, u32[]{:S(2)}, u32[]{:S(2)}) collective-permute-start(bf16[2,256,1536]{2,1,0:T(8,128)(2,1)} %dynamic-slice_bitcast_fusion.1), channel_id=1, source_target_pairs={{0,4},{4,0},{8,12},{12,8},{1,5},{5,1},{9,13},{13,9},{2,6},{6,2},{1... | collective-permute-start | bytes 4718600 | tf_op jit(solution)/shard_map/ppermute | solution.py:222
  167.3 4.0 copy-start.7
  167.3 2.6 copy-start.11
  168.6 9.7 %collective-permute-start.3 = (bf16[2,256,1536]{2,1,0:T(8,128)(2,1)}, bf16[2,256,1536]{2,1,0:T(8,128)(2,1)}, u32[]{:S(2)}, u32[]{:S(2)}) collective-permute-start(bf16[2,256,1536]{2,1,0:T(8,128)(2,1)} %dynamic-slice_bitcast_fusion), channel_id=1, source_target_pairs={{0,4},{4,0},{8,12},{12,8},{1,5},{5,1},{9,13},{13,9},{2,6},{6,2},{1... | collective-permute-start | bytes 4718600 | tf_op jit(solution)/shard_map/ppermute | solution.py:222
  171.3 40.2 %collective-permute-start = (bf16[528,1536]{1,0:T(8,128)(2,1)}, bf16[528,1536]{1,0:T(8,128)(2,1)}, u32[]{:S(2)}, u32[]{:S(2)}) collective-permute-start(bf16[528,1536]{1,0:T(8,128)(2,1)} %pad_maximum_fusion), channel_id=1, source_target_pairs={{0,0},{1,4},{2,8},{3,12},{4,1},{5,5},{6,9},{7,13},{8,2},{9,6},{10,... | collective-permute-start | bytes 4866056 | tf_op jit(solution)/shard_map/ppermute | solution.py:307
  174.1 4.2 copy-start.8
  176.6 3.6 copy-start.2
  177.7 34.5 %collective-permute-start.2 = (bf16[256,1536]{1,0:T(8,128)(2,1)}, bf16[256,1536]{1,0:T(8,128)(2,1)}, u32[]{:S(2)}, u32[]{:S(2)}) collective-permute-start(bf16[256,1536]{1,0:T(8,128)(2,1)} %fusion.27), channel_id=1, source_target_pairs={{0,8},{4,12},{8,0},{12,4},{1,9},{5,13},{9,1},{13,5},{2,10},{6,14},... | collective-permute-start | bytes 2359304 | tf_op jit(solution)/shard_map/ppermute | solution.py:226
  182.1 54.2 %collective-permute-start.4 = (bf16[256,1536]{1,0:T(8,128)(2,1)}, bf16[256,1536]{1,0:T(8,128)(2,1)}, u32[]{:S(2)}, u32[]{:S(2)}) collective-permute-start(bf16[256,1536]{1,0:T(8,128)(2,1)} %fusion.28), channel_id=1, source_target_pairs={{0,8},{4,12},{8,0},{12,4},{1,9},{5,13},{9,1},{13,5},{2,10},{6,14},... | collective-permute-start | bytes 2359304 | tf_op jit(solution)/shard_map/ppermute | solution.py:226
  183.0 53.4 %copy-start.4 = (f32[2,256,1536]{2,1,0:T(8,128)S(1)}, f32[2,256,1536]{2,1,0:T(8,128)}, u32[]{:S(2)}) copy-start(f32[2,256,1536]{2,1,0:T(8,128)} %copy-done.3) | copy-start | bytes 9437188
  259.2 119.2 %reduce-scatter.5.cloned.1.call-start = ((), (), s32[]{:S(2)}) async-start(), calls=%async_computation.7 | async-start | bytes 1310720 | tf_op jit(solution)/shard_map/reduce_scatter | solution.py:339
  259.3 57.6 %copy-start.15 = (bf16[1536,1024]{1,0:T(8,128)(2,1)S(1)}, bf16[1536,1024]{1,0:T(8,128)(2,1)}, u32[]{:S(2)}) copy-start(bf16[1536,1024]{1,0:T(8,128)(2,1)} %param.16) | copy-start | bytes 9437188
  316.8 183.5 %reduce-scatter.3.cloned.1.call-start = ((), (), s32[]{:S(2)}) async-start(), calls=%async_computation.6 | async-start | bytes 5242880 | tf_op jit(solution)/shard_map/reduce_scatter | solution.py:336
  329.4 52.9 %collective-permute-start.5 = (bf16[512,1536]{1,0:T(8,128)(2,1)S(1)}, bf16[512,1536]{1,0:T(8,128)(2,1)S(1)}, u32[]{:S(2)}, u32[]{:S(2)}) collective-permute-start(bf16[512,1536]{1,0:T(8,128)(2,1)S(1)} %copy-done.10), channel_id=1, source_target_pairs={{0,0},{1,4},{2,8},{3,12},{4,1},{5,5},{6,9},{7,13},{8,2},{9,6},{10,... | collective-permute-start | bytes 4718600 | tf_op jit(solution)/shard_map/ppermute | solution.py:324
  378.4 108.8 %collective-permute-start.6 = (bf16[512,256]{1,0:T(8,128)(2,1)}, bf16[512,256]{1,0:T(8,128)(2,1)S(1)}, u32[]{:S(2)}, u32[]{:S(2)}) collective-permute-start(bf16[512,256]{1,0:T(8,128)(2,1)} %reduce-scatter.5.cloned.1.call-done), channel_id=1, source_target_pairs={{0,1},{1,2},{2,3},{4,5},{5,6},{6,7},{8,9},{9,10},{10,11},{12,13},{... | collective-permute-start | bytes 786440 | tf_op jit(solution)/shard_map/ppermute | solution.py:18
  380.3 106.8 %collective-permute-start.7 = (bf16[512,256]{1,0:T(8,128)(2,1)}, bf16[512,256]{1,0:T(8,128)(2,1)S(1)}, u32[]{:S(2)}, u32[]{:S(2)}) collective-permute-start(bf16[512,256]{1,0:T(8,128)(2,1)} %reduce-scatter.5.cloned.1.call-done), channel_id=1, source_target_pairs={{0,2},{1,3},{4,6},{5,7},{8,10},{9,11},{12,14},{13,15},{16,18},{17,... | collective-permute-start | bytes 786440 | tf_op jit(solution)/shard_map/ppermute | solution.py:18
  381.6 105.6 %collective-permute-start.8 = (bf16[512,256]{1,0:T(8,128)(2,1)}, bf16[512,256]{1,0:T(8,128)(2,1)S(1)}, u32[]{:S(2)}, u32[]{:S(2)}) collective-permute-start(bf16[512,256]{1,0:T(8,128)(2,1)} %reduce-scatter.5.cloned.1.call-done), channel_id=1, source_target_pairs={{0,3},{4,7},{8,11},{12,15},{16,19},{20,23},{24,27},{28,31}} | collective-permute-start | bytes 786440 | tf_op jit(solution)/shard_map/ppermute | solution.py:18
  500.3 27.9 %copy-start.1 = (bf16[1024,1536]{1,0:T(8,128)(2,1)S(1)}, bf16[1024,1536]{1,0:T(8,128)(2,1)}, u32[]{:S(2)}) copy-start(bf16[1024,1536]{1,0:T(8,128)(2,1)} %param.14) | copy-start | bytes 9437188
  (7 other events, 10.9 us)
Sparse Core Ops, SparseCore 0:
  29.4 30.3 all-gather.4
  70.8 44.4 all-gather.6
  117.4 44.4 all-gather.8
  259.3 51.6 all-gather.10
  316.9 61.4 reduce-scatter.4
  380.5 119.7 reduce-scatter.2

commit v10 on v9

--- a/solution.py
+++ b/solution.py
@@ -321,7 +321,10 @@
         halves.append(heads_reduce_scatter(part.astype(jnp.bfloat16), n_heads))
     own_sum = jnp.concatenate(halves, axis=0)
     mixed_sum = stream_t.astype(jnp.float32) + own_sum
-    stream_next = lax.ppermute(mixed_sum.astype(jnp.bfloat16), ("heads", "seq"), swap)
+    next_t = mixed_sum.astype(jnp.bfloat16)
+    next_early = lax.ppermute(next_t[:half_rows], ("heads", "seq"), swap)
+    next_late = lax.ppermute(next_t[half_rows:], ("heads", "seq"), swap)
+    stream_next = jnp.concatenate([next_early, next_late], axis=0)
     total_sq = lax.psum(jnp.sum(mixed_sum * mixed_sum, axis=1), "seq")
     normed = (
         mixed_sum
@@ -333,9 +336,7 @@
     kv_mine = lax.dynamic_index_in_dim(kv_weight, kv_group, 0, keepdims=False)
     q_part = jnp.dot(normed_all, query_weight, preferred_element_type=jnp.float32)
     kv_part = jnp.dot(normed_all, kv_mine, preferred_element_type=jnp.float32)
-    queries = lax.psum_scatter(
-        q_part.astype(jnp.bfloat16), "seq", scatter_dimension=0, tiled=True
-    )
+    queries = lax.psum_scatter(q_part.astype(jnp.bfloat16), "seq", scatter_dimension=0, tiled=True)
     kv_own = lax.psum_scatter(kv_part.astype(jnp.bfloat16), "seq", scatter_dimension=0, tiled=True)
     earlier_kv = [from_behind(kv_own, "seq", dist) for dist in range(1, n_seq)]
     kv_stack = jnp.stack([kv_own] + earlier_kv, axis=0)

time: 537 us -> 535 us (level)
    unnamed x39 -> x38, local copies, waits for them, and re-layouts: 21.3 us -> 17.5 us
  transfers between devices with their start and end apart: 15 -> 16, of which waited for: 9 -> 9; matrix products, arithmetic and copies ran while one was open for 12% -> 12% of each run, Pallas kernels for 0% -> 0%
where the time goes in v10:
time: 535 us; the launch traced here: 532 us
  waiting for transfers between devices  347 us (65%)
  matrix products  51 us (10%)
  local copies, waits for them, and re-layouts  36.8 us (7%)
  other arithmetic  25.7 us (5%)
  Pallas kernels  25.2 us (5%)
  starting transfers between devices  16.4 us (3%)
  blocking collectives  16 us (3%)
  between operations  14.5 us (3%)
    ppermute x3, waiting for transfers between devices, from_behind(): lax.ppermute(value, axis, [(source, source + steps) for source in range(l...  104 us
    all_gather x2, waiting for transfers between devices, shards_fast_body(): lax.all_gather(lin_out[half * half_rows:(half + 1) * half_rows], 'seq', a...  79.6 us
    all_gather x1, waiting for transfers between devices, shards_fast_body(): normed_all = lax.all_gather(normed, 'heads', axis=0, tiled=True)  51.8 us
    reduce_scatter x1, waiting for transfers between devices, shards_fast_body(): lax.psum_scatter(kv_part.astype(jnp.bfloat16), 'seq', scatter_dimension=0...  41.6 us
    ppermute x1, waiting for transfers between devices, shards_fast_body(): lax.ppermute(jnp.concatenate([stream, gain_rows], axis=0), ('heads', 'seq...  28.5 us
    pallas_call x1, Pallas kernels, attention_pallas(): pl.pallas_call(attention_kernel, grid_spec=grid_spec, out_shape=jax.Shape...  25.2 us
    ppermute x2, waiting for transfers between devices, heads_reduce_scatter(): lax.ppermute(send2.astype(jnp.bfloat16), 'heads', [(i, i ^ 2) for i in ra...  22.3 us
    unnamed x38, local copies, waits for them, and re-layouts  17.5 us
  transfers between devices with their start and end apart: 16, of which 9 were waited for; matrix products, arithmetic and copies ran while one was open for 12% of the time, Pallas kernels for 0%

profile of v10, /device:TPU:21, one launch (start us, length us, event | category | flops | bytes accessed | tf_op | source)
XLA Modules:
  0.0 532.4 jit_solution(17085374571017845975)
XLA Ops:
  37.4 3.4 fusion.3
  40.8 4.3 fusion.7
  45.1 3.3 fusion.5
  48.4 4.5 fusion.6
  52.9 6.9 %all-gather.5.cloned.1.call-done = bf16[4,8,144,128]{3,2,1,0:T(8,128)(2,1)} async-done(((bf16[1,8,144,128]{3,2,1,0:T(8,128)(2,1)}), bf16[4,8,144,128]{3,2,1,0:T(8,128)(2,1)}) %all-gather.5.cloned.1.call-update) | async-done | bytes 1179664 | tf_op jit(solution)/shard_map/all_gather | solution.py:189
  62.6 4.2 multiply_reduce_fusion.2
  73.1 42.2 %all-gather.7.cloned.1.call-done = bf16[1024,1024]{0,1:T(8,128)(2,1)} async-done(((bf16[256,1024]{0,1:T(8,128)(2,1)}), bf16[1024,1024]{0,1:T(8,128)(2,1)}) %all-gather.7.cloned.1.call-update) | async-done | bytes 2097168 | tf_op jit(solution)/shard_map/all_gather | solution.py:317
  115.3 5.4 %convolution_convert_fusion.2 = bf16[1024,1536]{1,0:T(8,128)(2,1)S(1)} fusion(bf16[1024,1024]{0,1:T(8,128)(2,1)} %all-gather.7.cloned.1.call-done, bf16[1024,1536]{1,0:T(8,128)(2,1)S(1)} %copy-done), kind=kOutput, calls=%fused_computation.2 | convolution fusion | flops 3222798336 | bytes 8388608 | tf_op jit(solution)/shard_map/dot_general | solution.py:320
  124.5 37.4 %all-gather.9.cloned.1.call-done = bf16[1024,1024]{0,1:T(8,128)(2,1)} async-done(((bf16[256,1024]{0,1:T(8,128)(2,1)}), bf16[1024,1024]{0,1:T(8,128)(2,1)}) %all-gather.9.cloned.1.call-update) | async-done | bytes 2097168 | tf_op jit(solution)/shard_map/all_gather | solution.py:317
  161.9 5.4 %convolution_convert_fusion.1 = bf16[1024,1536]{1,0:T(8,128)(2,1)S(1)} fusion(bf16[1024,1024]{0,1:T(8,128)(2,1)} %all-gather.9.cloned.1.call-done, bf16[1024,1536]{1,0:T(8,128)(2,1)S(1)} %copy-done), kind=kOutput, calls=%fused_computation.1 | convolution fusion | flops 3222798336 | bytes 8388608 | tf_op jit(solution)/shard_map/dot_general | solution.py:320
  171.3 2.8 collective-permute-start
  183.0 28.5 %collective-permute-done = bf16[528,1536]{1,0:T(8,128)(2,1)} collective-permute-done((bf16[528,1536]{1,0:T(8,128)(2,1)}, bf16[528,1536]{1,0:T(8,128)(2,1)}, u32[]{:S(2)}, u32[]{:S(2)}) %collective-permute-start) | collective-permute-done | bytes 1622048 | tf_op jit(solution)/shard_map/ppermute | solution.py:307
  214.1 22.3 %collective-permute-done.4 = bf16[256,1536]{1,0:T(8,128)(2,1)} collective-permute-done((bf16[256,1536]{1,0:T(8,128)(2,1)}, bf16[256,1536]{1,0:T(8,128)(2,1)}, u32[]{:S(2)}, u32[]{:S(2)}) %collective-permute-start.4) | collective-permute-done | bytes 786464 | tf_op jit(solution)/shard_map/ppermute | solution.py:226
  239.6 16.0 %psum.7 = f32[512]{0:T(512)S(1)} all-reduce(f32[512]{0:T(512)S(1)} %multiply_reduce_fusion), channel_id=1, replica_groups=mesh['groups'=2,'heads'=4,'seq'=4] {'seq'}, use_global_device_ids=true, to_apply=%region_11.12 | all-reduce | flops 512 | bytes 4096 | tf_op jit(solution)/shard_map/psum | solution.py:328
  255.6 3.6 multiply_convert_fusion
  259.3 51.8 %all-gather.11.cloned.1.call-done = bf16[2048,1536]{1,0:T(8,128)(2,1)} async-done(((bf16[512,1536]{1,0:T(8,128)(2,1)}), bf16[2048,1536]{1,0:T(8,128)(2,1)}) %all-gather.11.cloned.1.call-update) | async-done | bytes 6291472 | tf_op jit(solution)/shard_map/all_gather | solution.py:334
  311.1 5.7 %convolution_convert_fusion.3 = bf16[2048,256]{1,0:T(8,128)(2,1)} fusion(bf16[2048,1536]{1,0:T(8,128)(2,1)} %all-gather.11.cloned.1.call-done, bf16[4,1536,256]{2,1,0:T(8,128)(2,1)} %param.17, s32[]{:T(128)S(6)} %select_n.80), kind=kOutput, calls=%fused_computation.8 | convolution fusion | flops 1611137024 | bytes 8126468 | tf_op jit(solution)/shard_map/dot_general | solution.py:338
  316.9 11.1 %convolution_convert_fusion = bf16[2048,1024]{1,0:T(8,128)(2,1)} fusion(bf16[2048,1536]{1,0:T(8,128)(2,1)} %all-gather.11.cloned.1.call-done, bf16[1536,1024]{1,0:T(8,128)(2,1)S(1)} %copy-done.15), kind=kOutput, calls=%fused_computation | convolution fusion | flops 6444548096 | bytes 13631488 | tf_op jit(solution)/shard_map/dot_general | solution.py:337
  330.4 3.2 collective-permute-start.5
  333.7 2.6 collective-permute-start.6
  336.2 41.6 %reduce-scatter.5.cloned.1.call-done = bf16[512,256]{1,0:T(8,128)(2,1)} async-done(((bf16[2048,256]{1,0:T(8,128)(2,1)}), bf16[512,256]{1,0:T(8,128)(2,1)}) %reduce-scatter.5.cloned.1.call-update) | async-done | bytes 262160 | tf_op jit(solution)/shard_map/reduce_scatter | solution.py:340
  383.2 104.4 %collective-permute-done.7 = bf16[512,256]{1,0:T(8,128)(2,1)S(1)} collective-permute-done((bf16[512,256]{1,0:T(8,128)(2,1)}, bf16[512,256]{1,0:T(8,128)(2,1)S(1)}, u32[]{:S(2)}, u32[]{:S(2)}) %collective-permute-start.7) | collective-permute-done | bytes 262176 | tf_op jit(solution)/shard_map/ppermute | solution.py:18
  488.7 11.6 %reduce-scatter.3.cloned.1.call-done.q_ref = bf16[512,1024]{1,0:T(8,128)(2,1)} async-done(((bf16[2048,1024]{1,0:T(8,128)(2,1)}), bf16[512,1024]{1,0:T(8,128)(2,1)}) %reduce-scatter.3.cloned.1.call-update) | async-done | bytes 1048592 | tf_op jit(solution)/shard_map/reduce_scatter | solution.py:339
  500.3 25.2 %shard_map.104 = bf16[512,1024]{1,0:T(8,128)(2,1)} custom-call(s32[1]{0:T(128)} %bitcast.40.pos_ref, bf16[512,1024]{1,0:T(8,128)(2,1)} %reduce-scatter.3.cloned.1.call-done.q_ref, bf16[4,512,256]{2,1,0:T(8,128)(2,1)} %pad_maximum_fusion.2.kv_ref), custom_call_target="tpu_custom_call" | custom-call | flops 4294967296 | bytes 3145728 | tf_op jit(solution)/shard_map/pallas_call | solution.py:279
  (124 shorter events, 70.5 us)
Async XLA Ops:
  7.2 108.1 %copy-start = (bf16[1024,1536]{1,0:T(8,128)(2,1)S(1)}, bf16[1024,1536]{1,0:T(8,128)(2,1)}, u32[]{:S(2)}) copy-start(bf16[1024,1536]{1,0:T(8,128)(2,1)} %param.14) | copy-start | bytes 9437188
  7.2 52.6 %all-gather.5.cloned.1.call-start = ((), (), s32[]{:S(2)}) async-start(), calls=%async_computation.2 | async-start | bytes 1474560 | tf_op jit(solution)/shard_map/all_gather | solution.py:189
  26.5 5.3 copy-start.13
  29.2 86.1 %all-gather.7.cloned.1.call-start = ((), (), s32[]{:S(2)}) async-start(), calls=%async_computation.3 | async-start | bytes 2621440 | tf_op jit(solution)/shard_map/all_gather | solution.py:317
  70.7 91.2 %all-gather.9.cloned.1.call-start = ((), (), s32[]{:S(2)}) async-start(), calls=%async_computation.4 | async-start | bytes 2621440 | tf_op jit(solution)/shard_map/all_gather | solution.py:317
  72.8 238.3 %all-gather.11.cloned.1.call-start = ((), (), s32[]{:S(2)}) async-start(), calls=%async_computation.5 | async-start | bytes 7864320 | tf_op jit(solution)/shard_map/all_gather | solution.py:334
  123.7 50.4 %collective-permute-start.1 = (bf16[2,256,1536]{2,1,0:T(8,128)(2,1)}, bf16[2,256,1536]{2,1,0:T(8,128)(2,1)}, u32[]{:S(2)}, u32[]{:S(2)}) collective-permute-start(bf16[2,256,1536]{2,1,0:T(8,128)(2,1)} %dynamic-slice_bitcast_fusion.1), channel_id=1, source_target_pairs={{0,4},{4,0},{8,12},{12,8},{1,5},{5,1},{9,13},{13,9},{2,6},{6,2},{1... | collective-permute-start | bytes 4718600 | tf_op jit(solution)/shard_map/ppermute | solution.py:222
  167.3 4.0 copy-start.8
  168.6 9.7 %collective-permute-start.3 = (bf16[2,256,1536]{2,1,0:T(8,128)(2,1)}, bf16[2,256,1536]{2,1,0:T(8,128)(2,1)}, u32[]{:S(2)}, u32[]{:S(2)}) collective-permute-start(bf16[2,256,1536]{2,1,0:T(8,128)(2,1)} %dynamic-slice_bitcast_fusion), channel_id=1, source_target_pairs={{0,4},{4,0},{8,12},{12,8},{1,5},{5,1},{9,13},{13,9},{2,6},{6,2},{1... | collective-permute-start | bytes 4718600 | tf_op jit(solution)/shard_map/ppermute | solution.py:222
  171.3 40.2 %collective-permute-start = (bf16[528,1536]{1,0:T(8,128)(2,1)}, bf16[528,1536]{1,0:T(8,128)(2,1)}, u32[]{:S(2)}, u32[]{:S(2)}) collective-permute-start(bf16[528,1536]{1,0:T(8,128)(2,1)} %pad_maximum_fusion), channel_id=1, source_target_pairs={{0,0},{1,4},{2,8},{3,12},{4,1},{5,5},{6,9},{7,13},{8,2},{9,6},{10,... | collective-permute-start | bytes 4866056 | tf_op jit(solution)/shard_map/ppermute | solution.py:307
  174.1 4.2 copy-start.9
  177.7 34.5 %collective-permute-start.2 = (bf16[256,1536]{1,0:T(8,128)(2,1)}, bf16[256,1536]{1,0:T(8,128)(2,1)}, u32[]{:S(2)}, u32[]{:S(2)}) collective-permute-start(bf16[256,1536]{1,0:T(8,128)(2,1)} %fusion.27), channel_id=1, source_target_pairs={{0,8},{4,12},{8,0},{12,4},{1,9},{5,13},{9,1},{13,5},{2,10},{6,14},... | collective-permute-start | bytes 2359304 | tf_op jit(solution)/shard_map/ppermute | solution.py:226
  182.1 54.2 %collective-permute-start.4 = (bf16[256,1536]{1,0:T(8,128)(2,1)}, bf16[256,1536]{1,0:T(8,128)(2,1)}, u32[]{:S(2)}, u32[]{:S(2)}) collective-permute-start(bf16[256,1536]{1,0:T(8,128)(2,1)} %fusion.28), channel_id=1, source_target_pairs={{0,8},{4,12},{8,0},{12,4},{1,9},{5,13},{9,1},{13,5},{2,10},{6,14},... | collective-permute-start | bytes 2359304 | tf_op jit(solution)/shard_map/ppermute | solution.py:226
  183.0 53.4 %copy-start.4 = (f32[2,256,1536]{2,1,0:T(8,128)S(1)}, f32[2,256,1536]{2,1,0:T(8,128)}, u32[]{:S(2)}) copy-start(f32[2,256,1536]{2,1,0:T(8,128)} %copy-done.3) | copy-start | bytes 9437188
  259.2 118.6 %reduce-scatter.5.cloned.1.call-start = ((), (), s32[]{:S(2)}) async-start(), calls=%async_computation.7 | async-start | bytes 1310720 | tf_op jit(solution)/shard_map/reduce_scatter | solution.py:340
  259.3 57.6 %copy-start.15 = (bf16[1536,1024]{1,0:T(8,128)(2,1)S(1)}, bf16[1536,1024]{1,0:T(8,128)(2,1)}, u32[]{:S(2)}) copy-start(bf16[1536,1024]{1,0:T(8,128)(2,1)} %param.16) | copy-start | bytes 9437188
  316.8 183.5 %reduce-scatter.3.cloned.1.call-start = ((), (), s32[]{:S(2)}) async-start(), calls=%async_computation.6 | async-start | bytes 5242880 | tf_op jit(solution)/shard_map/reduce_scatter | solution.py:339
  330.4 51.5 %collective-permute-start.5 = (bf16[256,1536]{1,0:T(8,128)(2,1)}, bf16[256,1536]{1,0:T(8,128)(2,1)S(1)}, u32[]{:S(2)}, u32[]{:S(2)}) collective-permute-start(bf16[256,1536]{1,0:T(8,128)(2,1)} %get-tuple-element.8), channel_id=1, source_target_pairs={{0,0},{1,4},{2,8},{3,12},{4,1},{5,5},{6,9},{7,13},{8,2},{9,6},{10,... | collective-permute-start | bytes 2359304 | tf_op jit(solution)/shard_map/ppermute | solution.py:325
  333.7 48.2 %collective-permute-start.6 = (bf16[256,1536]{1,0:T(8,128)(2,1)S(1)}, bf16[256,1536]{1,0:T(8,128)(2,1)S(1)}, u32[]{:S(2)}, u32[]{:S(2)}) collective-permute-start(bf16[256,1536]{1,0:T(8,128)(2,1)S(1)} %get-tuple-element.9), channel_id=1, source_target_pairs={{0,0},{1,4},{2,8},{3,12},{4,1},{5,5},{6,9},{7,13},{8,2},{9,6},{10,... | collective-permute-start | bytes 2359304 | tf_op jit(solution)/shard_map/ppermute | solution.py:326
  377.9 109.7 %copy-start.12 = (bf16[512,256]{1,0:T(8,128)(2,1)S(1)}, bf16[512,256]{1,0:T(8,128)(2,1)}, u32[]{:S(2)}) copy-start(bf16[512,256]{1,0:T(8,128)(2,1)} %reduce-scatter.5.cloned.1.call-done) | copy-start | bytes 786436
  377.9 109.7 %collective-permute-start.7 = (bf16[512,256]{1,0:T(8,128)(2,1)}, bf16[512,256]{1,0:T(8,128)(2,1)S(1)}, u32[]{:S(2)}, u32[]{:S(2)}) collective-permute-start(bf16[512,256]{1,0:T(8,128)(2,1)} %reduce-scatter.5.cloned.1.call-done), channel_id=1, source_target_pairs={{0,1},{1,2},{2,3},{4,5},{5,6},{6,7},{8,9},{9,10},{10,11},{12,13},{... | collective-permute-start | bytes 786440 | tf_op jit(solution)/shard_map/ppermute | solution.py:18
  379.9 107.7 %collective-permute-start.8 = (bf16[512,256]{1,0:T(8,128)(2,1)}, bf16[512,256]{1,0:T(8,128)(2,1)S(1)}, u32[]{:S(2)}, u32[]{:S(2)}) collective-permute-start(bf16[512,256]{1,0:T(8,128)(2,1)} %reduce-scatter.5.cloned.1.call-done), channel_id=1, source_target_pairs={{0,2},{1,3},{4,6},{5,7},{8,10},{9,11},{12,14},{13,15},{16,18},{17,... | collective-permute-start | bytes 786440 | tf_op jit(solution)/shard_map/ppermute | solution.py:18
  381.2 106.4 %collective-permute-start.9 = (bf16[512,256]{1,0:T(8,128)(2,1)}, bf16[512,256]{1,0:T(8,128)(2,1)S(1)}, u32[]{:S(2)}, u32[]{:S(2)}) collective-permute-start(bf16[512,256]{1,0:T(8,128)(2,1)} %reduce-scatter.5.cloned.1.call-done), channel_id=1, source_target_pairs={{0,3},{4,7},{8,11},{12,15},{16,19},{20,23},{24,27},{28,31}} | collective-permute-start | bytes 786440 | tf_op jit(solution)/shard_map/ppermute | solution.py:18
  500.3 25.2 %copy-start.1 = (bf16[1024,1536]{1,0:T(8,128)(2,1)S(1)}, bf16[1024,1536]{1,0:T(8,128)(2,1)}, u32[]{:S(2)}) copy-start(bf16[1024,1536]{1,0:T(8,128)(2,1)} %param.14) | copy-start | bytes 9437188
  (8 other events, 15.9 us)
Sparse Core Ops, SparseCore 0:
  29.4 30.3 all-gather.4
  70.8 44.4 all-gather.6
  117.4 44.4 all-gather.8
  259.3 51.6 all-gather.10
  316.9 60.8 reduce-scatter.4
  380.0 120.2 reduce-scatter.2

commit v11 on v10

--- a/solution.py
+++ b/solution.py
@@ -41,6 +41,15 @@
         "shd,she->hde", key_f, value_blk.astype(jnp.float32), precision=lax.Precision.HIGHEST
     )
     return (kv_state, intra_out + inter_out)
+
+
+def block_state(kv_state, key_blk, value_blk, decay_blk):
+    local_cum = jnp.cumsum(decay_blk, axis=0)
+    tail_decay = jnp.exp(local_cum[-1][None, :] - local_cum)
+    key_f = key_blk.astype(jnp.float32) * tail_decay[:, :, None]
+    return jnp.exp(local_cum[-1])[:, None, None] * kv_state + jnp.einsum(
+        "shd,she->hde", key_f, value_blk.astype(jnp.float32), precision=lax.Precision.HIGHEST
+    )
 
 
 def shards_base(
@@ -176,16 +185,22 @@
     shape4 = (tok_rows, heads_here, DH)
     q4, k4, v4 = (x.reshape(shape4) for x in (lin_query, lin_key, lin_value))
     state = jnp.zeros((heads_here, DH, DH), jnp.float32)
-    outs = []
+    starts = []
     for blk in range(nblocks):
         rows = slice(blk * BLOCK, (blk + 1) * BLOCK)
-        state, out = lightning_block(state, (q4[rows], k4[rows], v4[rows], log_decay[rows]))
-        outs.append(out)
-    local_out = jnp.concatenate(outs, axis=0)
+        starts.append(state)
+        state = block_state(state, k4[rows], v4[rows], log_decay[rows])
     decay_total = jnp.sum(log_decay, axis=0)
     pad_rows = 16
     total_rows = jnp.broadcast_to(decay_total[:, None, None], (heads_here, pad_rows, DH))
     packed = jnp.concatenate([state, total_rows], axis=1).astype(jnp.bfloat16)
+    packed, starts, q4, k4, v4 = lax.optimization_barrier((packed, starts, q4, k4, v4))
+    outs = []
+    for blk in range(nblocks):
+        rows = slice(blk * BLOCK, (blk + 1) * BLOCK)
+        _, out = lightning_block(starts[blk], (q4[rows], k4[rows], v4[rows], log_decay[rows]))
+        outs.append(out)
+    local_out = jnp.concatenate(outs, axis=0)
     gathered = lax.all_gather(packed[None], "seq", axis=0, tiled=True)
     gathered = gathered.astype(jnp.float32)
     states = gathered[:, :, :DH, :]

time: 535 us -> 535 us (level)
  waiting for transfers between devices: 347 us -> 353 us
    unnamed x38 -> x44, local copies, waits for them, and re-layouts: 17.5 us -> 12.2 us
  transfers between devices with their start and end apart: 16 -> 16, of which waited for: 9 -> 9; matrix products, arithmetic and copies ran while one was open for 12% -> 11% of each run, Pallas kernels for 0% -> 0%
where the time goes in v11:
time: 535 us; the launch traced here: 533 us
  waiting for transfers between devices  353 us (66%)
  matrix products  46.9 us (9%)
  local copies, waits for them, and re-layouts  33.5 us (6%)
  other arithmetic  27 us (5%)
  Pallas kernels  25.2 us (5%)
  starting transfers between devices  16.1 us (3%)
  blocking collectives  16 us (3%)
  between operations  14.5 us (3%)
    ppermute x3, waiting for transfers between devices, from_behind(): lax.ppermute(value, axis, [(source, source + steps) for source in range(l...  104 us
    all_gather x2, waiting for transfers between devices, shards_fast_body(): lax.all_gather(lin_out[half * half_rows:(half + 1) * half_rows], 'seq', a...  81 us
    all_gather x1, waiting for transfers between devices, shards_fast_body(): normed_all = lax.all_gather(normed, 'heads', axis=0, tiled=True)  51.8 us
    reduce_scatter x1, waiting for transfers between devices, shards_fast_body(): lax.psum_scatter(kv_part.astype(jnp.bfloat16), 'seq', scatter_dimension=0...  41.7 us
    ppermute x1, waiting for transfers between devices, shards_fast_body(): lax.ppermute(jnp.concatenate([stream, gain_rows], axis=0), ('heads', 'seq...  28.5 us
    pallas_call x1, Pallas kernels, attention_pallas(): pl.pallas_call(attention_kernel, grid_spec=grid_spec, out_shape=jax.Shape...  25.2 us
    ppermute x2, waiting for transfers between devices, heads_reduce_scatter(): lax.ppermute(send2.astype(jnp.bfloat16), 'heads', [(i, i ^ 2) for i in ra...  22.3 us
    psum x1, blocking collectives, shards_fast_body(): total_sq = lax.psum(jnp.sum(mixed_sum * mixed_sum, axis=1), 'seq')  16 us
  transfers between devices with their start and end apart: 16, of which 9 were waited for; matrix products, arithmetic and copies ran while one was open for 11% of the time, Pallas kernels for 0%

profile of v11, /device:TPU:21, one launch (start us, length us, event | category | flops | bytes accessed | tf_op | source)
XLA Modules:
  0.0 532.7 jit_solution(13987052959951951641)
XLA Ops:
  11.2 2.8 slice_convert_fusion.1
  20.8 2.5 copy.102
  38.8 3.3 fusion.18
  44.5 3.6 fusion.7
  48.1 3.6 fusion.10
  51.7 11.4 %all-gather.12.cloned.1.call-done = bf16[32,144,128]{2,1,0:T(8,128)(2,1)} async-done(((bf16[8,144,128]{2,1,0:T(8,128)(2,1)}), bf16[32,144,128]{2,1,0:T(8,128)(2,1)}) %all-gather.12.cloned.1.call-update) | async-done | bytes 1179664 | tf_op jit(solution)/shard_map/all_gather | solution.py:204
  65.9 3.7 multiply_reduce_fusion.2
  72.0 43.6 %all-gather.6.cloned.1.call-done = bf16[1024,1024]{0,1:T(8,128)(2,1)} async-done(((bf16[256,1024]{0,1:T(8,128)(2,1)}), bf16[1024,1024]{0,1:T(8,128)(2,1)}) %all-gather.6.cloned.1.call-update) | async-done | bytes 2097168 | tf_op jit(solution)/shard_map/all_gather | solution.py:332
  115.6 5.4 %convolution_convert_fusion.2 = bf16[1024,1536]{1,0:T(8,128)(2,1)S(1)} fusion(bf16[1024,1024]{0,1:T(8,128)(2,1)} %all-gather.6.cloned.1.call-done, bf16[1024,1536]{1,0:T(8,128)(2,1)S(1)} %copy-done), kind=kOutput, calls=%fused_computation.2 | convolution fusion | flops 3222798336 | bytes 8388608 | tf_op jit(solution)/shard_map/dot_general | solution.py:335
  124.9 37.4 %all-gather.8.cloned.1.call-done = bf16[1024,1024]{0,1:T(8,128)(2,1)} async-done(((bf16[256,1024]{0,1:T(8,128)(2,1)}), bf16[1024,1024]{0,1:T(8,128)(2,1)}) %all-gather.8.cloned.1.call-update) | async-done | bytes 2097168 | tf_op jit(solution)/shard_map/all_gather | solution.py:332
  162.3 5.4 %convolution_convert_fusion.1 = bf16[1024,1536]{1,0:T(8,128)(2,1)S(1)} fusion(bf16[1024,1024]{0,1:T(8,128)(2,1)} %all-gather.8.cloned.1.call-done, bf16[1024,1536]{1,0:T(8,128)(2,1)S(1)} %copy-done), kind=kOutput, calls=%fused_computation.1 | convolution fusion | flops 3222798336 | bytes 8388608 | tf_op jit(solution)/shard_map/dot_general | solution.py:335
  171.6 2.8 collective-permute-start
  183.3 28.5 %collective-permute-done = bf16[528,1536]{1,0:T(8,128)(2,1)} collective-permute-done((bf16[528,1536]{1,0:T(8,128)(2,1)}, bf16[528,1536]{1,0:T(8,128)(2,1)}, u32[]{:S(2)}, u32[]{:S(2)}) %collective-permute-start) | collective-permute-done | bytes 1622048 | tf_op jit(solution)/shard_map/ppermute | solution.py:322
  214.4 22.3 %collective-permute-done.4 = bf16[256,1536]{1,0:T(8,128)(2,1)} collective-permute-done((bf16[256,1536]{1,0:T(8,128)(2,1)}, bf16[256,1536]{1,0:T(8,128)(2,1)}, u32[]{:S(2)}, u32[]{:S(2)}) %collective-permute-start.4) | collective-permute-done | bytes 786464 | tf_op jit(solution)/shard_map/ppermute | solution.py:241
  239.9 16.0 %psum.7 = f32[512]{0:T(512)S(1)} all-reduce(f32[512]{0:T(512)S(1)} %multiply_reduce_fusion), channel_id=1, replica_groups=mesh['groups'=2,'heads'=4,'seq'=4] {'seq'}, use_global_device_ids=true, to_apply=%region_11.12 | all-reduce | flops 512 | bytes 4096 | tf_op jit(solution)/shard_map/psum | solution.py:343
  255.9 3.6 multiply_convert_fusion
  259.6 51.8 %all-gather.10.cloned.1.call-done = bf16[2048,1536]{1,0:T(8,128)(2,1)} async-done(((bf16[512,1536]{1,0:T(8,128)(2,1)}), bf16[2048,1536]{1,0:T(8,128)(2,1)}) %all-gather.10.cloned.1.call-update) | async-done | bytes 6291472 | tf_op jit(solution)/shard_map/all_gather | solution.py:349
  311.4 5.7 %convolution_convert_fusion.3 = bf16[2048,256]{1,0:T(8,128)(2,1)} fusion(bf16[2048,1536]{1,0:T(8,128)(2,1)} %all-gather.10.cloned.1.call-done, bf16[4,1536,256]{2,1,0:T(8,128)(2,1)} %param.17, s32[]{:T(128)S(6)} %select_n.80), kind=kOutput, calls=%fused_computation.8 | convolution fusion | flops 1611137024 | bytes 8126468 | tf_op jit(solution)/shard_map/dot_general | solution.py:353
  317.2 11.1 %convolution_convert_fusion = bf16[2048,1024]{1,0:T(8,128)(2,1)} fusion(bf16[2048,1536]{1,0:T(8,128)(2,1)} %all-gather.10.cloned.1.call-done, bf16[1536,1024]{1,0:T(8,128)(2,1)S(1)} %copy-done.19), kind=kOutput, calls=%fused_computation | convolution fusion | flops 6444548096 | bytes 13631488 | tf_op jit(solution)/shard_map/dot_general | solution.py:352
  330.7 3.2 collective-permute-start.5
  336.5 41.7 %reduce-scatter.5.cloned.1.call-done = bf16[512,256]{1,0:T(8,128)(2,1)} async-done(((bf16[2048,256]{1,0:T(8,128)(2,1)}), bf16[512,256]{1,0:T(8,128)(2,1)}) %reduce-scatter.5.cloned.1.call-update) | async-done | bytes 262160 | tf_op jit(solution)/shard_map/reduce_scatter | solution.py:355
  383.5 104.4 %collective-permute-done.7 = bf16[512,256]{1,0:T(8,128)(2,1)S(1)} collective-permute-done((bf16[512,256]{1,0:T(8,128)(2,1)}, bf16[512,256]{1,0:T(8,128)(2,1)S(1)}, u32[]{:S(2)}, u32[]{:S(2)}) %collective-permute-start.7) | collective-permute-done | bytes 262176 | tf_op jit(solution)/shard_map/ppermute | solution.py:18
  489.1 11.6 %reduce-scatter.3.cloned.1.call-done.q_ref = bf16[512,1024]{1,0:T(8,128)(2,1)} async-done(((bf16[2048,1024]{1,0:T(8,128)(2,1)}), bf16[512,1024]{1,0:T(8,128)(2,1)}) %reduce-scatter.3.cloned.1.call-update) | async-done | bytes 1048592 | tf_op jit(solution)/shard_map/reduce_scatter | solution.py:354
  500.7 25.2 %shard_map.104 = bf16[512,1024]{1,0:T(8,128)(2,1)} custom-call(s32[1]{0:T(128)} %bitcast.41.pos_ref, bf16[512,1024]{1,0:T(8,128)(2,1)} %reduce-scatter.3.cloned.1.call-done.q_ref, bf16[4,512,256]{2,1,0:T(8,128)(2,1)} %pad_maximum_fusion.2.kv_ref), custom_call_target="tpu_custom_call" | custom-call | flops 4294967296 | bytes 3145728 | tf_op jit(solution)/shard_map/pallas_call | solution.py:294
  (133 shorter events, 67.6 us)
Async XLA Ops:
  7.2 108.5 %copy-start = (bf16[1024,1536]{1,0:T(8,128)(2,1)S(1)}, bf16[1024,1536]{1,0:T(8,128)(2,1)}, u32[]{:S(2)}) copy-start(bf16[1024,1536]{1,0:T(8,128)(2,1)} %param.14) | copy-start | bytes 9437188
  7.2 55.9 %all-gather.12.cloned.1.call-start = ((), (), s32[]{:S(2)}) async-start(), calls=%async_computation.7 | async-start | bytes 1474560 | tf_op jit(solution)/shard_map/all_gather | solution.py:204
  32.6 83.0 %all-gather.6.cloned.1.call-start = ((), (), s32[]{:S(2)}) async-start(), calls=%async_computation.2 | async-start | bytes 2621440 | tf_op jit(solution)/shard_map/all_gather | solution.py:332
  32.7 4.5 copy-start.17
  71.0 91.2 %all-gather.8.cloned.1.call-start = ((), (), s32[]{:S(2)}) async-start(), calls=%async_computation.3 | async-start | bytes 2621440 | tf_op jit(solution)/shard_map/all_gather | solution.py:332
  71.8 239.6 %all-gather.10.cloned.1.call-start = ((), (), s32[]{:S(2)}) async-start(), calls=%async_computation.4 | async-start | bytes 7864320 | tf_op jit(solution)/shard_map/all_gather | solution.py:349
  124.0 50.4 %collective-permute-start.1 = (bf16[2,256,1536]{2,1,0:T(8,128)(2,1)}, bf16[2,256,1536]{2,1,0:T(8,128)(2,1)}, u32[]{:S(2)}, u32[]{:S(2)}) collective-permute-start(bf16[2,256,1536]{2,1,0:T(8,128)(2,1)} %dynamic-slice_bitcast_fusion.1), channel_id=1, source_target_pairs={{0,4},{4,0},{8,12},{12,8},{1,5},{5,1},{9,13},{13,9},{2,6},{6,2},{1... | collective-permute-start | bytes 4718600 | tf_op jit(solution)/shard_map/ppermute | solution.py:237
  167.6 4.0 copy-start.11
  168.9 9.8 %collective-permute-start.3 = (bf16[2,256,1536]{2,1,0:T(8,128)(2,1)}, bf16[2,256,1536]{2,1,0:T(8,128)(2,1)}, u32[]{:S(2)}, u32[]{:S(2)}) collective-permute-start(bf16[2,256,1536]{2,1,0:T(8,128)(2,1)} %dynamic-slice_bitcast_fusion), channel_id=1, source_target_pairs={{0,4},{4,0},{8,12},{12,8},{1,5},{5,1},{9,13},{13,9},{2,6},{6,2},{1... | collective-permute-start | bytes 4718600 | tf_op jit(solution)/shard_map/ppermute | solution.py:237
  171.6 40.2 %collective-permute-start = (bf16[528,1536]{1,0:T(8,128)(2,1)}, bf16[528,1536]{1,0:T(8,128)(2,1)}, u32[]{:S(2)}, u32[]{:S(2)}) collective-permute-start(bf16[528,1536]{1,0:T(8,128)(2,1)} %pad_maximum_fusion), channel_id=1, source_target_pairs={{0,0},{1,4},{2,8},{3,12},{4,1},{5,5},{6,9},{7,13},{8,2},{9,6},{10,... | collective-permute-start | bytes 4866056 | tf_op jit(solution)/shard_map/ppermute | solution.py:322
  174.5 4.2 copy-start.12
  178.0 34.5 %collective-permute-start.2 = (bf16[256,1536]{1,0:T(8,128)(2,1)}, bf16[256,1536]{1,0:T(8,128)(2,1)}, u32[]{:S(2)}, u32[]{:S(2)}) collective-permute-start(bf16[256,1536]{1,0:T(8,128)(2,1)} %fusion.29), channel_id=1, source_target_pairs={{0,8},{4,12},{8,0},{12,4},{1,9},{5,13},{9,1},{13,5},{2,10},{6,14},... | collective-permute-start | bytes 2359304 | tf_op jit(solution)/shard_map/ppermute | solution.py:241
  182.4 54.3 %collective-permute-start.4 = (bf16[256,1536]{1,0:T(8,128)(2,1)}, bf16[256,1536]{1,0:T(8,128)(2,1)}, u32[]{:S(2)}, u32[]{:S(2)}) collective-permute-start(bf16[256,1536]{1,0:T(8,128)(2,1)} %fusion.30), channel_id=1, source_target_pairs={{0,8},{4,12},{8,0},{12,4},{1,9},{5,13},{9,1},{13,5},{2,10},{6,14},... | collective-permute-start | bytes 2359304 | tf_op jit(solution)/shard_map/ppermute | solution.py:241
  183.3 53.4 %copy-start.4 = (f32[2,256,1536]{2,1,0:T(8,128)S(1)}, f32[2,256,1536]{2,1,0:T(8,128)}, u32[]{:S(2)}) copy-start(f32[2,256,1536]{2,1,0:T(8,128)} %copy-done.3) | copy-start | bytes 9437188
  259.5 118.6 %reduce-scatter.5.cloned.1.call-start = ((), (), s32[]{:S(2)}) async-start(), calls=%async_computation.6 | async-start | bytes 1310720 | tf_op jit(solution)/shard_map/reduce_scatter | solution.py:355
  259.6 57.6 %copy-start.19 = (bf16[1536,1024]{1,0:T(8,128)(2,1)S(1)}, bf16[1536,1024]{1,0:T(8,128)(2,1)}, u32[]{:S(2)}) copy-start(bf16[1536,1024]{1,0:T(8,128)(2,1)} %param.16) | copy-start | bytes 9437188
  317.1 183.5 %reduce-scatter.3.cloned.1.call-start = ((), (), s32[]{:S(2)}) async-start(), calls=%async_computation.5 | async-start | bytes 5242880 | tf_op jit(solution)/shard_map/reduce_scatter | solution.py:354
  330.7 51.5 %collective-permute-start.5 = (bf16[256,1536]{1,0:T(8,128)(2,1)}, bf16[256,1536]{1,0:T(8,128)(2,1)S(1)}, u32[]{:S(2)}, u32[]{:S(2)}) collective-permute-start(bf16[256,1536]{1,0:T(8,128)(2,1)} %get-tuple-element.20), channel_id=1, source_target_pairs={{0,0},{1,4},{2,8},{3,12},{4,1},{5,5},{6,9},{7,13},{8,2},{9,6},{10,... | collective-permute-start | bytes 2359304 | tf_op jit(solution)/shard_map/ppermute | solution.py:340
  334.0 48.2 %collective-permute-start.6 = (bf16[256,1536]{1,0:T(8,128)(2,1)S(1)}, bf16[256,1536]{1,0:T(8,128)(2,1)S(1)}, u32[]{:S(2)}, u32[]{:S(2)}) collective-permute-start(bf16[256,1536]{1,0:T(8,128)(2,1)S(1)} %get-tuple-element.21), channel_id=1, source_target_pairs={{0,0},{1,4},{2,8},{3,12},{4,1},{5,5},{6,9},{7,13},{8,2},{9,6},{10,... | collective-permute-start | bytes 2359304 | tf_op jit(solution)/shard_map/ppermute | solution.py:341
  378.2 109.7 %copy-start.16 = (bf16[512,256]{1,0:T(8,128)(2,1)S(1)}, bf16[512,256]{1,0:T(8,128)(2,1)}, u32[]{:S(2)}) copy-start(bf16[512,256]{1,0:T(8,128)(2,1)} %reduce-scatter.5.cloned.1.call-done) | copy-start | bytes 786436
  378.2 109.7 %collective-permute-start.7 = (bf16[512,256]{1,0:T(8,128)(2,1)}, bf16[512,256]{1,0:T(8,128)(2,1)S(1)}, u32[]{:S(2)}, u32[]{:S(2)}) collective-permute-start(bf16[512,256]{1,0:T(8,128)(2,1)} %reduce-scatter.5.cloned.1.call-done), channel_id=1, source_target_pairs={{0,1},{1,2},{2,3},{4,5},{5,6},{6,7},{8,9},{9,10},{10,11},{12,13},{... | collective-permute-start | bytes 786440 | tf_op jit(solution)/shard_map/ppermute | solution.py:18
  380.2 107.7 %collective-permute-start.8 = (bf16[512,256]{1,0:T(8,128)(2,1)}, bf16[512,256]{1,0:T(8,128)(2,1)S(1)}, u32[]{:S(2)}, u32[]{:S(2)}) collective-permute-start(bf16[512,256]{1,0:T(8,128)(2,1)} %reduce-scatter.5.cloned.1.call-done), channel_id=1, source_target_pairs={{0,2},{1,3},{4,6},{5,7},{8,10},{9,11},{12,14},{13,15},{16,18},{17,... | collective-permute-start | bytes 786440 | tf_op jit(solution)/shard_map/ppermute | solution.py:18
  381.5 106.4 %collective-permute-start.9 = (bf16[512,256]{1,0:T(8,128)(2,1)}, bf16[512,256]{1,0:T(8,128)(2,1)S(1)}, u32[]{:S(2)}, u32[]{:S(2)}) collective-permute-start(bf16[512,256]{1,0:T(8,128)(2,1)} %reduce-scatter.5.cloned.1.call-done), channel_id=1, source_target_pairs={{0,3},{4,7},{8,11},{12,15},{16,19},{20,23},{24,27},{28,31}} | collective-permute-start | bytes 786440 | tf_op jit(solution)/shard_map/ppermute | solution.py:18
  500.7 25.2 %copy-start.1 = (bf16[1024,1536]{1,0:T(8,128)(2,1)S(1)}, bf16[1024,1536]{1,0:T(8,128)(2,1)}, u32[]{:S(2)}) copy-start(bf16[1024,1536]{1,0:T(8,128)(2,1)} %param.14) | copy-start | bytes 9437188
  (12 other events, 28.9 us)
Sparse Core Ops, SparseCore 0:
  32.7 30.3 all-gather.11
  71.2 44.4 all-gather.5
  117.8 44.4 all-gather.7
  259.7 51.7 all-gather.9
  317.3 60.8 reduce-scatter.4
  380.3 120.2 reduce-scatter.2

commit v12 on v11

--- a/solution.py
+++ b/solution.py
@@ -328,10 +328,9 @@
     lin_out = lightning_local(lin_query, lin_key, lin_value, log_decay)
     halves = []
     half_rows = tok_rows // 2
-    for half in range(2):
-        lin_all = lax.all_gather(
-            lin_out[half * half_rows : (half + 1) * half_rows], "seq", axis=0, tiled=True
-        )
+    cut = 3 * tok_rows // 4 if tok_rows % 32 == 0 else half_rows
+    for lo, hi in ((0, cut), (cut, tok_rows)):
+        lin_all = lax.all_gather(lin_out[lo:hi], "seq", axis=0, tiled=True)
         part = jnp.dot(lin_all, out_weight, preferred_element_type=jnp.float32)
         halves.append(heads_reduce_scatter(part.astype(jnp.bfloat16), n_heads))
     own_sum = jnp.concatenate(halves, axis=0)

time: 535 us -> 553 us (1.034)
  waiting for transfers between devices: 353 us -> 383 us
  blocking collectives: 16 us -> 7.9 us
    all_gather x2, waiting for transfers between devices: 81 us -> 125 us  [shards_fast_body(): lin_all = lax.all_gather(lin_out[lo:hi], 'seq', axis=0, tiled=True)]
    ppermute x1, waiting for transfers between devices: 28.5 us -> 0.01 us  [shards_fast_body(): lax.ppermute(jnp.concatenate([stream, gain_rows], axis=0), ('heads', 'seq...]
    ppermute x2, waiting for transfers between devices: 22.3 us -> 40.1 us  [heads_reduce_scatter(): lax.ppermute(send2.astype(jnp.bfloat16), 'heads', [(i, i ^ 2) for i in ra...]
    psum x1, blocking collectives: 16 us -> 7.9 us  [shards_fast_body(): total_sq = lax.psum(jnp.sum(mixed_sum * mixed_sum, axis=1), 'seq')]
    unnamed x44 -> x38, local copies, waits for them, and re-layouts: 12.2 us -> 12.4 us
  transfers between devices with their start and end apart: 16 -> 16, of which waited for: 9 -> 8; matrix products, arithmetic and copies ran while one was open for 11% -> 8% of each run, Pallas kernels for 0% -> 0%
where the time goes in v12:
time: 553 us; the launch traced here: 551 us
  waiting for transfers between devices  383 us (69%)
  matrix products  46.7 us (8%)
  local copies, waits for them, and re-layouts  33.6 us (6%)
  other arithmetic  25.9 us (5%)
  Pallas kernels  25.2 us (5%)
  starting transfers between devices  14.6 us (3%)
  between operations  14.5 us (3%)
  blocking collectives  7.9 us (1%)
    all_gather x2, waiting for transfers between devices, shards_fast_body(): lin_all = lax.all_gather(lin_out[lo:hi], 'seq', axis=0, tiled=True)  125 us
    ppermute x3, waiting for transfers between devices, from_behind(): lax.ppermute(value, axis, [(source, source + steps) for source in range(l...  105 us
    all_gather x1, waiting for transfers between devices, shards_fast_body(): normed_all = lax.all_gather(normed, 'heads', axis=0, tiled=True)  48.9 us
    reduce_scatter x1, waiting for transfers between devices, shards_fast_body(): lax.psum_scatter(kv_part.astype(jnp.bfloat16), 'seq', scatter_dimension=0...  41.5 us
    ppermute x2, waiting for transfers between devices, heads_reduce_scatter(): lax.ppermute(send2.astype(jnp.bfloat16), 'heads', [(i, i ^ 2) for i in ra...  40.1 us
    pallas_call x1, Pallas kernels, attention_pallas(): pl.pallas_call(attention_kernel, grid_spec=grid_spec, out_shape=jax.Shape...  25.2 us
    unnamed x38, local copies, waits for them, and re-layouts  12.4 us
    reduce_scatter x1, waiting for transfers between devices, shards_fast_body(): lax.psum_scatter(q_part.astype(jnp.bfloat16), 'seq', scatter_dimension=0,...  11.4 us
  transfers between devices with their start and end apart: 16, of which 8 were waited for; matrix products, arithmetic and copies ran while one was open for 8% of the time, Pallas kernels for 0%

profile of v12, /device:TPU:21, one launch (start us, length us, event | category | flops | bytes accessed | tf_op | source)
XLA Modules:
  0.0 551.4 jit_solution(6621501089922424781)
XLA Ops:
  11.2 2.8 slice_convert_fusion.1
  20.8 2.5 copy.102
  23.3 2.5 copy.103
  38.8 3.3 fusion.19
  44.5 3.6 fusion.7
  48.1 3.6 fusion.10
  51.7 11.4 %all-gather.12.cloned.1.call-done = bf16[32,144,128]{2,1,0:T(8,128)(2,1)} async-done(((bf16[8,144,128]{2,1,0:T(8,128)(2,1)}), bf16[32,144,128]{2,1,0:T(8,128)(2,1)}) %all-gather.12.cloned.1.call-update) | async-done | bytes 1179664 | tf_op jit(solution)/shard_map/all_gather | solution.py:204
  65.9 3.7 multiply_reduce_fusion.2
  72.1 61.7 %all-gather.6.cloned.1.call-done = bf16[1536,1024]{0,1:T(8,128)(2,1)} async-done(((bf16[384,1024]{0,1:T(8,128)(2,1)}), bf16[1536,1024]{0,1:T(8,128)(2,1)}) %all-gather.6.cloned.1.call-update) | async-done | bytes 3145744 | tf_op jit(solution)/shard_map/all_gather | solution.py:333
  133.9 7.3 %convolution_convert_fusion = bf16[1536,1536]{1,0:T(8,128)(2,1)S(1)} fusion(bf16[1536,1024]{0,1:T(8,128)(2,1)} %all-gather.6.cloned.1.call-done, bf16[1024,1536]{1,0:T(8,128)(2,1)S(1)} %copy-done), kind=kOutput, calls=%fused_computation | convolution fusion | flops 4834197504 | bytes 11010048 | tf_op jit(solution)/shard_map/dot_general | solution.py:334
  146.7 2.7 pad_maximum_fusion
  151.4 63.1 %all-gather.8.cloned.1.call-done = bf16[512,1024]{0,1:T(8,128)(2,1)} async-done(((bf16[128,1024]{0,1:T(8,128)(2,1)}), bf16[512,1024]{0,1:T(8,128)(2,1)}) %all-gather.8.cloned.1.call-update) | async-done | bytes 1048592 | tf_op jit(solution)/shard_map/all_gather | solution.py:333
  214.5 3.2 convolution_convert_fusion.2
  225.1 40.1 %collective-permute-done.4 = bf16[128,1536]{1,0:T(8,128)(2,1)S(1)} collective-permute-done((bf16[128,1536]{1,0:T(8,128)(2,1)S(1)}, bf16[128,1536]{1,0:T(8,128)(2,1)S(1)}, u32[]{:S(2)}, u32[]{:S(2)}) %collective-permute-start.4) | collective-permute-done | bytes 393248 | tf_op jit(solution)/shard_map/ppermute | solution.py:241
  269.6 7.9 %psum.7 = f32[512]{0:T(512)S(1)} all-reduce(f32[512]{0:T(512)S(1)} %multiply_reduce_fusion), channel_id=1, replica_groups=mesh['groups'=2,'heads'=4,'seq'=4] {'seq'}, use_global_device_ids=true, to_apply=%region_11.12 | all-reduce | flops 512 | bytes 4096 | tf_op jit(solution)/shard_map/psum | solution.py:342
  277.5 3.6 multiply_convert_fusion
  281.2 48.9 %all-gather.10.cloned.1.call-done = bf16[2048,1536]{1,0:T(8,128)(2,1)} async-done(((bf16[512,1536]{1,0:T(8,128)(2,1)}), bf16[2048,1536]{1,0:T(8,128)(2,1)}) %all-gather.10.cloned.1.call-update) | async-done | bytes 6291472 | tf_op jit(solution)/shard_map/all_gather | solution.py:348
  330.1 5.7 %convolution_convert_fusion.3 = bf16[2048,256]{1,0:T(8,128)(2,1)} fusion(bf16[2048,1536]{1,0:T(8,128)(2,1)} %all-gather.10.cloned.1.call-done, bf16[4,1536,256]{2,1,0:T(8,128)(2,1)} %param.17, s32[]{:T(128)S(6)} %select_n.82), kind=kOutput, calls=%fused_computation.7 | convolution fusion | flops 1611137024 | bytes 8126468 | tf_op jit(solution)/shard_map/dot_general | solution.py:352
  336.1 11.1 %convolution_convert_fusion.1 = bf16[2048,1024]{1,0:T(8,128)(2,1)} fusion(bf16[2048,1536]{1,0:T(8,128)(2,1)} %all-gather.10.cloned.1.call-done, bf16[1536,1024]{1,0:T(8,128)(2,1)S(1)} %copy-done.16), kind=kOutput, calls=%fused_computation.2 | convolution fusion | flops 6444548096 | bytes 13631488 | tf_op jit(solution)/shard_map/dot_general | solution.py:351
  349.7 3.3 collective-permute-start.5
  355.2 41.5 %reduce-scatter.5.cloned.1.call-done = bf16[512,256]{1,0:T(8,128)(2,1)} async-done(((bf16[2048,256]{1,0:T(8,128)(2,1)}), bf16[512,256]{1,0:T(8,128)(2,1)}) %reduce-scatter.5.cloned.1.call-update) | async-done | bytes 262160 | tf_op jit(solution)/shard_map/reduce_scatter | solution.py:354
  402.0 104.8 %collective-permute-done.7 = bf16[512,256]{1,0:T(8,128)(2,1)S(1)} collective-permute-done((bf16[512,256]{1,0:T(8,128)(2,1)}, bf16[512,256]{1,0:T(8,128)(2,1)S(1)}, u32[]{:S(2)}, u32[]{:S(2)}) %collective-permute-start.7) | collective-permute-done | bytes 262176 | tf_op jit(solution)/shard_map/ppermute | solution.py:18
  508.0 11.4 %reduce-scatter.3.cloned.1.call-done.q_ref = bf16[512,1024]{1,0:T(8,128)(2,1)} async-done(((bf16[2048,1024]{1,0:T(8,128)(2,1)}), bf16[512,1024]{1,0:T(8,128)(2,1)}) %reduce-scatter.3.cloned.1.call-update) | async-done | bytes 1048592 | tf_op jit(solution)/shard_map/reduce_scatter | solution.py:353
  519.4 25.2 %shard_map.104 = bf16[512,1024]{1,0:T(8,128)(2,1)} custom-call(s32[1]{0:T(128)} %bitcast.41.pos_ref, bf16[512,1024]{1,0:T(8,128)(2,1)} %reduce-scatter.3.cloned.1.call-done.q_ref, bf16[4,512,256]{2,1,0:T(8,128)(2,1)} %pad_maximum_fusion.2.kv_ref), custom_call_target="tpu_custom_call" | custom-call | flops 4294967296 | bytes 3145728 | tf_op jit(solution)/shard_map/pallas_call | solution.py:294
  (128 shorter events, 61.9 us)
Async XLA Ops:
  7.2 126.7 %copy-start = (bf16[1024,1536]{1,0:T(8,128)(2,1)S(1)}, bf16[1024,1536]{1,0:T(8,128)(2,1)}, u32[]{:S(2)}) copy-start(bf16[1024,1536]{1,0:T(8,128)(2,1)} %param.14) | copy-start | bytes 9437188
  7.2 55.9 %all-gather.12.cloned.1.call-start = ((), (), s32[]{:S(2)}) async-start(), calls=%async_computation.7 | async-start | bytes 1474560 | tf_op jit(solution)/shard_map/all_gather | solution.py:204
  32.6 101.3 %all-gather.6.cloned.1.call-start = ((), (), s32[]{:S(2)}) async-start(), calls=%async_computation.2 | async-start | bytes 3932160 | tf_op jit(solution)/shard_map/all_gather | solution.py:333
  32.7 4.5 copy-start.14
  38.6 3.6 copy-start.11
  71.9 142.7 %all-gather.8.cloned.1.call-start = ((), (), s32[]{:S(2)}) async-start(), calls=%async_computation.3 | async-start | bytes 1310720 | tf_op jit(solution)/shard_map/all_gather | solution.py:333
  141.2 5.5 copy-start.15
  144.1 74.8 %collective-permute-start.1 = (bf16[2,384,1536]{2,1,0:T(8,128)(2,1)}, bf16[2,384,1536]{2,1,0:T(8,128)(2,1)}, u32[]{:S(2)}, u32[]{:S(2)}) collective-permute-start(bf16[2,384,1536]{2,1,0:T(8,128)(2,1)} %dynamic-slice_bitcast_fusion), channel_id=1, source_target_pairs={{0,4},{4,0},{8,12},{12,8},{1,5},{5,1},{9,13},{13,9},{2,6},{6,2},{1... | collective-permute-start | bytes 7077896 | tf_op jit(solution)/shard_map/ppermute | solution.py:237
  146.6 183.5 %all-gather.10.cloned.1.call-start = ((), (), s32[]{:S(2)}) async-start(), calls=%async_computation.4 | async-start | bytes 7864320 | tf_op jit(solution)/shard_map/all_gather | solution.py:348
  149.4 75.0 %collective-permute-start = (bf16[528,1536]{1,0:T(8,128)(2,1)}, bf16[528,1536]{1,0:T(8,128)(2,1)}, u32[]{:S(2)}, u32[]{:S(2)}) collective-permute-start(bf16[528,1536]{1,0:T(8,128)(2,1)} %pad_maximum_fusion), channel_id=1, source_target_pairs={{0,0},{1,4},{2,8},{3,12},{4,1},{5,5},{6,9},{7,13},{8,2},{9,6},{10,... | collective-permute-start | bytes 4866056 | tf_op jit(solution)/shard_map/ppermute | solution.py:322
  214.5 4.3 copy-start.6
  217.8 4.7 collective-permute-start.3
  222.5 42.8 %collective-permute-start.2 = (bf16[384,1536]{1,0:T(8,128)(2,1)}, bf16[384,1536]{1,0:T(8,128)(2,1)}, u32[]{:S(2)}, u32[]{:S(2)}) collective-permute-start(bf16[384,1536]{1,0:T(8,128)(2,1)} %fusion.12), channel_id=1, source_target_pairs={{0,8},{4,12},{8,0},{12,4},{1,9},{5,13},{9,1},{13,5},{2,10},{6,14},... | collective-permute-start | bytes 3538952 | tf_op jit(solution)/shard_map/ppermute | solution.py:241
  223.9 41.4 %collective-permute-start.4 = (bf16[128,1536]{1,0:T(8,128)(2,1)S(1)}, bf16[128,1536]{1,0:T(8,128)(2,1)S(1)}, u32[]{:S(2)}, u32[]{:S(2)}) collective-permute-start(bf16[128,1536]{1,0:T(8,128)(2,1)S(1)} %fusion.48), channel_id=1, source_target_pairs={{0,8},{4,12},{8,0},{12,4},{1,9},{5,13},{9,1},{13,5},{2,10},{6,14},... | collective-permute-start | bytes 1179656 | tf_op jit(solution)/shard_map/ppermute | solution.py:241
  281.1 115.6 %reduce-scatter.5.cloned.1.call-start = ((), (), s32[]{:S(2)}) async-start(), calls=%async_computation.6 | async-start | bytes 1310720 | tf_op jit(solution)/shard_map/reduce_scatter | solution.py:354
  281.2 54.9 %copy-start.16 = (bf16[1536,1024]{1,0:T(8,128)(2,1)S(1)}, bf16[1536,1024]{1,0:T(8,128)(2,1)}, u32[]{:S(2)}) copy-start(bf16[1536,1024]{1,0:T(8,128)(2,1)} %param.16) | copy-start | bytes 9437188
  335.8 183.5 %reduce-scatter.3.cloned.1.call-start = ((), (), s32[]{:S(2)}) async-start(), calls=%async_computation.5 | async-start | bytes 5242880 | tf_op jit(solution)/shard_map/reduce_scatter | solution.py:353
  349.7 51.1 %collective-permute-start.5 = (bf16[256,1536]{1,0:T(8,128)(2,1)}, bf16[256,1536]{1,0:T(8,128)(2,1)S(1)}, u32[]{:S(2)}, u32[]{:S(2)}) collective-permute-start(bf16[256,1536]{1,0:T(8,128)(2,1)} %get-tuple-element.20), channel_id=1, source_target_pairs={{0,0},{1,4},{2,8},{3,12},{4,1},{5,5},{6,9},{7,13},{8,2},{9,6},{10,... | collective-permute-start | bytes 2359304 | tf_op jit(solution)/shard_map/ppermute | solution.py:339
  352.9 47.9 %collective-permute-start.6 = (bf16[256,1536]{1,0:T(8,128)(2,1)S(1)}, bf16[256,1536]{1,0:T(8,128)(2,1)S(1)}, u32[]{:S(2)}, u32[]{:S(2)}) collective-permute-start(bf16[256,1536]{1,0:T(8,128)(2,1)S(1)} %get-tuple-element.21), channel_id=1, source_target_pairs={{0,0},{1,4},{2,8},{3,12},{4,1},{5,5},{6,9},{7,13},{8,2},{9,6},{10,... | collective-permute-start | bytes 2359304 | tf_op jit(solution)/shard_map/ppermute | solution.py:340
  396.7 110.1 %copy-start.13 = (bf16[512,256]{1,0:T(8,128)(2,1)S(1)}, bf16[512,256]{1,0:T(8,128)(2,1)}, u32[]{:S(2)}) copy-start(bf16[512,256]{1,0:T(8,128)(2,1)} %reduce-scatter.5.cloned.1.call-done) | copy-start | bytes 786436
  396.7 110.1 %collective-permute-start.7 = (bf16[512,256]{1,0:T(8,128)(2,1)}, bf16[512,256]{1,0:T(8,128)(2,1)S(1)}, u32[]{:S(2)}, u32[]{:S(2)}) collective-permute-start(bf16[512,256]{1,0:T(8,128)(2,1)} %reduce-scatter.5.cloned.1.call-done), channel_id=1, source_target_pairs={{0,1},{1,2},{2,3},{4,5},{5,6},{6,7},{8,9},{9,10},{10,11},{12,13},{... | collective-permute-start | bytes 786440 | tf_op jit(solution)/shard_map/ppermute | solution.py:18
  398.8 108.0 %collective-permute-start.8 = (bf16[512,256]{1,0:T(8,128)(2,1)}, bf16[512,256]{1,0:T(8,128)(2,1)S(1)}, u32[]{:S(2)}, u32[]{:S(2)}) collective-permute-start(bf16[512,256]{1,0:T(8,128)(2,1)} %reduce-scatter.5.cloned.1.call-done), channel_id=1, source_target_pairs={{0,2},{1,3},{4,6},{5,7},{8,10},{9,11},{12,14},{13,15},{16,18},{17,... | collective-permute-start | bytes 786440 | tf_op jit(solution)/shard_map/ppermute | solution.py:18
  400.1 106.7 %collective-permute-start.9 = (bf16[512,256]{1,0:T(8,128)(2,1)}, bf16[512,256]{1,0:T(8,128)(2,1)S(1)}, u32[]{:S(2)}, u32[]{:S(2)}) collective-permute-start(bf16[512,256]{1,0:T(8,128)(2,1)} %reduce-scatter.5.cloned.1.call-done), channel_id=1, source_target_pairs={{0,3},{4,7},{8,11},{12,15},{16,19},{20,23},{24,27},{28,31}} | collective-permute-start | bytes 786440 | tf_op jit(solution)/shard_map/ppermute | solution.py:18
  519.4 25.2 %copy-start.1 = (bf16[1024,1536]{1,0:T(8,128)(2,1)S(1)}, bf16[1024,1536]{1,0:T(8,128)(2,1)}, u32[]{:S(2)}) copy-start(bf16[1024,1536]{1,0:T(8,128)(2,1)} %param.14) | copy-start | bytes 9437188
  (9 other events, 19.8 us)
Sparse Core Ops, SparseCore 0:
  32.7 30.3 all-gather.11
  72.0 61.8 all-gather.5
  146.7 67.7 all-gather.7
  281.3 48.8 all-gather.9
  336.0 60.7 reduce-scatter.4
  398.9 120.4 reduce-scatter.2

commit v13 on v11

--- a/solution.py
+++ b/solution.py
@@ -194,7 +194,10 @@
     pad_rows = 16
     total_rows = jnp.broadcast_to(decay_total[:, None, None], (heads_here, pad_rows, DH))
     packed = jnp.concatenate([state, total_rows], axis=1).astype(jnp.bfloat16)
-    packed, starts, q4, k4, v4 = lax.optimization_barrier((packed, starts, q4, k4, v4))
+    packed, starts, lin_query, k4, v4 = lax.optimization_barrier(
+        (packed, starts, lin_query, k4, v4)
+    )
+    q4 = lin_query.reshape(shape4)
     outs = []
     for blk in range(nblocks):
         rows = slice(blk * BLOCK, (blk + 1) * BLOCK)
@@ -268,7 +271,7 @@
     row_total = jnp.zeros((rows, 1), jnp.float32)
     weighted = jnp.zeros((rows, DH), jnp.float32)
     for dist in range(n_blk):
-        expos = jnp.where(allowed_of(dist), jnp.exp(s_ref[dist] - row_max), 0.0)
+        expos = jnp.exp(s_ref[dist] - row_max)
         row_total = row_total + jnp.sum(expos, axis=1, keepdims=True)
         weighted = weighted + jnp.dot(
             expos.astype(jnp.bfloat16), kv_ref[dist, :, DH:], preferred_element_type=jnp.float32

time: 535 us -> 532 us (level)
    unnamed x44 -> x45, local copies, waits for them, and re-layouts: 12.2 us -> 9.93 us
where the time goes in v13:
time: 532 us; the launch traced here: 530 us
  waiting for transfers between devices  353 us (66%)
  matrix products  46.1 us (9%)
  local copies, waits for them, and re-layouts  32.6 us (6%)
  other arithmetic  27 us (5%)
  Pallas kernels  24.2 us (5%)
  starting transfers between devices  16.1 us (3%)
  blocking collectives  16 us (3%)
  between operations  14.5 us (3%)
    ppermute x3, waiting for transfers between devices, from_behind(): lax.ppermute(value, axis, [(source, source + steps) for source in range(l...  104 us
    all_gather x2, waiting for transfers between devices, shards_fast_body(): lax.all_gather(lin_out[half * half_rows:(half + 1) * half_rows], 'seq', a...  81 us
    all_gather x1, waiting for transfers between devices, shards_fast_body(): normed_all = lax.all_gather(normed, 'heads', axis=0, tiled=True)  51.8 us
    reduce_scatter x1, waiting for transfers between devices, shards_fast_body(): lax.psum_scatter(kv_part.astype(jnp.bfloat16), 'seq', scatter_dimension=0...  41.7 us
    ppermute x1, waiting for transfers between devices, shards_fast_body(): lax.ppermute(jnp.concatenate([stream, gain_rows], axis=0), ('heads', 'seq...  28.5 us
    pallas_call x1, Pallas kernels, attention_pallas(): pl.pallas_call(attention_kernel, grid_spec=grid_spec, out_shape=jax.Shape...  24.2 us
    ppermute x2, waiting for transfers between devices, heads_reduce_scatter(): lax.ppermute(send2.astype(jnp.bfloat16), 'heads', [(i, i ^ 2) for i in ra...  22.3 us
    psum x1, blocking collectives, shards_fast_body(): total_sq = lax.psum(jnp.sum(mixed_sum * mixed_sum, axis=1), 'seq')  16 us
  transfers between devices with their start and end apart: 16, of which 9 were waited for; matrix products, arithmetic and copies ran while one was open for 11% of the time, Pallas kernels for 0%

profile of v13, /device:TPU:21, one launch (start us, length us, event | category | flops | bytes accessed | tf_op | source)
XLA Modules:
  0.0 530.0 jit_solution(16047213909855961650)
XLA Ops:
  11.2 2.8 slice_convert_fusion.1
  20.8 2.5 copy.112
  23.3 2.5 copy.113
  42.1 3.7 fusion.4
  45.8 3.7 fusion.7
  49.5 11.3 %all-gather.12.cloned.1.call-done = bf16[32,144,128]{2,1,0:T(8,128)(2,1)} async-done(((bf16[8,144,128]{2,1,0:T(8,128)(2,1)}), bf16[32,144,128]{2,1,0:T(8,128)(2,1)}) %all-gather.12.cloned.1.call-update) | async-done | bytes 1179664 | tf_op jit(solution)/shard_map/all_gather | solution.py:207
  63.6 4.2 multiply_reduce_fusion.2
  70.3 43.6 %all-gather.6.cloned.1.call-done = bf16[1024,1024]{0,1:T(8,128)(2,1)} async-done(((bf16[256,1024]{0,1:T(8,128)(2,1)}), bf16[1024,1024]{0,1:T(8,128)(2,1)}) %all-gather.6.cloned.1.call-update) | async-done | bytes 2097168 | tf_op jit(solution)/shard_map/all_gather | solution.py:335
  113.9 5.4 %convolution_convert_fusion.2 = bf16[1024,1536]{1,0:T(8,128)(2,1)S(1)} fusion(bf16[1024,1024]{0,1:T(8,128)(2,1)} %all-gather.6.cloned.1.call-done, bf16[1024,1536]{1,0:T(8,128)(2,1)S(1)} %copy-done), kind=kOutput, calls=%fused_computation.2 | convolution fusion | flops 3222798336 | bytes 8388608 | tf_op jit(solution)/shard_map/dot_general | solution.py:338
  123.1 37.4 %all-gather.8.cloned.1.call-done = bf16[1024,1024]{0,1:T(8,128)(2,1)} async-done(((bf16[256,1024]{0,1:T(8,128)(2,1)}), bf16[1024,1024]{0,1:T(8,128)(2,1)}) %all-gather.8.cloned.1.call-update) | async-done | bytes 2097168 | tf_op jit(solution)/shard_map/all_gather | solution.py:335
  160.5 5.4 %convolution_convert_fusion.1 = bf16[1024,1536]{1,0:T(8,128)(2,1)S(1)} fusion(bf16[1024,1024]{0,1:T(8,128)(2,1)} %all-gather.8.cloned.1.call-done, bf16[1024,1536]{1,0:T(8,128)(2,1)S(1)} %copy-done), kind=kOutput, calls=%fused_computation.1 | convolution fusion | flops 3222798336 | bytes 8388608 | tf_op jit(solution)/shard_map/dot_general | solution.py:338
  169.8 2.8 collective-permute-start
  181.5 28.5 %collective-permute-done = bf16[528,1536]{1,0:T(8,128)(2,1)} collective-permute-done((bf16[528,1536]{1,0:T(8,128)(2,1)}, bf16[528,1536]{1,0:T(8,128)(2,1)}, u32[]{:S(2)}, u32[]{:S(2)}) %collective-permute-start) | collective-permute-done | bytes 1622048 | tf_op jit(solution)/shard_map/ppermute | solution.py:325
  212.6 22.3 %collective-permute-done.4 = bf16[256,1536]{1,0:T(8,128)(2,1)} collective-permute-done((bf16[256,1536]{1,0:T(8,128)(2,1)}, bf16[256,1536]{1,0:T(8,128)(2,1)}, u32[]{:S(2)}, u32[]{:S(2)}) %collective-permute-start.4) | collective-permute-done | bytes 786464 | tf_op jit(solution)/shard_map/ppermute | solution.py:244
  238.1 16.0 %psum.7 = f32[512]{0:T(512)S(1)} all-reduce(f32[512]{0:T(512)S(1)} %multiply_reduce_fusion), channel_id=1, replica_groups=mesh['groups'=2,'heads'=4,'seq'=4] {'seq'}, use_global_device_ids=true, to_apply=%region_11.12 | all-reduce | flops 512 | bytes 4096 | tf_op jit(solution)/shard_map/psum | solution.py:346
  254.2 3.6 multiply_convert_fusion
  257.9 51.8 %all-gather.10.cloned.1.call-done = bf16[2048,1536]{1,0:T(8,128)(2,1)} async-done(((bf16[512,1536]{1,0:T(8,128)(2,1)}), bf16[2048,1536]{1,0:T(8,128)(2,1)}) %all-gather.10.cloned.1.call-update) | async-done | bytes 6291472 | tf_op jit(solution)/shard_map/all_gather | solution.py:352
  309.6 5.7 %convolution_convert_fusion.3 = bf16[2048,256]{1,0:T(8,128)(2,1)} fusion(bf16[2048,1536]{1,0:T(8,128)(2,1)} %all-gather.10.cloned.1.call-done, bf16[4,1536,256]{2,1,0:T(8,128)(2,1)} %param.17, s32[]{:T(128)S(6)} %select_n.80), kind=kOutput, calls=%fused_computation.8 | convolution fusion | flops 1611137024 | bytes 8126468 | tf_op jit(solution)/shard_map/dot_general | solution.py:356
  315.4 11.1 %convolution_convert_fusion = bf16[2048,1024]{1,0:T(8,128)(2,1)} fusion(bf16[2048,1536]{1,0:T(8,128)(2,1)} %all-gather.10.cloned.1.call-done, bf16[1536,1024]{1,0:T(8,128)(2,1)S(1)} %copy-done.20), kind=kOutput, calls=%fused_computation | convolution fusion | flops 6444548096 | bytes 13631488 | tf_op jit(solution)/shard_map/dot_general | solution.py:355
  329.0 3.2 collective-permute-start.5
  334.8 41.7 %reduce-scatter.5.cloned.1.call-done = bf16[512,256]{1,0:T(8,128)(2,1)} async-done(((bf16[2048,256]{1,0:T(8,128)(2,1)}), bf16[512,256]{1,0:T(8,128)(2,1)}) %reduce-scatter.5.cloned.1.call-update) | async-done | bytes 262160 | tf_op jit(solution)/shard_map/reduce_scatter | solution.py:358
  381.7 104.4 %collective-permute-done.7 = bf16[512,256]{1,0:T(8,128)(2,1)S(1)} collective-permute-done((bf16[512,256]{1,0:T(8,128)(2,1)}, bf16[512,256]{1,0:T(8,128)(2,1)S(1)}, u32[]{:S(2)}, u32[]{:S(2)}) %collective-permute-start.7) | collective-permute-done | bytes 262176 | tf_op jit(solution)/shard_map/ppermute | solution.py:18
  487.3 11.6 %reduce-scatter.3.cloned.1.call-done.q_ref = bf16[512,1024]{1,0:T(8,128)(2,1)} async-done(((bf16[2048,1024]{1,0:T(8,128)(2,1)}), bf16[512,1024]{1,0:T(8,128)(2,1)}) %reduce-scatter.3.cloned.1.call-update) | async-done | bytes 1048592 | tf_op jit(solution)/shard_map/reduce_scatter | solution.py:357
  498.9 24.2 %shard_map.104 = bf16[512,1024]{1,0:T(8,128)(2,1)} custom-call(s32[1]{0:T(128)} %bitcast.42.pos_ref, bf16[512,1024]{1,0:T(8,128)(2,1)} %reduce-scatter.3.cloned.1.call-done.q_ref, bf16[4,512,256]{2,1,0:T(8,128)(2,1)} %pad_maximum_fusion.2.kv_ref), custom_call_target="tpu_custom_call" | custom-call | flops 4294967296 | bytes 3145728 | tf_op jit(solution)/shard_map/pallas_call | solution.py:297
  (135 shorter events, 66.0 us)
Async XLA Ops:
  7.2 106.7 %copy-start = (bf16[1024,1536]{1,0:T(8,128)(2,1)S(1)}, bf16[1024,1536]{1,0:T(8,128)(2,1)}, u32[]{:S(2)}) copy-start(bf16[1024,1536]{1,0:T(8,128)(2,1)} %param.14) | copy-start | bytes 9437188
  7.2 53.6 %all-gather.12.cloned.1.call-start = ((), (), s32[]{:S(2)}) async-start(), calls=%async_computation.7 | async-start | bytes 1474560 | tf_op jit(solution)/shard_map/all_gather | solution.py:207
  30.3 83.6 %all-gather.6.cloned.1.call-start = ((), (), s32[]{:S(2)}) async-start(), calls=%async_computation.2 | async-start | bytes 2621440 | tf_op jit(solution)/shard_map/all_gather | solution.py:335
  30.5 4.6 copy-start.18
  69.3 91.2 %all-gather.8.cloned.1.call-start = ((), (), s32[]{:S(2)}) async-start(), calls=%async_computation.3 | async-start | bytes 2621440 | tf_op jit(solution)/shard_map/all_gather | solution.py:335
  70.0 239.6 %all-gather.10.cloned.1.call-start = ((), (), s32[]{:S(2)}) async-start(), calls=%async_computation.4 | async-start | bytes 7864320 | tf_op jit(solution)/shard_map/all_gather | solution.py:352
  122.2 50.4 %collective-permute-start.1 = (bf16[2,256,1536]{2,1,0:T(8,128)(2,1)}, bf16[2,256,1536]{2,1,0:T(8,128)(2,1)}, u32[]{:S(2)}, u32[]{:S(2)}) collective-permute-start(bf16[2,256,1536]{2,1,0:T(8,128)(2,1)} %dynamic-slice_bitcast_fusion.1), channel_id=1, source_target_pairs={{0,4},{4,0},{8,12},{12,8},{1,5},{5,1},{9,13},{13,9},{2,6},{6,2},{1... | collective-permute-start | bytes 4718600 | tf_op jit(solution)/shard_map/ppermute | solution.py:240
  165.9 4.0 copy-start.10
  167.1 9.7 %collective-permute-start.3 = (bf16[2,256,1536]{2,1,0:T(8,128)(2,1)}, bf16[2,256,1536]{2,1,0:T(8,128)(2,1)}, u32[]{:S(2)}, u32[]{:S(2)}) collective-permute-start(bf16[2,256,1536]{2,1,0:T(8,128)(2,1)} %dynamic-slice_bitcast_fusion), channel_id=1, source_target_pairs={{0,4},{4,0},{8,12},{12,8},{1,5},{5,1},{9,13},{13,9},{2,6},{6,2},{1... | collective-permute-start | bytes 4718600 | tf_op jit(solution)/shard_map/ppermute | solution.py:240
  169.8 40.2 %collective-permute-start = (bf16[528,1536]{1,0:T(8,128)(2,1)}, bf16[528,1536]{1,0:T(8,128)(2,1)}, u32[]{:S(2)}, u32[]{:S(2)}) collective-permute-start(bf16[528,1536]{1,0:T(8,128)(2,1)} %pad_maximum_fusion), channel_id=1, source_target_pairs={{0,0},{1,4},{2,8},{3,12},{4,1},{5,5},{6,9},{7,13},{8,2},{9,6},{10,... | collective-permute-start | bytes 4866056 | tf_op jit(solution)/shard_map/ppermute | solution.py:325
  172.7 4.2 copy-start.11
  176.3 34.5 %collective-permute-start.2 = (bf16[256,1536]{1,0:T(8,128)(2,1)}, bf16[256,1536]{1,0:T(8,128)(2,1)}, u32[]{:S(2)}, u32[]{:S(2)}) collective-permute-start(bf16[256,1536]{1,0:T(8,128)(2,1)} %fusion.26), channel_id=1, source_target_pairs={{0,8},{4,12},{8,0},{12,4},{1,9},{5,13},{9,1},{13,5},{2,10},{6,14},... | collective-permute-start | bytes 2359304 | tf_op jit(solution)/shard_map/ppermute | solution.py:244
  180.7 54.2 %collective-permute-start.4 = (bf16[256,1536]{1,0:T(8,128)(2,1)}, bf16[256,1536]{1,0:T(8,128)(2,1)}, u32[]{:S(2)}, u32[]{:S(2)}) collective-permute-start(bf16[256,1536]{1,0:T(8,128)(2,1)} %fusion.27), channel_id=1, source_target_pairs={{0,8},{4,12},{8,0},{12,4},{1,9},{5,13},{9,1},{13,5},{2,10},{6,14},... | collective-permute-start | bytes 2359304 | tf_op jit(solution)/shard_map/ppermute | solution.py:244
  181.5 53.4 %copy-start.4 = (f32[2,256,1536]{2,1,0:T(8,128)S(1)}, f32[2,256,1536]{2,1,0:T(8,128)}, u32[]{:S(2)}) copy-start(f32[2,256,1536]{2,1,0:T(8,128)} %copy-done.3) | copy-start | bytes 9437188
  257.8 118.6 %reduce-scatter.5.cloned.1.call-start = ((), (), s32[]{:S(2)}) async-start(), calls=%async_computation.6 | async-start | bytes 1310720 | tf_op jit(solution)/shard_map/reduce_scatter | solution.py:358
  257.8 57.6 %copy-start.20 = (bf16[1536,1024]{1,0:T(8,128)(2,1)S(1)}, bf16[1536,1024]{1,0:T(8,128)(2,1)}, u32[]{:S(2)}) copy-start(bf16[1536,1024]{1,0:T(8,128)(2,1)} %param.16) | copy-start | bytes 9437188
  315.4 183.5 %reduce-scatter.3.cloned.1.call-start = ((), (), s32[]{:S(2)}) async-start(), calls=%async_computation.5 | async-start | bytes 5242880 | tf_op jit(solution)/shard_map/reduce_scatter | solution.py:357
  329.0 51.5 %collective-permute-start.5 = (bf16[256,1536]{1,0:T(8,128)(2,1)}, bf16[256,1536]{1,0:T(8,128)(2,1)S(1)}, u32[]{:S(2)}, u32[]{:S(2)}) collective-permute-start(bf16[256,1536]{1,0:T(8,128)(2,1)} %get-tuple-element.20), channel_id=1, source_target_pairs={{0,0},{1,4},{2,8},{3,12},{4,1},{5,5},{6,9},{7,13},{8,2},{9,6},{10,... | collective-permute-start | bytes 2359304 | tf_op jit(solution)/shard_map/ppermute | solution.py:343
  332.2 48.2 %collective-permute-start.6 = (bf16[256,1536]{1,0:T(8,128)(2,1)S(1)}, bf16[256,1536]{1,0:T(8,128)(2,1)S(1)}, u32[]{:S(2)}, u32[]{:S(2)}) collective-permute-start(bf16[256,1536]{1,0:T(8,128)(2,1)S(1)} %get-tuple-element.21), channel_id=1, source_target_pairs={{0,0},{1,4},{2,8},{3,12},{4,1},{5,5},{6,9},{7,13},{8,2},{9,6},{10,... | collective-permute-start | bytes 2359304 | tf_op jit(solution)/shard_map/ppermute | solution.py:344
  376.4 109.7 %copy-start.17 = (bf16[512,256]{1,0:T(8,128)(2,1)S(1)}, bf16[512,256]{1,0:T(8,128)(2,1)}, u32[]{:S(2)}) copy-start(bf16[512,256]{1,0:T(8,128)(2,1)} %reduce-scatter.5.cloned.1.call-done) | copy-start | bytes 786436
  376.4 109.7 %collective-permute-start.7 = (bf16[512,256]{1,0:T(8,128)(2,1)}, bf16[512,256]{1,0:T(8,128)(2,1)S(1)}, u32[]{:S(2)}, u32[]{:S(2)}) collective-permute-start(bf16[512,256]{1,0:T(8,128)(2,1)} %reduce-scatter.5.cloned.1.call-done), channel_id=1, source_target_pairs={{0,1},{1,2},{2,3},{4,5},{5,6},{6,7},{8,9},{9,10},{10,11},{12,13},{... | collective-permute-start | bytes 786440 | tf_op jit(solution)/shard_map/ppermute | solution.py:18
  378.5 107.7 %collective-permute-start.8 = (bf16[512,256]{1,0:T(8,128)(2,1)}, bf16[512,256]{1,0:T(8,128)(2,1)S(1)}, u32[]{:S(2)}, u32[]{:S(2)}) collective-permute-start(bf16[512,256]{1,0:T(8,128)(2,1)} %reduce-scatter.5.cloned.1.call-done), channel_id=1, source_target_pairs={{0,2},{1,3},{4,6},{5,7},{8,10},{9,11},{12,14},{13,15},{16,18},{17,... | collective-permute-start | bytes 786440 | tf_op jit(solution)/shard_map/ppermute | solution.py:18
  379.8 106.4 %collective-permute-start.9 = (bf16[512,256]{1,0:T(8,128)(2,1)}, bf16[512,256]{1,0:T(8,128)(2,1)S(1)}, u32[]{:S(2)}, u32[]{:S(2)}) collective-permute-start(bf16[512,256]{1,0:T(8,128)(2,1)} %reduce-scatter.5.cloned.1.call-done), channel_id=1, source_target_pairs={{0,3},{4,7},{8,11},{12,15},{16,19},{20,23},{24,27},{28,31}} | collective-permute-start | bytes 786440 | tf_op jit(solution)/shard_map/ppermute | solution.py:18
  498.9 24.2 %copy-start.1 = (bf16[1024,1536]{1,0:T(8,128)(2,1)S(1)}, bf16[1024,1536]{1,0:T(8,128)(2,1)}, u32[]{:S(2)}) copy-start(bf16[1024,1536]{1,0:T(8,128)(2,1)} %param.14) | copy-start | bytes 9437188
  (13 other events, 29.5 us)
Sparse Core Ops, SparseCore 0:
  30.4 30.3 all-gather.11
  69.4 44.4 all-gather.5
  116.0 44.4 all-gather.7
  257.9 51.6 all-gather.9
  315.5 60.8 reduce-scatter.4
  378.6 120.2 reduce-scatter.2

commit v14 on v13

--- a/solution.py
+++ b/solution.py
@@ -271,7 +271,7 @@
     row_total = jnp.zeros((rows, 1), jnp.float32)
     weighted = jnp.zeros((rows, DH), jnp.float32)
     for dist in range(n_blk):
-        expos = jnp.exp(s_ref[dist] - row_max)
+        expos = jnp.where(allowed_of(dist), jnp.exp(s_ref[dist] - row_max), 0.0)
         row_total = row_total + jnp.sum(expos, axis=1, keepdims=True)
         weighted = weighted + jnp.dot(
             expos.astype(jnp.bfloat16), kv_ref[dist, :, DH:], preferred_element_type=jnp.float32
@@ -322,11 +322,13 @@
     mine_b = lax.axis_index("seq")
     swap = [(x * n_seq + y, y * n_seq + x) for x in range(n_heads) for y in range(n_seq)]
     gain_rows = jnp.broadcast_to(norm_gain[None, :], (16, norm_gain.shape[0]))
+    split_rows = tok_rows // 2
     packed = lax.ppermute(
-        jnp.concatenate([stream, gain_rows], axis=0), ("heads", "seq"), swap
-    )
-    stream_t = packed[:tok_rows]
-    gain_b = packed[tok_rows]
+        jnp.concatenate([stream[:split_rows], gain_rows], axis=0), ("heads", "seq"), swap
+    )
+    rest = lax.ppermute(stream[split_rows:], ("heads", "seq"), swap)
+    stream_t = jnp.concatenate([packed[:split_rows], rest], axis=0)
+    gain_b = packed[split_rows]
 
     lin_out = lightning_local(lin_query, lin_key, lin_value, log_decay)
     halves = []

time: 532 us -> 533 us (level)
    ppermute x1 -> x2, waiting for transfers between devices: 28.5 us -> 7.51 us  [the longest x1 7.51 us: shards_fast_body(): lax.ppermute(jnp.concatenate([stream[:split_rows], gain_rows], axis=0), (...]
    ppermute x2, waiting for transfers between devices: 22.3 us -> 42.9 us  [heads_reduce_scatter(): lax.ppermute(send2.astype(jnp.bfloat16), 'heads', [(i, i ^ 2) for i in ra...]
  transfers between devices with their start and end apart: 16 -> 17, of which waited for: 9 -> 10; matrix products, arithmetic and copies ran while one was open for 11% -> 11% of each run, Pallas kernels for 0% -> 0%
where the time goes in v14:
time: 533 us; the launch traced here: 531 us
  waiting for transfers between devices  352 us (66%)
  matrix products  46.1 us (9%)
  local copies, waits for them, and re-layouts  34.8 us (7%)
  other arithmetic  26.5 us (5%)
  Pallas kernels  25.2 us (5%)
  starting transfers between devices  21 us (4%)
  between operations  14.6 us (3%)
  blocking collectives  11 us (2%)
    ppermute x3, waiting for transfers between devices, from_behind(): lax.ppermute(value, axis, [(source, source + steps) for source in range(l...  105 us
    all_gather x2, waiting for transfers between devices, shards_fast_body(): lax.all_gather(lin_out[half * half_rows:(half + 1) * half_rows], 'seq', a...  81 us
    all_gather x1, waiting for transfers between devices, shards_fast_body(): normed_all = lax.all_gather(normed, 'heads', axis=0, tiled=True)  50.9 us
    ppermute x2, waiting for transfers between devices, heads_reduce_scatter(): lax.ppermute(send2.astype(jnp.bfloat16), 'heads', [(i, i ^ 2) for i in ra...  42.9 us
    reduce_scatter x1, waiting for transfers between devices, shards_fast_body(): lax.psum_scatter(kv_part.astype(jnp.bfloat16), 'seq', scatter_dimension=0...  41.5 us
    pallas_call x1, Pallas kernels, attention_pallas(): pl.pallas_call(attention_kernel, grid_spec=grid_spec, out_shape=jax.Shape...  25.2 us
    reduce_scatter x1, waiting for transfers between devices, shards_fast_body(): lax.psum_scatter(q_part.astype(jnp.bfloat16), 'seq', scatter_dimension=0,...  11.4 us
    all_gather x1, waiting for transfers between devices, lightning_local(): gathered = lax.all_gather(packed[None], 'seq', axis=0, tiled=True)  11.3 us
  transfers between devices with their start and end apart: 17, of which 10 were waited for; matrix products, arithmetic and copies ran while one was open for 11% of the time, Pallas kernels for 0%

profile of v14, /device:TPU:21, one launch (start us, length us, event | category | flops | bytes accessed | tf_op | source)
XLA Modules:
  0.0 531.3 jit_solution(5369944060209782616)
XLA Ops:
  11.2 2.8 slice_convert_fusion.1
  42.1 3.7 fusion.4
  45.8 3.7 fusion.7
  49.5 11.3 %all-gather.12.cloned.1.call-done = bf16[32,144,128]{2,1,0:T(8,128)(2,1)} async-done(((bf16[8,144,128]{2,1,0:T(8,128)(2,1)}), bf16[32,144,128]{2,1,0:T(8,128)(2,1)}) %all-gather.12.cloned.1.call-update) | async-done | bytes 1179664 | tf_op jit(solution)/shard_map/all_gather | solution.py:207
  63.6 4.2 multiply_reduce_fusion.2
  70.3 43.6 %all-gather.6.cloned.1.call-done = bf16[1024,1024]{0,1:T(8,128)(2,1)} async-done(((bf16[256,1024]{0,1:T(8,128)(2,1)}), bf16[1024,1024]{0,1:T(8,128)(2,1)}) %all-gather.6.cloned.1.call-update) | async-done | bytes 2097168 | tf_op jit(solution)/shard_map/all_gather | solution.py:337
  113.9 5.4 %convolution_convert_fusion.2 = bf16[1024,1536]{1,0:T(8,128)(2,1)S(1)} fusion(bf16[1024,1024]{0,1:T(8,128)(2,1)} %all-gather.6.cloned.1.call-done, bf16[1024,1536]{1,0:T(8,128)(2,1)S(1)} %copy-done), kind=kOutput, calls=%fused_computation.2 | convolution fusion | flops 3222798336 | bytes 8388608 | tf_op jit(solution)/shard_map/dot_general | solution.py:340
  123.1 37.4 %all-gather.8.cloned.1.call-done = bf16[1024,1024]{0,1:T(8,128)(2,1)} async-done(((bf16[256,1024]{0,1:T(8,128)(2,1)}), bf16[1024,1024]{0,1:T(8,128)(2,1)}) %all-gather.8.cloned.1.call-update) | async-done | bytes 2097168 | tf_op jit(solution)/shard_map/all_gather | solution.py:337
  160.5 5.4 %convolution_convert_fusion.1 = bf16[1024,1536]{1,0:T(8,128)(2,1)S(1)} fusion(bf16[1024,1024]{0,1:T(8,128)(2,1)} %all-gather.8.cloned.1.call-done, bf16[1024,1536]{1,0:T(8,128)(2,1)S(1)} %copy-done), kind=kOutput, calls=%fused_computation.1 | convolution fusion | flops 3222798336 | bytes 8388608 | tf_op jit(solution)/shard_map/dot_general | solution.py:340
  170.4 2.8 collective-permute-start
  182.2 4.9 collective-permute-start.1
  187.0 7.5 %collective-permute-done = bf16[272,1536]{1,0:T(8,128)(2,1)} collective-permute-done((bf16[272,1536]{1,0:T(8,128)(2,1)}, bf16[272,1536]{1,0:T(8,128)(2,1)}, u32[]{:S(2)}, u32[]{:S(2)}) %collective-permute-start) | collective-permute-done | bytes 835616 | tf_op jit(solution)/shard_map/ppermute | solution.py:326
  196.7 9.4 %collective-permute-done.3 = bf16[256,1536]{1,0:T(8,128)(2,1)} collective-permute-done((bf16[256,1536]{1,0:T(8,128)(2,1)}, bf16[256,1536]{1,0:T(8,128)(2,1)}, u32[]{:S(2)}, u32[]{:S(2)}) %collective-permute-start.3) | collective-permute-done | bytes 786464 | tf_op jit(solution)/shard_map/ppermute | solution.py:244
  208.0 33.5 %collective-permute-done.5 = bf16[256,1536]{1,0:T(8,128)(2,1)} collective-permute-done((bf16[256,1536]{1,0:T(8,128)(2,1)}, bf16[256,1536]{1,0:T(8,128)(2,1)}, u32[]{:S(2)}, u32[]{:S(2)}) %collective-permute-start.5) | collective-permute-done | bytes 786464 | tf_op jit(solution)/shard_map/ppermute | solution.py:244
  244.4 11.0 %psum.7 = f32[512]{0:T(512)S(1)} all-reduce(f32[512]{0:T(512)S(1)} %multiply_reduce_fusion), channel_id=1, replica_groups=mesh['groups'=2,'heads'=4,'seq'=4] {'seq'}, use_global_device_ids=true, to_apply=%region_11.12 | all-reduce | flops 512 | bytes 4096 | tf_op jit(solution)/shard_map/psum | solution.py:348
  255.4 3.6 multiply_convert_fusion
  259.0 50.9 %all-gather.10.cloned.1.call-done = bf16[2048,1536]{1,0:T(8,128)(2,1)} async-done(((bf16[512,1536]{1,0:T(8,128)(2,1)}), bf16[2048,1536]{1,0:T(8,128)(2,1)}) %all-gather.10.cloned.1.call-update) | async-done | bytes 6291472 | tf_op jit(solution)/shard_map/all_gather | solution.py:354
  309.9 5.7 %convolution_convert_fusion.3 = bf16[2048,256]{1,0:T(8,128)(2,1)} fusion(bf16[2048,1536]{1,0:T(8,128)(2,1)} %all-gather.10.cloned.1.call-done, bf16[4,1536,256]{2,1,0:T(8,128)(2,1)} %param.17, s32[]{:T(128)S(6)} %select_n.80), kind=kOutput, calls=%fused_computation.8 | convolution fusion | flops 1611137024 | bytes 8126468 | tf_op jit(solution)/shard_map/dot_general | solution.py:358
  316.0 11.1 %convolution_convert_fusion = bf16[2048,1024]{1,0:T(8,128)(2,1)} fusion(bf16[2048,1536]{1,0:T(8,128)(2,1)} %all-gather.10.cloned.1.call-done, bf16[1536,1024]{1,0:T(8,128)(2,1)S(1)} %copy-done.21), kind=kOutput, calls=%fused_computation | convolution fusion | flops 6444548096 | bytes 13631488 | tf_op jit(solution)/shard_map/dot_general | solution.py:357
  329.5 3.2 collective-permute-start.6
  335.1 41.5 %reduce-scatter.5.cloned.1.call-done = bf16[512,256]{1,0:T(8,128)(2,1)} async-done(((bf16[2048,256]{1,0:T(8,128)(2,1)}), bf16[512,256]{1,0:T(8,128)(2,1)}) %reduce-scatter.5.cloned.1.call-update) | async-done | bytes 262160 | tf_op jit(solution)/shard_map/reduce_scatter | solution.py:360
  381.9 104.8 %collective-permute-done.8 = bf16[512,256]{1,0:T(8,128)(2,1)S(1)} collective-permute-done((bf16[512,256]{1,0:T(8,128)(2,1)}, bf16[512,256]{1,0:T(8,128)(2,1)S(1)}, u32[]{:S(2)}, u32[]{:S(2)}) %collective-permute-start.8) | collective-permute-done | bytes 262176 | tf_op jit(solution)/shard_map/ppermute | solution.py:18
  487.8 11.4 %reduce-scatter.3.cloned.1.call-done.q_ref = bf16[512,1024]{1,0:T(8,128)(2,1)} async-done(((bf16[2048,1024]{1,0:T(8,128)(2,1)}), bf16[512,1024]{1,0:T(8,128)(2,1)}) %reduce-scatter.3.cloned.1.call-update) | async-done | bytes 1048592 | tf_op jit(solution)/shard_map/reduce_scatter | solution.py:359
  499.2 25.2 %shard_map.104 = bf16[512,1024]{1,0:T(8,128)(2,1)} custom-call(s32[1]{0:T(128)} %bitcast.42.pos_ref, bf16[512,1024]{1,0:T(8,128)(2,1)} %reduce-scatter.3.cloned.1.call-done.q_ref, bf16[4,512,256]{2,1,0:T(8,128)(2,1)} %pad_maximum_fusion.1.kv_ref), custom_call_target="tpu_custom_call" | custom-call | flops 4294967296 | bytes 3145728 | tf_op jit(solution)/shard_map/pallas_call | solution.py:297
  (141 shorter events, 72.8 us)
Async XLA Ops:
  7.2 106.7 %copy-start = (bf16[1024,1536]{1,0:T(8,128)(2,1)S(1)}, bf16[1024,1536]{1,0:T(8,128)(2,1)}, u32[]{:S(2)}) copy-start(bf16[1024,1536]{1,0:T(8,128)(2,1)} %param.14) | copy-start | bytes 9437188
  7.2 53.6 %all-gather.12.cloned.1.call-start = ((), (), s32[]{:S(2)}) async-start(), calls=%async_computation.7 | async-start | bytes 1474560 | tf_op jit(solution)/shard_map/all_gather | solution.py:207
  30.3 83.6 %all-gather.6.cloned.1.call-start = ((), (), s32[]{:S(2)}) async-start(), calls=%async_computation.2 | async-start | bytes 2621440 | tf_op jit(solution)/shard_map/all_gather | solution.py:337
  30.5 4.6 copy-start.19
  69.3 91.2 %all-gather.8.cloned.1.call-start = ((), (), s32[]{:S(2)}) async-start(), calls=%async_computation.3 | async-start | bytes 2621440 | tf_op jit(solution)/shard_map/all_gather | solution.py:337
  70.0 239.9 %all-gather.10.cloned.1.call-start = ((), (), s32[]{:S(2)}) async-start(), calls=%async_computation.4 | async-start | bytes 7864320 | tf_op jit(solution)/shard_map/all_gather | solution.py:354
  122.2 51.0 %collective-permute-start.2 = (bf16[2,256,1536]{2,1,0:T(8,128)(2,1)}, bf16[2,256,1536]{2,1,0:T(8,128)(2,1)}, u32[]{:S(2)}, u32[]{:S(2)}) collective-permute-start(bf16[2,256,1536]{2,1,0:T(8,128)(2,1)} %dynamic-slice_bitcast_fusion.1), channel_id=1, source_target_pairs={{0,4},{4,0},{8,12},{12,8},{1,5},{5,1},{9,13},{13,9},{2,6},{6,2},{1... | collective-permute-start | bytes 4718600 | tf_op jit(solution)/shard_map/ppermute | solution.py:240
  167.1 10.4 %collective-permute-start.4 = (bf16[2,256,1536]{2,1,0:T(8,128)(2,1)}, bf16[2,256,1536]{2,1,0:T(8,128)(2,1)}, u32[]{:S(2)}, u32[]{:S(2)}) collective-permute-start(bf16[2,256,1536]{2,1,0:T(8,128)(2,1)} %dynamic-slice_bitcast_fusion), channel_id=1, source_target_pairs={{0,4},{4,0},{8,12},{12,8},{1,5},{5,1},{9,13},{13,9},{2,6},{6,2},{1... | collective-permute-start | bytes 4718600 | tf_op jit(solution)/shard_map/ppermute | solution.py:240
  170.4 24.2 %collective-permute-start = (bf16[272,1536]{1,0:T(8,128)(2,1)}, bf16[272,1536]{1,0:T(8,128)(2,1)}, u32[]{:S(2)}, u32[]{:S(2)}) collective-permute-start(bf16[272,1536]{1,0:T(8,128)(2,1)} %pad_maximum_fusion.2), channel_id=1, source_target_pairs={{0,0},{1,4},{2,8},{3,12},{4,1},{5,5},{6,9},{7,13},{8,2},{9,6},{10,... | collective-permute-start | bytes 2506760 | tf_op jit(solution)/shard_map/ppermute | solution.py:326
  176.9 29.2 %collective-permute-start.3 = (bf16[256,1536]{1,0:T(8,128)(2,1)}, bf16[256,1536]{1,0:T(8,128)(2,1)}, u32[]{:S(2)}, u32[]{:S(2)}) collective-permute-start(bf16[256,1536]{1,0:T(8,128)(2,1)} %fusion.26), channel_id=1, source_target_pairs={{0,8},{4,12},{8,0},{12,4},{1,9},{5,13},{9,1},{13,5},{2,10},{6,14},... | collective-permute-start | bytes 2359304 | tf_op jit(solution)/shard_map/ppermute | solution.py:244
  181.3 60.1 %collective-permute-start.5 = (bf16[256,1536]{1,0:T(8,128)(2,1)}, bf16[256,1536]{1,0:T(8,128)(2,1)}, u32[]{:S(2)}, u32[]{:S(2)}) collective-permute-start(bf16[256,1536]{1,0:T(8,128)(2,1)} %fusion.27), channel_id=1, source_target_pairs={{0,8},{4,12},{8,0},{12,4},{1,9},{5,13},{9,1},{13,5},{2,10},{6,14},... | collective-permute-start | bytes 2359304 | tf_op jit(solution)/shard_map/ppermute | solution.py:244
  182.2 60.6 %collective-permute-start.1 = (bf16[256,1536]{1,0:T(8,128)(2,1)}, bf16[256,1536]{1,0:T(8,128)(2,1)}, u32[]{:S(2)}, u32[]{:S(2)}) collective-permute-start(bf16[256,1536]{1,0:T(8,128)(2,1)} %get-tuple-element.23), channel_id=1, source_target_pairs={{0,0},{1,4},{2,8},{3,12},{4,1},{5,5},{6,9},{7,13},{8,2},{9,6},{10,... | collective-permute-start | bytes 2359304 | tf_op jit(solution)/shard_map/ppermute | solution.py:329
  195.7 47.0 %copy-start.5 = (bf16[256,1536]{1,0:T(8,128)(2,1)}, bf16[256,1536]{1,0:T(8,128)(2,1)S(1)}, u32[]{:S(2)}) copy-start(bf16[256,1536]{1,0:T(8,128)(2,1)S(1)} %slice.151) | copy-start | bytes 2359300
  195.8 45.7 %copy-start.4 = (f32[2,256,1536]{2,1,0:T(8,128)S(1)}, f32[2,256,1536]{2,1,0:T(8,128)}, u32[]{:S(2)}) copy-start(f32[2,256,1536]{2,1,0:T(8,128)} %copy-done.3) | copy-start | bytes 9437188
  259.0 117.6 %reduce-scatter.5.cloned.1.call-start = ((), (), s32[]{:S(2)}) async-start(), calls=%async_computation.6 | async-start | bytes 1310720 | tf_op jit(solution)/shard_map/reduce_scatter | solution.py:360
  259.0 56.9 %copy-start.21 = (bf16[1536,1024]{1,0:T(8,128)(2,1)S(1)}, bf16[1536,1024]{1,0:T(8,128)(2,1)}, u32[]{:S(2)}) copy-start(bf16[1536,1024]{1,0:T(8,128)(2,1)} %param.16) | copy-start | bytes 9437188
  315.7 183.5 %reduce-scatter.3.cloned.1.call-start = ((), (), s32[]{:S(2)}) async-start(), calls=%async_computation.5 | async-start | bytes 5242880 | tf_op jit(solution)/shard_map/reduce_scatter | solution.py:359
  329.5 51.1 %collective-permute-start.6 = (bf16[256,1536]{1,0:T(8,128)(2,1)}, bf16[256,1536]{1,0:T(8,128)(2,1)S(1)}, u32[]{:S(2)}, u32[]{:S(2)}) collective-permute-start(bf16[256,1536]{1,0:T(8,128)(2,1)} %get-tuple-element.20), channel_id=1, source_target_pairs={{0,0},{1,4},{2,8},{3,12},{4,1},{5,5},{6,9},{7,13},{8,2},{9,6},{10,... | collective-permute-start | bytes 2359304 | tf_op jit(solution)/shard_map/ppermute | solution.py:345
  332.8 47.9 %collective-permute-start.7 = (bf16[256,1536]{1,0:T(8,128)(2,1)S(1)}, bf16[256,1536]{1,0:T(8,128)(2,1)S(1)}, u32[]{:S(2)}, u32[]{:S(2)}) collective-permute-start(bf16[256,1536]{1,0:T(8,128)(2,1)S(1)} %get-tuple-element.21), channel_id=1, source_target_pairs={{0,0},{1,4},{2,8},{3,12},{4,1},{5,5},{6,9},{7,13},{8,2},{9,6},{10,... | collective-permute-start | bytes 2359304 | tf_op jit(solution)/shard_map/ppermute | solution.py:346
  376.6 110.1 %copy-start.18 = (bf16[512,256]{1,0:T(8,128)(2,1)S(1)}, bf16[512,256]{1,0:T(8,128)(2,1)}, u32[]{:S(2)}) copy-start(bf16[512,256]{1,0:T(8,128)(2,1)} %reduce-scatter.5.cloned.1.call-done) | copy-start | bytes 786436
  376.6 110.1 %collective-permute-start.8 = (bf16[512,256]{1,0:T(8,128)(2,1)}, bf16[512,256]{1,0:T(8,128)(2,1)S(1)}, u32[]{:S(2)}, u32[]{:S(2)}) collective-permute-start(bf16[512,256]{1,0:T(8,128)(2,1)} %reduce-scatter.5.cloned.1.call-done), channel_id=1, source_target_pairs={{0,1},{1,2},{2,3},{4,5},{5,6},{6,7},{8,9},{9,10},{10,11},{12,13},{... | collective-permute-start | bytes 786440 | tf_op jit(solution)/shard_map/ppermute | solution.py:18
  378.6 108.0 %collective-permute-start.9 = (bf16[512,256]{1,0:T(8,128)(2,1)}, bf16[512,256]{1,0:T(8,128)(2,1)S(1)}, u32[]{:S(2)}, u32[]{:S(2)}) collective-permute-start(bf16[512,256]{1,0:T(8,128)(2,1)} %reduce-scatter.5.cloned.1.call-done), channel_id=1, source_target_pairs={{0,2},{1,3},{4,6},{5,7},{8,10},{9,11},{12,14},{13,15},{16,18},{17,... | collective-permute-start | bytes 786440 | tf_op jit(solution)/shard_map/ppermute | solution.py:18
  379.9 106.7 %collective-permute-start.10 = (bf16[512,256]{1,0:T(8,128)(2,1)}, bf16[512,256]{1,0:T(8,128)(2,1)S(1)}, u32[]{:S(2)}, u32[]{:S(2)}) collective-permute-start(bf16[512,256]{1,0:T(8,128)(2,1)} %reduce-scatter.5.cloned.1.call-done), channel_id=1, source_target_pairs={{0,3},{4,7},{8,11},{12,15},{16,19},{20,23},{24,27},{28,31}} | collective-permute-start | bytes 786440 | tf_op jit(solution)/shard_map/ppermute | solution.py:18
  499.2 25.2 %copy-start.1 = (bf16[1024,1536]{1,0:T(8,128)(2,1)S(1)}, bf16[1024,1536]{1,0:T(8,128)(2,1)}, u32[]{:S(2)}) copy-start(bf16[1024,1536]{1,0:T(8,128)(2,1)} %param.14) | copy-start | bytes 9437188
  (15 other events, 37.6 us)
Sparse Core Ops, SparseCore 0:
  30.4 30.3 all-gather.11
  69.4 44.4 all-gather.5
  116.0 44.4 all-gather.7
  259.1 50.8 all-gather.9
  315.8 60.7 reduce-scatter.4
  378.7 120.4 reduce-scatter.2

commit v15 on v14

--- a/solution.py
+++ b/solution.py
@@ -204,17 +204,15 @@
         _, out = lightning_block(starts[blk], (q4[rows], k4[rows], v4[rows], log_decay[rows]))
         outs.append(out)
     local_out = jnp.concatenate(outs, axis=0)
-    gathered = lax.all_gather(packed[None], "seq", axis=0, tiled=True)
-    gathered = gathered.astype(jnp.float32)
-    states = gathered[:, :, :DH, :]
-    totals = gathered[:, :, DH, 0]
+    n_seq = lax.axis_size("seq")
     position = lax.axis_index("seq")
-    device_order = jnp.arange(totals.shape[0])
-    earlier = (device_order < position)[:, None]
-    before = jnp.sum(jnp.where(earlier, totals, 0.0), axis=0)
-    inclusive = jnp.cumsum(totals, axis=0)
-    factors = jnp.where(earlier, jnp.exp(jnp.where(earlier, before[None, :] - inclusive, 0.0)), 0.0)
-    incoming = jnp.einsum("jh,jhde->hde", factors, states, precision=lax.Precision.HIGHEST)
+    incoming = jnp.zeros(state.shape, jnp.float32)
+    between = jnp.zeros((heads_here,), jnp.float32)
+    for dist in range(1, n_seq):
+        got = from_behind(packed, "seq", dist).astype(jnp.float32)
+        factor = jnp.where(dist <= position, jnp.exp(between), 0.0)
+        incoming = incoming + factor[:, None, None] * got[:, :DH, :]
+        between = between + got[:, DH, 0]
     running = jnp.cumsum(log_decay, axis=0)
     query_f = q4.astype(jnp.float32) * jnp.exp(running)[:, :, None]
     carried = jnp.einsum("thd,hde->the", query_f, incoming, precision=lax.Precision.HIGHEST)

time: 533 us -> 532 us (level)
  waiting for transfers between devices: 352 us -> 343 us
  starting transfers between devices: 21 us -> 26.9 us
    all_gather x1 -> x0, waiting for transfers between devices: 11.3 us -> none  [lightning_local(): gathered = lax.all_gather(packed[None], 'seq', axis=0, tiled=True)]
    ppermute x3 -> x6, starting transfers between devices: 4.01 us -> 9.86 us  [from_behind(): lax.ppermute(value, axis, [(source, source + steps) for source in range(l...]
    ppermute x3 -> x6, waiting for transfers between devices: 105 us -> 105 us  [from_behind(): lax.ppermute(value, axis, [(source, source + steps) for source in range(l...]
  transfers between devices with their start and end apart: 17 -> 19, of which waited for: 10 -> 9; matrix products, arithmetic and copies ran while one was open for 11% -> 12% of each run, Pallas kernels for 0% -> 0%
where the time goes in v15:
time: 532 us; the launch traced here: 530 us
  waiting for transfers between devices  343 us (64%)
  matrix products  47.5 us (9%)
  local copies, waits for them, and re-layouts  35.3 us (7%)
  other arithmetic  27.1 us (5%)
  starting transfers between devices  26.9 us (5%)
  Pallas kernels  25.2 us (5%)
  between operations  14.3 us (3%)
  blocking collectives  10.9 us (2%)
    ppermute x6, waiting for transfers between devices, from_behind(): lax.ppermute(value, axis, [(source, source + steps) for source in range(l...  105 us
    all_gather x2, waiting for transfers between devices, shards_fast_body(): lax.all_gather(lin_out[half * half_rows:(half + 1) * half_rows], 'seq', a...  83 us
    all_gather x1, waiting for transfers between devices, shards_fast_body(): normed_all = lax.all_gather(normed, 'heads', axis=0, tiled=True)  50.9 us
    ppermute x2, waiting for transfers between devices, heads_reduce_scatter(): lax.ppermute(send2.astype(jnp.bfloat16), 'heads', [(i, i ^ 2) for i in ra...  42.8 us
    reduce_scatter x1, waiting for transfers between devices, shards_fast_body(): lax.psum_scatter(kv_part.astype(jnp.bfloat16), 'seq', scatter_dimension=0...  41.4 us
    pallas_call x1, Pallas kernels, attention_pallas(): pl.pallas_call(attention_kernel, grid_spec=grid_spec, out_shape=jax.Shape...  25.2 us
    reduce_scatter x1, waiting for transfers between devices, shards_fast_body(): lax.psum_scatter(q_part.astype(jnp.bfloat16), 'seq', scatter_dimension=0,...  11.3 us
    dot_general x1, matrix products, shards_fast_body(): jnp.dot(normed_all, query_weight, preferred_element_type=jnp.float32)  11.1 us
  transfers between devices with their start and end apart: 19, of which 9 were waited for; matrix products, arithmetic and copies ran while one was open for 12% of the time, Pallas kernels for 0%

profile of v15, /device:TPU:21, one launch (start us, length us, event | category | flops | bytes accessed | tf_op | source)
XLA Modules:
  0.0 529.9 jit_solution(15191002002613911848)
XLA Ops:
  11.7 2.8 slice_convert_fusion.1
  30.8 3.2 collective-permute-start.2
  46.1 3.2 fusion.15
  51.3 3.7 fusion.4
  55.0 3.7 fusion.7
  60.2 4.5 multiply_reduce_fusion.1
  67.2 45.5 %all-gather.4.cloned.1.call-done = bf16[1024,1024]{0,1:T(8,128)(2,1)} async-done(((bf16[256,1024]{0,1:T(8,128)(2,1)}), bf16[1024,1024]{0,1:T(8,128)(2,1)}) %all-gather.4.cloned.1.call-update) | async-done | bytes 2097168 | tf_op jit(solution)/shard_map/all_gather | solution.py:335
  112.8 5.4 %convolution_convert_fusion.2 = bf16[1024,1536]{1,0:T(8,128)(2,1)S(1)} fusion(bf16[1024,1024]{0,1:T(8,128)(2,1)} %all-gather.4.cloned.1.call-done, bf16[1024,1536]{1,0:T(8,128)(2,1)S(1)} %copy-done), kind=kOutput, calls=%fused_computation.2 | convolution fusion | flops 3222798336 | bytes 8388608 | tf_op jit(solution)/shard_map/dot_general | solution.py:338
  121.9 37.4 %all-gather.6.cloned.1.call-done = bf16[1024,1024]{0,1:T(8,128)(2,1)} async-done(((bf16[256,1024]{0,1:T(8,128)(2,1)}), bf16[1024,1024]{0,1:T(8,128)(2,1)}) %all-gather.6.cloned.1.call-update) | async-done | bytes 2097168 | tf_op jit(solution)/shard_map/all_gather | solution.py:335
  159.4 5.4 %convolution_convert_fusion.1 = bf16[1024,1536]{1,0:T(8,128)(2,1)S(1)} fusion(bf16[1024,1024]{0,1:T(8,128)(2,1)} %all-gather.6.cloned.1.call-done, bf16[1024,1536]{1,0:T(8,128)(2,1)S(1)} %copy-done), kind=kOutput, calls=%fused_computation.1 | convolution fusion | flops 3222798336 | bytes 8388608 | tf_op jit(solution)/shard_map/dot_general | solution.py:338
  181.1 4.8 collective-permute-start.1
  185.9 7.5 %collective-permute-done = bf16[272,1536]{1,0:T(8,128)(2,1)} collective-permute-done((bf16[272,1536]{1,0:T(8,128)(2,1)}, bf16[272,1536]{1,0:T(8,128)(2,1)}, u32[]{:S(2)}, u32[]{:S(2)}) %collective-permute-start) | collective-permute-done | bytes 835616 | tf_op jit(solution)/shard_map/ppermute | solution.py:324
  195.6 9.4 %collective-permute-done.6 = bf16[256,1536]{1,0:T(8,128)(2,1)} collective-permute-done((bf16[256,1536]{1,0:T(8,128)(2,1)}, bf16[256,1536]{1,0:T(8,128)(2,1)}, u32[]{:S(2)}, u32[]{:S(2)}) %collective-permute-start.6) | collective-permute-done | bytes 786464 | tf_op jit(solution)/shard_map/ppermute | solution.py:242
  206.8 33.5 %collective-permute-done.8 = bf16[256,1536]{1,0:T(8,128)(2,1)} collective-permute-done((bf16[256,1536]{1,0:T(8,128)(2,1)}, bf16[256,1536]{1,0:T(8,128)(2,1)}, u32[]{:S(2)}, u32[]{:S(2)}) %collective-permute-start.8) | collective-permute-done | bytes 786464 | tf_op jit(solution)/shard_map/ppermute | solution.py:242
  243.3 10.9 %psum.7 = f32[512]{0:T(512)S(1)} all-reduce(f32[512]{0:T(512)S(1)} %multiply_reduce_fusion), channel_id=1, replica_groups=mesh['groups'=2,'heads'=4,'seq'=4] {'seq'}, use_global_device_ids=true, to_apply=%region_9.10 | all-reduce | flops 512 | bytes 4096 | tf_op jit(solution)/shard_map/psum | solution.py:346
  254.3 3.6 multiply_convert_fusion
  257.9 50.9 %all-gather.8.cloned.1.call-done = bf16[2048,1536]{1,0:T(8,128)(2,1)} async-done(((bf16[512,1536]{1,0:T(8,128)(2,1)}), bf16[2048,1536]{1,0:T(8,128)(2,1)}) %all-gather.8.cloned.1.call-update) | async-done | bytes 6291472 | tf_op jit(solution)/shard_map/all_gather | solution.py:352
  308.9 5.7 %convolution_convert_fusion.3 = bf16[2048,256]{1,0:T(8,128)(2,1)} fusion(bf16[2048,1536]{1,0:T(8,128)(2,1)} %all-gather.8.cloned.1.call-done, bf16[4,1536,256]{2,1,0:T(8,128)(2,1)} %param.17, s32[]{:T(128)S(6)} %select_n.93), kind=kOutput, calls=%fused_computation.8 | convolution fusion | flops 1611137024 | bytes 8126468 | tf_op jit(solution)/shard_map/dot_general | solution.py:356
  314.9 11.1 %convolution_convert_fusion = bf16[2048,1024]{1,0:T(8,128)(2,1)} fusion(bf16[2048,1536]{1,0:T(8,128)(2,1)} %all-gather.8.cloned.1.call-done, bf16[1536,1024]{1,0:T(8,128)(2,1)S(1)} %copy-done.24), kind=kOutput, calls=%fused_computation | convolution fusion | flops 6444548096 | bytes 13631488 | tf_op jit(solution)/shard_map/dot_general | solution.py:355
  328.5 3.2 collective-permute-start.10
  334.0 41.4 %reduce-scatter.5.cloned.1.call-done = bf16[512,256]{1,0:T(8,128)(2,1)} async-done(((bf16[2048,256]{1,0:T(8,128)(2,1)}), bf16[512,256]{1,0:T(8,128)(2,1)}) %reduce-scatter.5.cloned.1.call-update) | async-done | bytes 262160 | tf_op jit(solution)/shard_map/reduce_scatter | solution.py:358
  380.8 104.9 %collective-permute-done.11 = bf16[512,256]{1,0:T(8,128)(2,1)S(1)} collective-permute-done((bf16[512,256]{1,0:T(8,128)(2,1)}, bf16[512,256]{1,0:T(8,128)(2,1)S(1)}, u32[]{:S(2)}, u32[]{:S(2)}) %collective-permute-start.11) | collective-permute-done | bytes 262176 | tf_op jit(solution)/shard_map/ppermute | solution.py:18
  486.8 11.3 %reduce-scatter.3.cloned.1.call-done.q_ref = bf16[512,1024]{1,0:T(8,128)(2,1)} async-done(((bf16[2048,1024]{1,0:T(8,128)(2,1)}), bf16[512,1024]{1,0:T(8,128)(2,1)}) %reduce-scatter.3.cloned.1.call-update) | async-done | bytes 1048592 | tf_op jit(solution)/shard_map/reduce_scatter | solution.py:357
  498.1 25.2 %shard_map.104 = bf16[512,1024]{1,0:T(8,128)(2,1)} custom-call(s32[1]{0:T(128)} %bitcast.37.pos_ref, bf16[512,1024]{1,0:T(8,128)(2,1)} %reduce-scatter.3.cloned.1.call-done.q_ref, bf16[4,512,256]{2,1,0:T(8,128)(2,1)} %pad_maximum_fusion.1.kv_ref), custom_call_target="tpu_custom_call" | custom-call | flops 4294967296 | bytes 3145728 | tf_op jit(solution)/shard_map/pallas_call | solution.py:295
  (145 shorter events, 77.3 us)
Async XLA Ops:
  7.2 105.6 %copy-start = (bf16[1024,1536]{1,0:T(8,128)(2,1)S(1)}, bf16[1024,1536]{1,0:T(8,128)(2,1)}, u32[]{:S(2)}) copy-start(bf16[1024,1536]{1,0:T(8,128)(2,1)} %param.14) | copy-start | bytes 9437188
  7.2 105.6 %all-gather.4.cloned.1.call-start = ((), (), s32[]{:S(2)}) async-start(), calls=%async_computation.2 | async-start | bytes 2621440 | tf_op jit(solution)/shard_map/all_gather | solution.py:335
  30.8 28.1 %collective-permute-start.2 = (bf16[8,144,128]{2,1,0:T(8,128)(2,1)}, bf16[8,144,128]{2,1,0:T(8,128)(2,1)}, u32[]{:S(2)}, u32[]{:S(2)}) collective-permute-start(bf16[8,144,128]{2,1,0:T(8,128)(2,1)} %pad_maximum_fusion.3), channel_id=1, source_target_pairs={{0,1},{1,2},{2,3},{4,5},{5,6},{6,7},{8,9},{9,10},{10,11},{12,13},{... | collective-permute-start | bytes 884744 | tf_op jit(solution)/shard_map/ppermute | solution.py:18
  34.0 26.0 %collective-permute-start.3 = (bf16[8,144,128]{2,1,0:T(8,128)(2,1)}, bf16[8,144,128]{2,1,0:T(8,128)(2,1)S(1)}, u32[]{:S(2)}, u32[]{:S(2)}) collective-permute-start(bf16[8,144,128]{2,1,0:T(8,128)(2,1)} %pad_maximum_fusion.3), channel_id=1, source_target_pairs={{0,2},{1,3},{4,6},{5,7},{8,10},{9,11},{12,14},{13,15},{16,18},{17,... | collective-permute-start | bytes 884744 | tf_op jit(solution)/shard_map/ppermute | solution.py:18
  35.3 24.9 %collective-permute-start.4 = (bf16[8,144,128]{2,1,0:T(8,128)(2,1)}, bf16[8,144,128]{2,1,0:T(8,128)(2,1)}, u32[]{:S(2)}, u32[]{:S(2)}) collective-permute-start(bf16[8,144,128]{2,1,0:T(8,128)(2,1)} %pad_maximum_fusion.3), channel_id=1, source_target_pairs={{0,3},{4,7},{8,11},{12,15},{16,19},{20,23},{24,27},{28,31}} | collective-permute-start | bytes 884744 | tf_op jit(solution)/shard_map/ppermute | solution.py:18
  66.2 93.2 %all-gather.6.cloned.1.call-start = ((), (), s32[]{:S(2)}) async-start(), calls=%async_computation.3 | async-start | bytes 2621440 | tf_op jit(solution)/shard_map/all_gather | solution.py:335
  67.0 241.9 %all-gather.8.cloned.1.call-start = ((), (), s32[]{:S(2)}) async-start(), calls=%async_computation.4 | async-start | bytes 7864320 | tf_op jit(solution)/shard_map/all_gather | solution.py:352
  121.1 51.0 %collective-permute-start.5 = (bf16[2,256,1536]{2,1,0:T(8,128)(2,1)}, bf16[2,256,1536]{2,1,0:T(8,128)(2,1)}, u32[]{:S(2)}, u32[]{:S(2)}) collective-permute-start(bf16[2,256,1536]{2,1,0:T(8,128)(2,1)} %dynamic-slice_bitcast_fusion.1), channel_id=1, source_target_pairs={{0,4},{4,0},{8,12},{12,8},{1,5},{5,1},{9,13},{13,9},{2,6},{6,2},{1... | collective-permute-start | bytes 4718600 | tf_op jit(solution)/shard_map/ppermute | solution.py:238
  166.0 10.5 %collective-permute-start.7 = (bf16[2,256,1536]{2,1,0:T(8,128)(2,1)}, bf16[2,256,1536]{2,1,0:T(8,128)(2,1)}, u32[]{:S(2)}, u32[]{:S(2)}) collective-permute-start(bf16[2,256,1536]{2,1,0:T(8,128)(2,1)} %dynamic-slice_bitcast_fusion), channel_id=1, source_target_pairs={{0,4},{4,0},{8,12},{12,8},{1,5},{5,1},{9,13},{13,9},{2,6},{6,2},{1... | collective-permute-start | bytes 4718600 | tf_op jit(solution)/shard_map/ppermute | solution.py:238
  169.3 24.2 %collective-permute-start = (bf16[272,1536]{1,0:T(8,128)(2,1)}, bf16[272,1536]{1,0:T(8,128)(2,1)}, u32[]{:S(2)}, u32[]{:S(2)}) collective-permute-start(bf16[272,1536]{1,0:T(8,128)(2,1)} %pad_maximum_fusion.2), channel_id=1, source_target_pairs={{0,0},{1,4},{2,8},{3,12},{4,1},{5,5},{6,9},{7,13},{8,2},{9,6},{10,... | collective-permute-start | bytes 2506760 | tf_op jit(solution)/shard_map/ppermute | solution.py:324
  175.9 29.1 %collective-permute-start.6 = (bf16[256,1536]{1,0:T(8,128)(2,1)}, bf16[256,1536]{1,0:T(8,128)(2,1)}, u32[]{:S(2)}, u32[]{:S(2)}) collective-permute-start(bf16[256,1536]{1,0:T(8,128)(2,1)} %fusion.26), channel_id=1, source_target_pairs={{0,8},{4,12},{8,0},{12,4},{1,9},{5,13},{9,1},{13,5},{2,10},{6,14},... | collective-permute-start | bytes 2359304 | tf_op jit(solution)/shard_map/ppermute | solution.py:242
  180.2 60.1 %collective-permute-start.8 = (bf16[256,1536]{1,0:T(8,128)(2,1)}, bf16[256,1536]{1,0:T(8,128)(2,1)}, u32[]{:S(2)}, u32[]{:S(2)}) collective-permute-start(bf16[256,1536]{1,0:T(8,128)(2,1)} %fusion.27), channel_id=1, source_target_pairs={{0,8},{4,12},{8,0},{12,4},{1,9},{5,13},{9,1},{13,5},{2,10},{6,14},... | collective-permute-start | bytes 2359304 | tf_op jit(solution)/shard_map/ppermute | solution.py:242
  181.1 60.6 %collective-permute-start.1 = (bf16[256,1536]{1,0:T(8,128)(2,1)}, bf16[256,1536]{1,0:T(8,128)(2,1)}, u32[]{:S(2)}, u32[]{:S(2)}) collective-permute-start(bf16[256,1536]{1,0:T(8,128)(2,1)} %get-tuple-element.25), channel_id=1, source_target_pairs={{0,0},{1,4},{2,8},{3,12},{4,1},{5,5},{6,9},{7,13},{8,2},{9,6},{10,... | collective-permute-start | bytes 2359304 | tf_op jit(solution)/shard_map/ppermute | solution.py:327
  194.7 47.0 %copy-start.5 = (bf16[256,1536]{1,0:T(8,128)(2,1)}, bf16[256,1536]{1,0:T(8,128)(2,1)S(1)}, u32[]{:S(2)}) copy-start(bf16[256,1536]{1,0:T(8,128)(2,1)S(1)} %slice.166) | copy-start | bytes 2359300
  194.7 45.6 %copy-start.4 = (f32[2,256,1536]{2,1,0:T(8,128)S(1)}, f32[2,256,1536]{2,1,0:T(8,128)}, u32[]{:S(2)}) copy-start(f32[2,256,1536]{2,1,0:T(8,128)} %copy-done.3) | copy-start | bytes 9437188
  257.9 117.6 %reduce-scatter.5.cloned.1.call-start = ((), (), s32[]{:S(2)}) async-start(), calls=%async_computation.6 | async-start | bytes 1310720 | tf_op jit(solution)/shard_map/reduce_scatter | solution.py:358
  257.9 57.0 %copy-start.24 = (bf16[1536,1024]{1,0:T(8,128)(2,1)S(1)}, bf16[1536,1024]{1,0:T(8,128)(2,1)}, u32[]{:S(2)}) copy-start(bf16[1536,1024]{1,0:T(8,128)(2,1)} %param.16) | copy-start | bytes 9437188
  314.6 183.5 %reduce-scatter.3.cloned.1.call-start = ((), (), s32[]{:S(2)}) async-start(), calls=%async_computation.5 | async-start | bytes 5242880 | tf_op jit(solution)/shard_map/reduce_scatter | solution.py:357
  328.5 51.0 %collective-permute-start.10 = (bf16[256,1536]{1,0:T(8,128)(2,1)}, bf16[256,1536]{1,0:T(8,128)(2,1)S(1)}, u32[]{:S(2)}, u32[]{:S(2)}) collective-permute-start(bf16[256,1536]{1,0:T(8,128)(2,1)} %get-tuple-element.23), channel_id=1, source_target_pairs={{0,0},{1,4},{2,8},{3,12},{4,1},{5,5},{6,9},{7,13},{8,2},{9,6},{10,... | collective-permute-start | bytes 2359304 | tf_op jit(solution)/shard_map/ppermute | solution.py:344
  331.7 47.8 %collective-permute-start.9 = (bf16[256,1536]{1,0:T(8,128)(2,1)S(1)}, bf16[256,1536]{1,0:T(8,128)(2,1)S(1)}, u32[]{:S(2)}, u32[]{:S(2)}) collective-permute-start(bf16[256,1536]{1,0:T(8,128)(2,1)S(1)} %get-tuple-element.22), channel_id=1, source_target_pairs={{0,0},{1,4},{2,8},{3,12},{4,1},{5,5},{6,9},{7,13},{8,2},{9,6},{10,... | collective-permute-start | bytes 2359304 | tf_op jit(solution)/shard_map/ppermute | solution.py:343
  375.5 110.2 %copy-start.17 = (bf16[512,256]{1,0:T(8,128)(2,1)S(1)}, bf16[512,256]{1,0:T(8,128)(2,1)}, u32[]{:S(2)}) copy-start(bf16[512,256]{1,0:T(8,128)(2,1)} %reduce-scatter.5.cloned.1.call-done) | copy-start | bytes 786436
  375.5 110.2 %collective-permute-start.11 = (bf16[512,256]{1,0:T(8,128)(2,1)}, bf16[512,256]{1,0:T(8,128)(2,1)S(1)}, u32[]{:S(2)}, u32[]{:S(2)}) collective-permute-start(bf16[512,256]{1,0:T(8,128)(2,1)} %reduce-scatter.5.cloned.1.call-done), channel_id=1, source_target_pairs={{0,1},{1,2},{2,3},{4,5},{5,6},{6,7},{8,9},{9,10},{10,11},{12,13},{... | collective-permute-start | bytes 786440 | tf_op jit(solution)/shard_map/ppermute | solution.py:18
  377.5 108.1 %collective-permute-start.12 = (bf16[512,256]{1,0:T(8,128)(2,1)}, bf16[512,256]{1,0:T(8,128)(2,1)S(1)}, u32[]{:S(2)}, u32[]{:S(2)}) collective-permute-start(bf16[512,256]{1,0:T(8,128)(2,1)} %reduce-scatter.5.cloned.1.call-done), channel_id=1, source_target_pairs={{0,2},{1,3},{4,6},{5,7},{8,10},{9,11},{12,14},{13,15},{16,18},{17,... | collective-permute-start | bytes 786440 | tf_op jit(solution)/shard_map/ppermute | solution.py:18
  378.8 106.8 %collective-permute-start.13 = (bf16[512,256]{1,0:T(8,128)(2,1)}, bf16[512,256]{1,0:T(8,128)(2,1)S(1)}, u32[]{:S(2)}, u32[]{:S(2)}) collective-permute-start(bf16[512,256]{1,0:T(8,128)(2,1)} %reduce-scatter.5.cloned.1.call-done), channel_id=1, source_target_pairs={{0,3},{4,7},{8,11},{12,15},{16,19},{20,23},{24,27},{28,31}} | collective-permute-start | bytes 786440 | tf_op jit(solution)/shard_map/ppermute | solution.py:18
  (20 other events, 86.2 us)
Sparse Core Ops, SparseCore 0:
  66.3 46.3 all-gather.3
  114.9 44.4 all-gather.5
  258.0 50.8 all-gather.7
  314.7 60.6 reduce-scatter.4
  377.6 120.4 reduce-scatter.2
